TPU v7x, 1024 devices: a whole 4x4x32 slice. The times are simulated.
1024 devices in a mesh: span: 32 (over z_lo, core), wall: 32 (over z_hi, y, x).
Axes of the slice: x: 4, y: 4, z: 32 (z_hi: 2, z_lo: 16; z = z_hi * 16 + z_lo), core: 2. Of those that a mesh axis runs over, the one named last changes fastest.
Arguments:
- field: float32 [5, 5, 5, 32, 64, 128], P(None, None, None, 'span', 'wall'), may hold values from -6 to 6
- velocity: float32 [3, 5, 5, 5, 32, 64, 128], P(None, None, None, None, 'span', 'wall'), may hold values from -6 to 6
- cells: int32 [131072], P(('span', 'wall')), may hold values from 0 to 255
- destination: int32 [131072, 1], P(('span', 'wall')), may hold values from 0 to 31; in each aligned block of 128 rows (0 to 127, 128 to 255, ...) at most 16 rows name the same one
- targets: bfloat16 [131072, 128], P(('span', 'wall')), may hold values from -6 to 6
- weight_in: bfloat16 [32, 128, 256], P('span'), may hold values from -0.5 to 0.5
- weight_two: bfloat16 [32, 256, 256], P('span'), may hold values from -0.375 to 0.375
- weight_three: bfloat16 [32, 256, 256], P('span'), may hold values from -0.375 to 0.375
- weight_four: bfloat16 [32, 256, 256], P('span'), may hold values from -0.375 to 0.375
- weight_out: bfloat16 [32, 256, 128], P('span'), may hold values from -0.375 to 0.375
Outputs:
- new_field: float32 [5, 5, 5, 32, 64, 128], P(None, None, None, 'span', 'wall')
- grad_in: float32 [32, 128, 256], P('span')
- grad_two: float32 [32, 256, 256], P('span')
- grad_three: float32 [32, 256, 256], P('span')
- grad_four: float32 [32, 256, 256], P('span')
- grad_out: float32 [32, 256, 128], P('span')
Inputs may be any that keep to these rules, and one draw needn't show every extreme that they name: `cells`: A local element index of the owning device. `destination`: among the 128 rows of one device at most 16 name the same station, and in every draw some device has exactly 16 rows naming one station.
All inputs are finite; a program needn't handle non-finite values.
Results may differ from a plain program's by a relative error of at most 0.0065.
Values may be sent and summed in bfloat16 or wider, within the bound.
No kernel may reach another device: no remote copies, remote signals or barrier semaphores. Data moves between devices by JAX's collectives and lax.ppermute only.
A program may use at most 32 MiB of HBM per device.

v0:
```python
import math

import jax
import jax.numpy as jnp
from jax import lax
from jax.sharding import PartitionSpec as P

P_SIZE = 5
S = 128
FEAT = 128


step_scale = 0.04


def extended(x, sides, width):
    for axis, dim in sides:
        size, length = (lax.axis_size(axis), x.shape[dim])
        up = [(i, (i + 1) % size) for i in range(size - 1)]
        down = [(j, i) for i, j in up]
        last = lax.slice_in_dim(x, length - width, length, axis=dim)
        first = lax.slice_in_dim(x, 0, width, axis=dim)
        before = lax.ppermute(last, axis, up)
        after = lax.ppermute(first, axis, down)
        x = jnp.concatenate([before, x, after], axis=dim)
    return x


def legendre_pair(order, point):
    value_prev = 1.0
    value_now = point
    slope_prev = 0.0
    slope_now = 1.0
    for degree in range(1, order):
        value_next = ((2 * degree + 1) * point * value_now - degree * value_prev) / (degree + 1)
        slope_next = slope_prev + (2 * degree + 1) * value_now
        value_prev, value_now = (value_now, value_next)
        slope_prev, slope_now = (slope_now, slope_next)
    return (value_now, slope_now)


def gauss_nodes(count):
    found = []
    for index in range(count):
        guess = math.cos(math.pi * (index + 0.75) / (count + 0.5))
        for sweep in range(60):
            value, slope = legendre_pair(count, guess)
            guess = guess - value / slope
        found.append(guess)
    return sorted(found)


def fr_tables():
    nodes = gauss_nodes(P_SIZE)
    bary = []
    for j in range(P_SIZE):
        product = 1.0
        for m in range(P_SIZE):
            if m != j:
                product = product * (nodes[j] - nodes[m])
        bary.append(1.0 / product)
    deriv = [[0.0] * P_SIZE for row_index in range(P_SIZE)]
    for i in range(P_SIZE):
        for j in range(P_SIZE):
            if i != j:
                deriv[i][j] = bary[j] / bary[i] / (nodes[i] - nodes[j])
        deriv[i][i] = -sum((deriv[i][j] for j in range(P_SIZE) if j != i))

    def basis_at(point):
        values = []
        for j in range(P_SIZE):
            product = 1.0
            for m in range(P_SIZE):
                if m != j:
                    product = product * (point - nodes[m]) / (nodes[j] - nodes[m])
            values.append(product)
        return values

    left_value = basis_at(-1.0)
    right_value = basis_at(1.0)
    sign = (-1.0) ** P_SIZE
    slope_left = [
        0.5 * sign * (legendre_pair(P_SIZE, x)[1] - legendre_pair(P_SIZE - 1, x)[1]) for x in nodes
    ]
    slope_right = [-slope_left[P_SIZE - 1 - i] for i in range(P_SIZE)]
    return tuple(
        (
            jnp.asarray(table, jnp.float32)
            for table in (deriv, left_value, right_value, slope_left, slope_right)
        )
    )


def along(matrix, field, axis):
    return jnp.moveaxis(
        jnp.tensordot(matrix, field, axes=([1], [axis]), precision=lax.Precision.HIGHEST), 0, axis
    )


def at_face(vector, field, axis):
    return jnp.tensordot(vector, field, axes=([0], [axis]), precision=lax.Precision.HIGHEST)


def spread(face, vector, axis, ndim):
    target_shape = [1] * ndim
    target_shape[axis] = vector.shape[0]
    return jnp.expand_dims(face, axis) * vector.reshape(target_shape)


def upwind(state_before, speed_before, state_after, speed_after):
    mean_speed = 0.5 * (speed_before + speed_after)
    return 0.5 * mean_speed * (state_before + state_after) - 0.5 * jnp.abs(mean_speed) * (
        state_after - state_before
    )


def face_states(field, speed, axis, tables):
    left_value = tables[1]
    right_value = tables[2]
    return (
        at_face(left_value, field, axis),
        at_face(left_value, speed, axis),
        at_face(right_value, field, axis),
        at_face(right_value, speed, axis),
    )


def divergence(field, speed, axis, own, before, after, tables):
    deriv, left_value, right_value, slope_left, slope_right = tables
    flux = speed * field
    volume = along(deriv, flux, axis)
    flux_left = at_face(left_value, flux, axis)
    flux_right = at_face(right_value, flux, axis)
    common_left = upwind(before[0], before[1], own[0], own[1])
    common_right = upwind(own[2], own[3], after[0], after[1])
    return (
        volume
        + spread(common_left - flux_left, slope_left, axis, field.ndim)
        + spread(common_right - flux_right, slope_right, axis, field.ndim)
    )


def forward(inputs, weights):
    acts = [inputs]
    pres = []
    hidden = inputs
    for layer in weights[:-1]:
        pre = jnp.dot(hidden, layer, preferred_element_type=jnp.float32)
        pres.append(pre)
        hidden = jax.nn.silu(pre).astype(jnp.bfloat16)
        acts.append(hidden)
    return (jnp.dot(hidden, weights[-1], preferred_element_type=jnp.float32), acts, pres)


def backward_layer(error, weight, pre):
    back = lax.dot_general(
        error, weight, (((1,), (1,)), ((), ())), preferred_element_type=jnp.float32
    )
    sigma = jax.nn.sigmoid(pre)
    return (back * sigma * (1.0 + pre * (1.0 - sigma))).astype(jnp.bfloat16)


def weight_grad(act, error):
    return lax.dot_general(act, error, (((0,), (0,)), ((), ())), preferred_element_type=jnp.float32)


def neighbour_faces(direction, field, speed, tables):
    count = field.shape[3 + direction]
    face_axis = 3 + direction
    stacked = jnp.stack([field, speed])
    if direction == 0:
        padded = extended(stacked, (("span", 4),), 1)
    else:
        padded = extended(stacked, (("wall", 5),), 1)
    padded_left = at_face(tables[1], padded, 1 + direction)
    padded_right = at_face(tables[2], padded, 1 + direction)
    before = lax.slice_in_dim(padded_right, 0, count, axis=face_axis)
    after = lax.slice_in_dim(padded_left, 2, count + 2, axis=face_axis)
    return ((before[0], before[1]), (after[0], after[1]))


def local(
    field,
    velocity,
    cells,
    destination,
    targets,
    weight_in,
    weight_two,
    weight_three,
    weight_four,
    weight_out,
):
    tables = fr_tables()
    total = jnp.zeros_like(field)
    for direction in range(3):
        speed = velocity[direction]
        own = face_states(field, speed, direction, tables)
        if direction < 2:
            before, after = neighbour_faces(direction, field, speed, tables)
        else:
            before = (jnp.roll(own[2], 1, 4), jnp.roll(own[3], 1, 4))
            after = (jnp.roll(own[0], -1, 4), jnp.roll(own[1], -1, 4))
        total = total + divergence(field, speed, direction, own, before, after, tables)
    new_field = field - step_scale * total
    local_count = field.shape[3] * field.shape[4] * field.shape[5]
    speed_means = jnp.mean(velocity.reshape(3, P_SIZE * P_SIZE * P_SIZE, local_count), axis=1)
    values = jnp.concatenate(
        [new_field.reshape(P_SIZE * P_SIZE * P_SIZE, local_count), speed_means], axis=0
    )
    rows = jnp.take(values, cells, axis=1).T.astype(jnp.bfloat16)
    span_count = lax.axis_size("span")
    slot_count = S // 8
    dest = destination[:, 0]
    onehot = (dest[:, None] == jnp.arange(span_count, dtype=jnp.int32)[None, :]).astype(jnp.int32)
    slots = jnp.sum((jnp.cumsum(onehot, axis=0) - 1) * onehot, axis=1)
    position = dest * slot_count + slots
    row_buffer = jnp.zeros((span_count * slot_count, FEAT), jnp.bfloat16).at[position].set(rows)
    target_buffer = (
        jnp.zeros((span_count * slot_count, targets.shape[1]), jnp.bfloat16)
        .at[position]
        .set(targets)
    )
    flag_buffer = (
        jnp.zeros((span_count * slot_count,), jnp.bfloat16)
        .at[position]
        .set(jnp.ones((rows.shape[0],), jnp.bfloat16))
    )
    got_rows, got_targets, got_flags = (
        lax.all_to_all(
            row_buffer.reshape(span_count, slot_count, FEAT),
            "span",
            split_axis=0,
            concat_axis=0,
            tiled=True,
        ),
        lax.all_to_all(
            target_buffer.reshape(span_count, slot_count, -1),
            "span",
            split_axis=0,
            concat_axis=0,
            tiled=True,
        ),
        lax.all_to_all(
            flag_buffer.reshape(span_count, slot_count),
            "span",
            split_axis=0,
            concat_axis=0,
            tiled=True,
        ),
    )
    inputs = got_rows.reshape(span_count * slot_count, FEAT)
    wanted = got_targets.reshape(span_count * slot_count, -1).astype(jnp.float32)
    flags = got_flags.reshape(span_count * slot_count).astype(jnp.float32)
    row_scale = flags / jnp.maximum(jnp.sum(flags), 1.0)
    layer_one = weight_in[0]
    layer_two = weight_two[0]
    layer_three = weight_three[0]
    layer_four = weight_four[0]
    layer_last = weight_out[0]
    weights = (layer_one, layer_two, layer_three, layer_four, layer_last)
    output, acts, pres = forward(inputs, weights)
    error = (row_scale[:, None] * (output - wanted)).astype(jnp.bfloat16)
    grad_last = weight_grad(acts[4], error)
    error = backward_layer(error, layer_last, pres[3])
    grad_fourth = weight_grad(acts[3], error)
    error = backward_layer(error, layer_four, pres[2])
    grad_third = weight_grad(acts[2], error)
    error = backward_layer(error, layer_three, pres[1])
    grad_second = weight_grad(acts[1], error)
    error = backward_layer(error, layer_two, pres[0])
    grad_first = weight_grad(acts[0], error)
    grad_first, grad_second, grad_third, grad_fourth, grad_last = lax.psum(
        (grad_first, grad_second, grad_third, grad_fourth, grad_last), "wall"
    )
    return (
        new_field,
        grad_first[None],
        grad_second[None],
        grad_third[None],
        grad_fourth[None],
        grad_last[None],
    )


def solution(mesh):
    in_specs = (
        P(None, None, None, "span", "wall", None),
        P(None, None, None, None, "span", "wall", None),
        P(("span", "wall")),
        P(("span", "wall"), None),
        P(("span", "wall"), None),
        P("span", None, None),
        P("span", None, None),
        P("span", None, None),
        P("span", None, None),
        P("span", None, None),
    )
    out_specs = (
        P(None, None, None, "span", "wall", None),
        P("span", None, None),
        P("span", None, None),
        P("span", None, None),
        P("span", None, None),
        P("span", None, None),
    )
    return jax.shard_map(local, mesh=mesh, in_specs=in_specs, out_specs=out_specs, check_vma=False)
```

profile of v0, /device:TPU:2, one launch (start us, length us, event | category | flops | bytes accessed | tf_op | source)
XLA Modules:
  0.0 1055.6 jit_solution(4390853622651327145)
XLA Ops:
  7.2 1.2 slice_bitcast_fusion.14
  8.6 1.8 collective-permute-start
  10.4 1.3 collective-permute-start.1
  11.9 3.4 collective-permute-start.2
  15.3 12.5 %collective-permute-start.3 = (f32[2,5,5,5,1,1,128]{6,5,4,3,2,1,0:T(1,128)S(1)}, f32[2,5,5,5,1,1,128]{6,5,4,3,2,1,0:T(1,128)S(1)}, u32[]{:S(2)}, u32[]{:S(2)}) collective-permute-start(f32[2,5,5,5,1,1,128]{6,5,4,3,2,1,0:T(1,128)S(1)} %get-tuple-element.38), channel_id=1, source_target_pairs={{1,0},{2,1},{3,2},{4,3},{5,4},{6,5},{7,6},{8,7},{9,8},{10,9},{11,1... | collective-permute-start | bytes 384008 | tf_op jit(solution)/shard_map/ppermute | solution.py:24
  28.3 1.3 scatter_custom_fusion.1
  29.6 0.7 all_to_all.16
  30.3 18.8 %all-to-all-start.1 = ((bf16[32,1,16]{2,1,0:T(2,128)(2,1)}), bf16[32,1,16]{2,1,0:T(2,128)(2,1)S(1)}, u32[]{:S(2)}, u32[]{:S(2)}) async-start(bf16[32,1,16]{2,1,0:T(2,128)(2,1)} %all_to_all.16), calls=%async_computation.1 | async-start | bytes 32768 | tf_op jit(solution)/shard_map/all_to_all | solution.py:244
  49.8 0.3 fusion.65
  50.1 0.3 fusion.63
  50.6 0.3 fusion.44
  51.2 0.3 fusion.49
  51.5 0.3 fusion.53
  52.0 0.3 fusion.51
  53.0 0.3 fusion.30
  53.3 0.3 fusion.57
  54.6 0.3 fusion.38
  57.8 0.3 maximum_bitcast_fusion
  58.2 0.8 fusion.24
  59.0 0.8 fusion.22
  60.1 0.3 pad_maximum_fusion
  60.7 1.2 fusion
  62.0 1.2 fusion.2
  63.3 0.4 fusion.20
  64.2 2.0 scatter_custom_fusion
  66.2 2.5 all-to-all-done.1
  68.7 17.3 %all-to-all-start = ((bf16[32,16,128]{2,1,0:T(8,128)(2,1)}), bf16[32,16,128]{2,1,0:T(8,128)(2,1)S(1)}, u32[]{:S(2)}, u32[]{:S(2)}) async-start(bf16[32,16,128]{2,1,0:T(8,128)(2,1)} %bitcast.135), calls=%async_computation | async-start | bytes 262144 | tf_op jit(solution)/shard_map/all_to_all | solution.py:230
  86.1 1.7 scatter_custom_fusion.2
  87.8 0.6 convert_reduce_fusion
  89.1 21.7 %all-to-all-done = bf16[32,16,128]{2,1,0:T(8,128)(2,1)S(1)} async-done(((bf16[32,16,128]{2,1,0:T(8,128)(2,1)}), bf16[32,16,128]{2,1,0:T(8,128)(2,1)S(1)}, u32[]{:S(2)}, u32[]{:S(2)}) %all-to-all-start) | async-done | bytes 131104 | tf_op jit(solution)/shard_map/all_to_all | solution.py:230
  110.8 7.7 all-to-all-start.2
  119.2 0.6 copy-done.18
  120.1 0.3 multiply_convert_fusion
  120.5 22.8 %all-to-all-done.2 = bf16[32,16,128]{2,1,0:T(8,128)(2,1)S(1)} async-done(((bf16[32,16,128]{2,1,0:T(8,128)(2,1)}), bf16[32,16,128]{2,1,0:T(8,128)(2,1)S(1)}, u32[]{:S(2)}, u32[]{:S(2)}) %all-to-all-start.2) | async-done | bytes 131104 | tf_op jit(solution)/shard_map/all_to_all | solution.py:237
  143.5 0.9 convolution_bitcast_fusion.3
  144.7 1.0 convolution_bitcast_fusion
  145.8 0.3 fusion.9
  146.1 1.0 convolution_bitcast_fusion.1
  147.1 0.3 fusion.10
  147.5 1.0 convolution_bitcast_fusion.2
  148.5 1.1 fusion.21
  149.7 0.7 copy.80
  150.4 893.0 %all-reduce.3.cloned.1.call-done = (f32[1,128,256]{2,1,0:T(8,128)}, f32[1,256,256]{2,1,0:T(8,128)}, f32[1,256,256]{2,1,0:T(8,128)}, f32[1,256,256]{2,1,0:T(8,128)}, f32[1,256,128]{2,1,0:T(8,128)}) async-done(((f32[1,128,256]{2,1,0:T(8,128)}, f32[1,256,256]{2,1,0:T(8,128)}, f32[1,256,256]{2,1,0:T(8,128)}, f32[1,256,256]{2,1,0:T(8,128)}, f32[1,256,128]{2,1,0:T(8,128)}), (f32[1,128,256]{2,1,0:T(8,128)}, ...) | async-done | bytes 1048592 | tf_op jit(solution)/shard_map/psum | solution.py:273
  1043.4 1.6 copy.197
  1045.0 1.7 copy.198
  1046.7 0.7 copy.199
  1047.4 0.7 copy.200
  1048.1 0.7 copy.201
  (107 shorter events, 8.8 us)
Async XLA Ops:
  7.2 113.0 %copy-start = (bf16[1,256,256]{2,1,0:T(8,128)(2,1)S(1)}, bf16[1,256,256]{2,1,0:T(8,128)(2,1)}, u32[]{:S(2)}) copy-start(bf16[1,256,256]{2,1,0:T(8,128)(2,1)} %param.23) | copy-start | bytes 393220
  7.2 1.3 copy-start.1
  8.4 19.4 %copy-start.13 = (s32[128,1]{0,1:T(1,128)S(1)}, s32[128,1]{0,1:T(1,128)}, u32[]{:S(2)}) copy-start(s32[128,1]{0,1:T(1,128)} %param.18) | copy-start | bytes 1540
  8.5 40.7 %copy-start.9 = (f32[5,1,1,1,1]{0,1,4,3,2:T(1,128)S(1)}, f32[5,1,1,1,1]{0,1,4,3,2:T(1,128)}, u32[]{:S(2)}) copy-start(f32[5,1,1,1,1]{0,1,4,3,2:T(1,128)} %constant.85) | copy-start | bytes 64
  8.5 41.0 %copy-start.8 = (f32[5,1,1,1,1]{0,1,4,3,2:T(1,128)S(1)}, f32[5,1,1,1,1]{0,1,4,3,2:T(1,128)}, u32[]{:S(2)}) copy-start(f32[5,1,1,1,1]{0,1,4,3,2:T(1,128)} %constant.86) | copy-start | bytes 64
  8.6 51.4 %collective-permute-start = (f32[2,5,5,5,1,2,128]{6,5,4,3,2,1,0:T(2,128)S(1)}, f32[2,5,5,5,1,2,128]{6,5,4,3,2,1,0:T(2,128)S(1)}, u32[]{:S(2)}, u32[]{:S(2)}) collective-permute-start(f32[2,5,5,5,1,2,128]{6,5,4,3,2,1,0:T(2,128)S(1)} %pad_maximum_fusion.1), channel_id=1, source_target_pairs={{0,32},{32,64},{64,96},{96,128},{128,160},{160,192},{192,224},{224... | collective-permute-start | bytes 768008 | tf_op jit(solution)/shard_map/ppermute | solution.py:23
  10.4 49.7 %collective-permute-start.1 = (f32[2,5,5,5,1,2,128]{6,5,4,3,2,1,0:T(2,128)S(1)}, f32[2,5,5,5,1,2,128]{6,5,4,3,2,1,0:T(2,128)S(1)}, u32[]{:S(2)}, u32[]{:S(2)}) collective-permute-start(f32[2,5,5,5,1,2,128]{6,5,4,3,2,1,0:T(2,128)S(1)} %pad_maximum_fusion.1), channel_id=1, source_target_pairs={{32,0},{64,32},{96,64},{128,96},{160,128},{192,160},{224,192},{256... | collective-permute-start | bytes 768008 | tf_op jit(solution)/shard_map/ppermute | solution.py:24
  11.7 38.7 %copy-start.2 = (f32[3,5,5,5,1,2,128]{6,5,4,3,2,1,0:T(2,128)S(1)}, f32[3,5,5,5,1,2,128]{6,5,4,3,2,1,0:T(2,128)}, u32[]{:S(2)}) copy-start(f32[3,5,5,5,1,2,128]{6,5,4,3,2,1,0:T(2,128)} %param.16) | copy-start | bytes 1152004
  11.9 45.9 %collective-permute-start.2 = (f32[2,5,5,5,1,1,128]{6,5,4,3,2,1,0:T(1,128)S(1)}, f32[2,5,5,5,1,1,128]{6,5,4,3,2,1,0:T(1,128)S(1)}, u32[]{:S(2)}, u32[]{:S(2)}) collective-permute-start(f32[2,5,5,5,1,1,128]{6,5,4,3,2,1,0:T(1,128)S(1)} %get-tuple-element.37), channel_id=1, source_target_pairs={{0,1},{1,2},{2,3},{3,4},{4,5},{5,6},{6,7},{7,8},{8,9},{9,10},{10,1... | collective-permute-start | bytes 384008 | tf_op jit(solution)/shard_map/ppermute | solution.py:23
  15.3 42.5 %collective-permute-start.3 = (f32[2,5,5,5,1,1,128]{6,5,4,3,2,1,0:T(1,128)S(1)}, f32[2,5,5,5,1,1,128]{6,5,4,3,2,1,0:T(1,128)S(1)}, u32[]{:S(2)}, u32[]{:S(2)}) collective-permute-start(f32[2,5,5,5,1,1,128]{6,5,4,3,2,1,0:T(1,128)S(1)} %get-tuple-element.38), channel_id=1, source_target_pairs={{1,0},{2,1},{3,2},{4,3},{5,4},{6,5},{7,6},{8,7},{9,8},{10,9},{11,1... | collective-permute-start | bytes 384008 | tf_op jit(solution)/shard_map/ppermute | solution.py:24
  30.3 38.4 %all-to-all-start.1 = ((bf16[32,1,16]{2,1,0:T(2,128)(2,1)}), bf16[32,1,16]{2,1,0:T(2,128)(2,1)S(1)}, u32[]{:S(2)}, u32[]{:S(2)}) async-start(bf16[32,1,16]{2,1,0:T(2,128)(2,1)} %all_to_all.16), calls=%async_computation.1 | async-start | bytes 32768 | tf_op jit(solution)/shard_map/all_to_all | solution.py:244
  53.0 2.2 copy-start.10
  55.2 2.1 copy-start.20
  57.4 0.7 copy-start.17
  57.8 1.2 copy-start.16
  60.0 0.7 copy-start.15
  60.7 1.3 copy-start.14
  61.9 1.4 copy-start.11
  62.0 1.4 copy-start.12
  63.9 54.8 %copy-start.7 = (bf16[1,128,256]{2,1,0:T(8,128)(2,1)S(1)}, bf16[1,128,256]{2,1,0:T(8,128)(2,1)}, u32[]{:S(2)}) copy-start(bf16[1,128,256]{2,1,0:T(8,128)(2,1)} %param.20) | copy-start | bytes 196612
  66.2 52.8 %copy-start.19 = (bf16[1,256,256]{2,1,0:T(8,128)(2,1)S(1)}, bf16[1,256,256]{2,1,0:T(8,128)(2,1)}, u32[]{:S(2)}) copy-start(bf16[1,256,256]{2,1,0:T(8,128)(2,1)} %param.21) | copy-start | bytes 393220
  68.7 42.1 %all-to-all-start = ((bf16[32,16,128]{2,1,0:T(8,128)(2,1)}), bf16[32,16,128]{2,1,0:T(8,128)(2,1)S(1)}, u32[]{:S(2)}, u32[]{:S(2)}) async-start(bf16[32,16,128]{2,1,0:T(8,128)(2,1)} %bitcast.135), calls=%async_computation | async-start | bytes 262144 | tf_op jit(solution)/shard_map/all_to_all | solution.py:230
  110.8 32.5 %all-to-all-start.2 = ((bf16[32,16,128]{2,1,0:T(8,128)(2,1)}), bf16[32,16,128]{2,1,0:T(8,128)(2,1)S(1)}, u32[]{:S(2)}, u32[]{:S(2)}) async-start(bf16[32,16,128]{2,1,0:T(8,128)(2,1)} %bitcast.142), calls=%async_computation.2 | async-start | bytes 262144 | tf_op jit(solution)/shard_map/all_to_all | solution.py:237
  118.5 924.9 %all-reduce.3.cloned.1.call-start = ((), (), s32[]{:S(2)}) async-start(), calls=%async_computation.3 | async-start | bytes 2097152 | tf_op jit(solution)/shard_map/psum | solution.py:273
  118.9 0.9 copy-start.18
  120.1 23.1 %copy-start.6 = (bf16[1,256,128]{2,1,0:T(8,128)(2,1)S(1)}, bf16[1,256,128]{2,1,0:T(8,128)(2,1)}, u32[]{:S(2)}) copy-start(bf16[1,256,128]{2,1,0:T(8,128)(2,1)} %param.24) | copy-start | bytes 196612
  1043.4 3.3 copy-start.4
  1043.4 4.0 copy-start.3
  1045.0 3.1 copy-start.5
Sparse Core Ops, SparseCore 0:
  149.8 893.5 all-reduce.2
where the time goes:
time: 1060 us
  waiting for transfers between devices  940 us (89%)
  starting transfers between devices  62.8 us (6%)
  matrix products  18 us (2%)
  between operations  15.5 us (1%)
  local copies, waits for them, and re-layouts  14.2 us (1%)
    psum x1, waiting for transfers between devices, local(): lax.psum((grad_first, grad_second, grad_third, grad_fourth, grad_last), '...  893 us
    all_to_all x1, waiting for transfers between devices, local(): lax.all_to_all(target_buffer.reshape(span_count, slot_count, -1), 'span',...  22.8 us
    all_to_all x1, waiting for transfers between devices, local(): lax.all_to_all(row_buffer.reshape(span_count, slot_count, FEAT), 'span',...  21.7 us
  transfers between devices with their start and end apart: 8, of which 4 were waited for; matrix products, arithmetic and copies ran while one was open for 2% of the time, Pallas kernels for 0%

commit v1 on v0

--- a/solution.py
+++ b/solution.py
@@ -215,43 +215,17 @@
     onehot = (dest[:, None] == jnp.arange(span_count, dtype=jnp.int32)[None, :]).astype(jnp.int32)
     slots = jnp.sum((jnp.cumsum(onehot, axis=0) - 1) * onehot, axis=1)
     position = dest * slot_count + slots
-    row_buffer = jnp.zeros((span_count * slot_count, FEAT), jnp.bfloat16).at[position].set(rows)
-    target_buffer = (
-        jnp.zeros((span_count * slot_count, targets.shape[1]), jnp.bfloat16)
-        .at[position]
-        .set(targets)
-    )
-    flag_buffer = (
-        jnp.zeros((span_count * slot_count,), jnp.bfloat16)
-        .at[position]
-        .set(jnp.ones((rows.shape[0],), jnp.bfloat16))
-    )
-    got_rows, got_targets, got_flags = (
-        lax.all_to_all(
-            row_buffer.reshape(span_count, slot_count, FEAT),
-            "span",
-            split_axis=0,
-            concat_axis=0,
-            tiled=True,
-        ),
-        lax.all_to_all(
-            target_buffer.reshape(span_count, slot_count, -1),
-            "span",
-            split_axis=0,
-            concat_axis=0,
-            tiled=True,
-        ),
-        lax.all_to_all(
-            flag_buffer.reshape(span_count, slot_count),
-            "span",
-            split_axis=0,
-            concat_axis=0,
-            tiled=True,
-        ),
-    )
-    inputs = got_rows.reshape(span_count * slot_count, FEAT)
-    wanted = got_targets.reshape(span_count * slot_count, -1).astype(jnp.float32)
-    flags = got_flags.reshape(span_count * slot_count).astype(jnp.float32)
+    out_width = targets.shape[1]
+    flag_block = jnp.zeros((rows.shape[0], 128), jnp.bfloat16).at[:, 0].set(1.0)
+    payload = jnp.concatenate([rows, targets, flag_block], axis=1)
+    width = payload.shape[1]
+    buffer = jnp.zeros((span_count * slot_count, width), jnp.bfloat16).at[position].set(payload)
+    got = lax.all_to_all(
+        buffer.reshape(span_count, slot_count, width), "span", split_axis=0, concat_axis=0, tiled=True
+    ).reshape(span_count * slot_count, width)
+    inputs = got[:, :FEAT]
+    wanted = got[:, FEAT : FEAT + out_width].astype(jnp.float32)
+    flags = got[:, FEAT + out_width].astype(jnp.float32)
     row_scale = flags / jnp.maximum(jnp.sum(flags), 1.0)
     layer_one = weight_in[0]
     layer_two = weight_two[0]
@@ -270,17 +244,40 @@
     grad_second = weight_grad(acts[1], error)
     error = backward_layer(error, layer_two, pres[0])
     grad_first = weight_grad(acts[0], error)
-    grad_first, grad_second, grad_third, grad_fourth, grad_last = lax.psum(
-        (grad_first, grad_second, grad_third, grad_fourth, grad_last), "wall"
-    )
-    return (
-        new_field,
-        grad_first[None],
-        grad_second[None],
-        grad_third[None],
-        grad_fourth[None],
-        grad_last[None],
-    )
+    grads = (grad_first, grad_second, grad_third, grad_fourth, grad_last)
+    summed = wall_sum(grads)
+    return (new_field,) + tuple(g[None] for g in summed)
+
+
+def wall_sum(grads):
+    size = lax.axis_size("wall")
+    bits = size.bit_length() - 1
+    if (1 << bits) != size:
+        return lax.psum(grads, "wall")
+    lanes = 128
+    flat = jnp.concatenate([g.reshape(-1, lanes) for g in grads], axis=0)
+    me = lax.axis_index("wall")
+    for bit in range(bits):
+        mine = (me >> bit) & 1
+        halves = flat.reshape(2, flat.shape[0] // 2, lanes)
+        keep = lax.dynamic_index_in_dim(halves, mine, 0, keepdims=False)
+        send = lax.dynamic_index_in_dim(halves, 1 - mine, 0, keepdims=False)
+        pairs = [(i, i ^ (1 << bit)) for i in range(size)]
+        flat = keep + lax.ppermute(send, "wall", pairs)
+    for bit in reversed(range(bits)):
+        mine = (me >> bit) & 1
+        pairs = [(i, i ^ (1 << bit)) for i in range(size)]
+        other = lax.ppermute(flat, "wall", pairs)
+        low = jnp.where(mine == 0, flat, other)
+        high = jnp.where(mine == 0, other, flat)
+        flat = jnp.concatenate([low, high], axis=0)
+    out = []
+    at = 0
+    for g in grads:
+        rows_of = g.size // lanes
+        out.append(flat[at : at + rows_of].reshape(g.shape))
+        at += rows_of
+    return tuple(out)
 
 
 def solution(mesh):

time: 1060 us -> 288 us (0.27)
  the two profiles are of different devices: /device:TPU:2 before, /device:TPU:30 now
where the time goes in v1:
time: 288 us; the launch traced here: 287 us
  waiting for transfers between devices  171 us (59%)
  starting transfers between devices  82 us (28%)
  matrix products  14.5 us (5%)
  local copies, waits for them, and re-layouts  10.3 us (4%)
  other arithmetic  6.06 us (2%)
  between operations  3.11 us (1%)
    ppermute x5, waiting for transfers between devices, wall_sum(): flat = keep + lax.ppermute(send, 'wall', pairs)  57.4 us
    ppermute x5, waiting for transfers between devices, wall_sum(): other = lax.ppermute(flat, 'wall', pairs)  52.3 us
    all_to_all x1, waiting for transfers between devices, local(): lax.all_to_all(buffer.reshape(span_count, slot_count, width), 'span', spl...  42.2 us
    ppermute x2, starting transfers between devices, extended(): before = lax.ppermute(last, axis, up)  31.6 us
    all_to_all x1, starting transfers between devices, local(): lax.all_to_all(buffer.reshape(span_count, slot_count, width), 'span', spl...  27.6 us
    ppermute x2, waiting for transfers between devices, extended(): after = lax.ppermute(first, axis, down)  19 us
    ppermute x5, starting transfers between devices, wall_sum(): other = lax.ppermute(flat, 'wall', pairs)  9.87 us
    ppermute x5, starting transfers between devices, wall_sum(): flat = keep + lax.ppermute(send, 'wall', pairs)  9.6 us
  transfers between devices with their start and end apart: 15, of which 12 were waited for; matrix products, arithmetic and copies ran while one was open for 4% of the time, Pallas kernels for 0%

profile of v1, /device:TPU:30, one launch (start us, length us, event | category | flops | bytes accessed | tf_op | source)
XLA Modules:
  0.0 286.9 jit_solution(14197406736137549541)
XLA Ops:
  0.7 1.3 slice_bitcast_fusion.15
  2.1 1.4 collective-permute-start.1
  3.5 3.0 %collective-permute-start = (f32[2,5,5,5,1,2,128]{6,5,4,3,2,1,0:T(2,128)S(1)}, f32[2,5,5,5,1,2,128]{6,5,4,3,2,1,0:T(2,128)S(1)}, u32[]{:S(2)}, u32[]{:S(2)}) collective-permute-start(f32[2,5,5,5,1,2,128]{6,5,4,3,2,1,0:T(2,128)S(1)} %pad_maximum_fusion.4), channel_id=1, source_target_pairs={{0,32},{32,64},{64,96},{96,128},{128,160},{160,192},{192,224},{224... | collective-permute-start | bytes 768008 | tf_op jit(solution)/shard_map/ppermute | solution.py:23
  6.8 28.5 %collective-permute-start.2 = (f32[2,5,5,5,1,1,128]{6,5,4,3,2,1,0:T(1,128)S(1)}, f32[2,5,5,5,1,1,128]{6,5,4,3,2,1,0:T(1,128)S(1)}, u32[]{:S(2)}, u32[]{:S(2)}) collective-permute-start(f32[2,5,5,5,1,1,128]{6,5,4,3,2,1,0:T(1,128)S(1)} %get-tuple-element.53), channel_id=1, source_target_pairs={{0,1},{1,2},{2,3},{3,4},{4,5},{5,6},{6,7},{7,8},{8,9},{9,10},{10,1... | collective-permute-start | bytes 384008 | tf_op jit(solution)/shard_map/ppermute | solution.py:23
  35.4 1.9 collective-permute-start.3
  37.3 0.6 compare_reduce_fusion
  47.8 19.0 %collective-permute-done.3 = f32[2,5,5,5,1,1,128]{6,5,4,3,2,1,0:T(1,128)S(1)} collective-permute-done((f32[2,5,5,5,1,1,128]{6,5,4,3,2,1,0:T(1,128)S(1)}, f32[2,5,5,5,1,1,128]{6,5,4,3,2,1,0:T(1,128)S(1)}, u32[]{:S(2)}, u32[]{:S(2)}) %collective-permute-start.3) | collective-permute-done | bytes 128032 | tf_op jit(solution)/shard_map/ppermute | solution.py:24
  66.7 0.3 maximum_bitcast_fusion
  67.1 0.8 fusion.21
  67.9 0.8 fusion.23
  69.4 1.2 fusion
  70.7 1.2 fusion.2
  72.1 0.4 fusion.20
  73.1 0.7 gather_fusion
  73.9 1.8 scatter_custom_fusion
  75.7 27.6 %all-to-all-start = ((bf16[32,16,384]{2,1,0:T(8,128)(2,1)}), bf16[32,16,384]{2,1,0:T(8,128)(2,1)S(1)}, u32[]{:S(2)}, u32[]{:S(2)}) async-start(bf16[32,16,384]{2,1,0:T(8,128)(2,1)} %bitcast.136), calls=%async_computation | async-start | bytes 786432 | tf_op jit(solution)/shard_map/all_to_all | solution.py:223
  103.4 42.2 %all-to-all-done = bf16[32,16,384]{2,1,0:T(8,128)(2,1)S(1)} async-done(((bf16[32,16,384]{2,1,0:T(8,128)(2,1)}), bf16[32,16,384]{2,1,0:T(8,128)(2,1)S(1)}, u32[]{:S(2)}, u32[]{:S(2)}) %all-to-all-start) | async-done | bytes 393248 | tf_op jit(solution)/shard_map/all_to_all | solution.py:223
  145.6 0.7 convert_reduce_fusion
  147.4 0.6 copy-done.15
  148.6 0.6 copy-done.3
  151.5 0.5 fusion.12
  152.2 0.4 convolution_dynamic-update-slice_fusion
  152.6 1.9 collective-permute-start.4
  154.6 13.5 %collective-permute-done.4 = f32[1024,128]{1,0:T(8,128)S(1)} collective-permute-done((f32[1024,128]{1,0:T(8,128)S(1)}, f32[1024,128]{1,0:T(8,128)S(1)}, u32[]{:S(2)}, u32[]{:S(2)}) %collective-permute-start.4) | collective-permute-done | bytes 524320 | tf_op jit(solution)/shard_map/ppermute | solution.py:266
  168.1 1.9 collective-permute-start.5
  170.0 10.5 %collective-permute-done.5 = f32[512,128]{1,0:T(8,128)S(1)} collective-permute-done((f32[512,128]{1,0:T(8,128)S(1)}, f32[512,128]{1,0:T(8,128)S(1)}, u32[]{:S(2)}, u32[]{:S(2)}) %collective-permute-start.5) | collective-permute-done | bytes 262176 | tf_op jit(solution)/shard_map/ppermute | solution.py:266
  180.6 1.9 collective-permute-start.6
  182.5 5.5 %collective-permute-done.6 = f32[256,128]{1,0:T(8,128)S(1)} collective-permute-done((f32[256,128]{1,0:T(8,128)S(1)}, f32[256,128]{1,0:T(8,128)S(1)}, u32[]{:S(2)}, u32[]{:S(2)}) %collective-permute-start.6) | collective-permute-done | bytes 131104 | tf_op jit(solution)/shard_map/ppermute | solution.py:266
  188.1 1.9 collective-permute-start.7
  190.0 5.7 %collective-permute-done.7 = f32[128,128]{1,0:T(8,128)S(1)} collective-permute-done((f32[128,128]{1,0:T(8,128)S(1)}, f32[128,128]{1,0:T(8,128)S(1)}, u32[]{:S(2)}, u32[]{:S(2)}) %collective-permute-start.7) | collective-permute-done | bytes 65568 | tf_op jit(solution)/shard_map/ppermute | solution.py:266
  195.8 1.9 collective-permute-start.8
  197.7 22.2 %collective-permute-done.8 = f32[64,128]{1,0:T(8,128)S(1)} collective-permute-done((f32[64,128]{1,0:T(8,128)S(1)}, f32[64,128]{1,0:T(8,128)S(1)}, u32[]{:S(2)}, u32[]{:S(2)}) %collective-permute-start.8) | collective-permute-done | bytes 32800 | tf_op jit(solution)/shard_map/ppermute | solution.py:266
  219.9 1.9 collective-permute-start.9
  221.8 22.2 %collective-permute-done.9 = f32[64,128]{1,0:T(8,128)S(1)} collective-permute-done((f32[64,128]{1,0:T(8,128)S(1)}, f32[64,128]{1,0:T(8,128)S(1)}, u32[]{:S(2)}, u32[]{:S(2)}) %collective-permute-start.9) | collective-permute-done | bytes 32800 | tf_op jit(solution)/shard_map/ppermute | solution.py:270
  244.0 1.9 collective-permute-start.10
  246.0 6.4 %collective-permute-done.10 = f32[128,128]{1,0:T(8,128)S(1)} collective-permute-done((f32[128,128]{1,0:T(8,128)S(1)}, f32[128,128]{1,0:T(8,128)S(1)}, u32[]{:S(2)}, u32[]{:S(2)}) %collective-permute-start.10) | collective-permute-done | bytes 65568 | tf_op jit(solution)/shard_map/ppermute | solution.py:270
  252.4 2.2 collective-permute-start.11
  254.7 4.6 %collective-permute-done.11 = f32[256,128]{1,0:T(8,128)S(1)} collective-permute-done((f32[256,128]{1,0:T(8,128)S(1)}, f32[256,128]{1,0:T(8,128)S(1)}, u32[]{:S(2)}, u32[]{:S(2)}) %collective-permute-start.11) | collective-permute-done | bytes 131104 | tf_op jit(solution)/shard_map/ppermute | solution.py:270
  259.4 1.9 collective-permute-start.12
  261.3 10.6 %collective-permute-done.12 = f32[512,128]{1,0:T(8,128)S(1)} collective-permute-done((f32[512,128]{1,0:T(8,128)S(1)}, f32[512,128]{1,0:T(8,128)S(1)}, u32[]{:S(2)}, u32[]{:S(2)}) %collective-permute-start.12) | collective-permute-done | bytes 262176 | tf_op jit(solution)/shard_map/ppermute | solution.py:270
  272.0 1.9 collective-permute-start.13
  274.0 0.7 copy.79
  274.7 8.4 %collective-permute-done.13 = f32[1024,128]{1,0:T(8,128)S(1)} collective-permute-done((f32[1024,128]{1,0:T(8,128)S(1)}, f32[1024,128]{1,0:T(8,128)S(1)}, u32[]{:S(2)}, u32[]{:S(2)}) %collective-permute-start.13) | collective-permute-done | bytes 524320 | tf_op jit(solution)/shard_map/ppermute | solution.py:270
  283.2 0.7 slice_bitcast_fusion
  283.9 0.8 broadcast_in_dim_reshape.15
  284.7 0.7 broadcast_in_dim_reshape.12
  285.4 0.8 broadcast_in_dim_reshape.14
  286.2 0.8 broadcast_in_dim_reshape.13
  (144 shorter events, 14.6 us)
Async XLA Ops:
  0.6 147.7 %copy-start = (bf16[1,256,256]{2,1,0:T(8,128)(2,1)S(1)}, bf16[1,256,256]{2,1,0:T(8,128)(2,1)}, u32[]{:S(2)}) copy-start(bf16[1,256,256]{2,1,0:T(8,128)(2,1)} %param.24) | copy-start | bytes 393220
  0.6 37.3 %copy-start.4 = (f32[5,1,1,1,1]{0,1,4,3,2:T(1,128)S(1)}, f32[5,1,1,1,1]{0,1,4,3,2:T(1,128)}, u32[]{:S(2)}) copy-start(f32[5,1,1,1,1]{0,1,4,3,2:T(1,128)} %constant.163) | copy-start | bytes 64
  0.7 1.3 copy-start.1
  0.7 37.3 %copy-start.18 = (s32[128]{0:T(128)S(1)}, s32[128]{0:T(128)}, u32[]{:S(2)}) copy-start(s32[128]{0:T(128)} %param.19) | copy-start | bytes 1540
  1.9 36.9 %copy-start.5 = (f32[5,1,1,1,1]{0,1,4,3,2:T(1,128)S(1)}, f32[5,1,1,1,1]{0,1,4,3,2:T(1,128)}, u32[]{:S(2)}) copy-start(f32[5,1,1,1,1]{0,1,4,3,2:T(1,128)} %constant.162) | copy-start | bytes 64
  2.1 37.7 %copy-start.2 = (f32[3,5,5,5,1,2,128]{6,5,4,3,2,1,0:T(2,128)S(1)}, f32[3,5,5,5,1,2,128]{6,5,4,3,2,1,0:T(2,128)}, u32[]{:S(2)}) copy-start(f32[3,5,5,5,1,2,128]{6,5,4,3,2,1,0:T(2,128)} %param.18) | copy-start | bytes 1152004
  2.1 66.8 %collective-permute-start.1 = (f32[2,5,5,5,1,2,128]{6,5,4,3,2,1,0:T(2,128)S(1)}, f32[2,5,5,5,1,2,128]{6,5,4,3,2,1,0:T(2,128)S(1)}, u32[]{:S(2)}, u32[]{:S(2)}) collective-permute-start(f32[2,5,5,5,1,2,128]{6,5,4,3,2,1,0:T(2,128)S(1)} %pad_maximum_fusion.4), channel_id=1, source_target_pairs={{32,0},{64,32},{96,64},{128,96},{160,128},{192,160},{224,192},{256... | collective-permute-start | bytes 768008 | tf_op jit(solution)/shard_map/ppermute | solution.py:24
  3.5 65.4 %collective-permute-start = (f32[2,5,5,5,1,2,128]{6,5,4,3,2,1,0:T(2,128)S(1)}, f32[2,5,5,5,1,2,128]{6,5,4,3,2,1,0:T(2,128)S(1)}, u32[]{:S(2)}, u32[]{:S(2)}) collective-permute-start(f32[2,5,5,5,1,2,128]{6,5,4,3,2,1,0:T(2,128)S(1)} %pad_maximum_fusion.4), channel_id=1, source_target_pairs={{0,32},{32,64},{64,96},{96,128},{128,160},{160,192},{192,224},{224... | collective-permute-start | bytes 768008 | tf_op jit(solution)/shard_map/ppermute | solution.py:23
  6.8 41.0 %collective-permute-start.2 = (f32[2,5,5,5,1,1,128]{6,5,4,3,2,1,0:T(1,128)S(1)}, f32[2,5,5,5,1,1,128]{6,5,4,3,2,1,0:T(1,128)S(1)}, u32[]{:S(2)}, u32[]{:S(2)}) collective-permute-start(f32[2,5,5,5,1,1,128]{6,5,4,3,2,1,0:T(1,128)S(1)} %get-tuple-element.53), channel_id=1, source_target_pairs={{0,1},{1,2},{2,3},{3,4},{4,5},{5,6},{6,7},{7,8},{8,9},{9,10},{10,1... | collective-permute-start | bytes 384008 | tf_op jit(solution)/shard_map/ppermute | solution.py:23
  35.4 31.4 %collective-permute-start.3 = (f32[2,5,5,5,1,1,128]{6,5,4,3,2,1,0:T(1,128)S(1)}, f32[2,5,5,5,1,1,128]{6,5,4,3,2,1,0:T(1,128)S(1)}, u32[]{:S(2)}, u32[]{:S(2)}) collective-permute-start(f32[2,5,5,5,1,1,128]{6,5,4,3,2,1,0:T(1,128)S(1)} %get-tuple-element.54), channel_id=1, source_target_pairs={{1,0},{2,1},{3,2},{4,3},{5,4},{6,5},{7,6},{8,7},{9,8},{10,9},{11,1... | collective-permute-start | bytes 384008 | tf_op jit(solution)/shard_map/ppermute | solution.py:24
  39.8 2.0 copy-start.6
  42.5 2.9 %copy-start.10 = (s32[128,1]{0,1:T(1,128)S(1)}, s32[128,1]{0,1:T(1,128)}, u32[]{:S(2)}) copy-start(s32[128,1]{0,1:T(1,128)} %param.20) | copy-start | bytes 1540
  45.5 21.6 %copy-start.14 = (f32[5,1,1,1,1,1]{0,1,5,4,3,2:T(1,128)S(1)}, f32[5,1,1,1,1,1]{0,1,5,4,3,2:T(1,128)}, u32[]{:S(2)}) copy-start(f32[5,1,1,1,1,1]{0,1,5,4,3,2:T(1,128)} %constant.166) | copy-start | bytes 64
  47.7 20.2 %copy-start.13 = (f32[5,1,1,1,1,1]{0,1,5,4,3,2:T(1,128)S(1)}, f32[5,1,1,1,1,1]{0,1,5,4,3,2:T(1,128)}, u32[]{:S(2)}) copy-start(f32[5,1,1,1,1,1]{0,1,5,4,3,2:T(1,128)} %constant.165) | copy-start | bytes 64
  68.8 0.7 copy-start.12
  69.4 1.2 copy-start.11
  70.6 1.4 copy-start.8
  70.6 1.4 copy-start.9
  72.1 1.8 copy-start.7
  73.0 74.1 %copy-start.16 = (bf16[1,128,256]{2,1,0:T(8,128)(2,1)S(1)}, bf16[1,128,256]{2,1,0:T(8,128)(2,1)}, u32[]{:S(2)}) copy-start(bf16[1,128,256]{2,1,0:T(8,128)(2,1)} %param.22) | copy-start | bytes 196612
  75.7 69.9 %all-to-all-start = ((bf16[32,16,384]{2,1,0:T(8,128)(2,1)}), bf16[32,16,384]{2,1,0:T(8,128)(2,1)S(1)}, u32[]{:S(2)}, u32[]{:S(2)}) async-start(bf16[32,16,384]{2,1,0:T(8,128)(2,1)} %bitcast.136), calls=%async_computation | async-start | bytes 786432 | tf_op jit(solution)/shard_map/all_to_all | solution.py:223
  147.1 0.9 copy-start.15
  148.3 0.9 copy-start.3
  148.3 1.1 copy-start.17
  152.6 15.4 %collective-permute-start.4 = (f32[1024,128]{1,0:T(8,128)S(1)}, f32[1024,128]{1,0:T(8,128)S(1)}, u32[]{:S(2)}, u32[]{:S(2)}) collective-permute-start(f32[1024,128]{1,0:T(8,128)S(1)} %dynamic-slice_bitcast_fusion), channel_id=1, source_target_pairs={{0,1},{1,0},{2,3},{3,2},{4,5},{5,4},{6,7},{7,6},{8,9},{9,8},{10,11... | collective-permute-start | bytes 1572872 | tf_op jit(solution)/shard_map/ppermute | solution.py:266
  168.1 12.4 %collective-permute-start.5 = (f32[512,128]{1,0:T(8,128)S(1)}, f32[512,128]{1,0:T(8,128)S(1)}, u32[]{:S(2)}, u32[]{:S(2)}) collective-permute-start(f32[512,128]{1,0:T(8,128)S(1)} %dynamic-slice_bitcast_fusion.1), channel_id=1, source_target_pairs={{0,2},{1,3},{2,0},{3,1},{4,6},{5,7},{6,4},{7,5},{8,10},{9,11},{10,... | collective-permute-start | bytes 786440 | tf_op jit(solution)/shard_map/ppermute | solution.py:266
  180.6 7.4 %collective-permute-start.6 = (f32[256,128]{1,0:T(8,128)S(1)}, f32[256,128]{1,0:T(8,128)S(1)}, u32[]{:S(2)}, u32[]{:S(2)}) collective-permute-start(f32[256,128]{1,0:T(8,128)S(1)} %dynamic-slice_bitcast_fusion.2), channel_id=1, source_target_pairs={{0,4},{1,5},{2,6},{3,7},{4,0},{5,1},{6,2},{7,3},{8,12},{9,13},{10,... | collective-permute-start | bytes 393224 | tf_op jit(solution)/shard_map/ppermute | solution.py:266
  188.1 7.7 %collective-permute-start.7 = (f32[128,128]{1,0:T(8,128)S(1)}, f32[128,128]{1,0:T(8,128)S(1)}, u32[]{:S(2)}, u32[]{:S(2)}) collective-permute-start(f32[128,128]{1,0:T(8,128)S(1)} %dynamic-slice_bitcast_fusion.3), channel_id=1, source_target_pairs={{0,8},{1,9},{2,10},{3,11},{4,12},{5,13},{6,14},{7,15},{8,0},{9,1},... | collective-permute-start | bytes 196616 | tf_op jit(solution)/shard_map/ppermute | solution.py:266
  195.8 24.1 %collective-permute-start.8 = (f32[64,128]{1,0:T(8,128)S(1)}, f32[64,128]{1,0:T(8,128)S(1)}, u32[]{:S(2)}, u32[]{:S(2)}) collective-permute-start(f32[64,128]{1,0:T(8,128)S(1)} %dynamic-slice_bitcast_fusion.4), channel_id=1, source_target_pairs={{0,16},{1,17},{2,18},{3,19},{4,20},{5,21},{6,22},{7,23},{8,24},{9,... | collective-permute-start | bytes 98312 | tf_op jit(solution)/shard_map/ppermute | solution.py:266
  219.9 24.1 %collective-permute-start.9 = (f32[64,128]{1,0:T(8,128)S(1)}, f32[64,128]{1,0:T(8,128)S(1)}, u32[]{:S(2)}, u32[]{:S(2)}) collective-permute-start(f32[64,128]{1,0:T(8,128)S(1)} %bitcast_add_fusion.6), channel_id=1, source_target_pairs={{0,16},{1,17},{2,18},{3,19},{4,20},{5,21},{6,22},{7,23},{8,24},{9,... | collective-permute-start | bytes 98312 | tf_op jit(solution)/shard_map/ppermute | solution.py:270
  244.0 8.4 %collective-permute-start.10 = (f32[128,128]{1,0:T(8,128)S(1)}, f32[128,128]{1,0:T(8,128)S(1)}, u32[]{:S(2)}, u32[]{:S(2)}) collective-permute-start(f32[128,128]{1,0:T(8,128)S(1)} %pad_maximum_fusion.8), channel_id=1, source_target_pairs={{0,8},{1,9},{2,10},{3,11},{4,12},{5,13},{6,14},{7,15},{8,0},{9,1},... | collective-permute-start | bytes 196616 | tf_op jit(solution)/shard_map/ppermute | solution.py:270
  252.4 6.9 %collective-permute-start.11 = (f32[256,128]{1,0:T(8,128)S(1)}, f32[256,128]{1,0:T(8,128)S(1)}, u32[]{:S(2)}, u32[]{:S(2)}) collective-permute-start(f32[256,128]{1,0:T(8,128)S(1)} %pad_maximum_fusion.6), channel_id=1, source_target_pairs={{0,4},{1,5},{2,6},{3,7},{4,0},{5,1},{6,2},{7,3},{8,12},{9,13},{10,... | collective-permute-start | bytes 393224 | tf_op jit(solution)/shard_map/ppermute | solution.py:270
  259.4 12.6 %collective-permute-start.12 = (f32[512,128]{1,0:T(8,128)S(1)}, f32[512,128]{1,0:T(8,128)S(1)}, u32[]{:S(2)}, u32[]{:S(2)}) collective-permute-start(f32[512,128]{1,0:T(8,128)S(1)} %pad_maximum_fusion.3), channel_id=1, source_target_pairs={{0,2},{1,3},{2,0},{3,1},{4,6},{5,7},{6,4},{7,5},{8,10},{9,11},{10,... | collective-permute-start | bytes 786440 | tf_op jit(solution)/shard_map/ppermute | solution.py:270
  272.0 11.1 %collective-permute-start.13 = (f32[1024,128]{1,0:T(8,128)S(1)}, f32[1024,128]{1,0:T(8,128)S(1)}, u32[]{:S(2)}, u32[]{:S(2)}) collective-permute-start(f32[1024,128]{1,0:T(8,128)S(1)} %pad_maximum_fusion.1), channel_id=1, source_target_pairs={{0,1},{1,0},{2,3},{3,2},{4,5},{5,4},{6,7},{7,6},{8,9},{9,8},{10,11... | collective-permute-start | bytes 1572872 | tf_op jit(solution)/shard_map/ppermute | solution.py:270

commit v2 on v1

--- a/solution.py
+++ b/solution.py
@@ -11,6 +11,7 @@
 
 
 step_scale = 0.04
+EMPTY_MARK = 1024.0
 
 
 def extended(x, sides, width):
@@ -216,16 +217,20 @@
     slots = jnp.sum((jnp.cumsum(onehot, axis=0) - 1) * onehot, axis=1)
     position = dest * slot_count + slots
     out_width = targets.shape[1]
-    flag_block = jnp.zeros((rows.shape[0], 128), jnp.bfloat16).at[:, 0].set(1.0)
-    payload = jnp.concatenate([rows, targets, flag_block], axis=1)
+    payload = jnp.concatenate([rows, targets], axis=1)
     width = payload.shape[1]
-    buffer = jnp.zeros((span_count * slot_count, width), jnp.bfloat16).at[position].set(payload)
+    empty = jnp.concatenate(
+        [jnp.zeros((1, FEAT), jnp.bfloat16), jnp.full((1, out_width), EMPTY_MARK, jnp.bfloat16)], axis=1
+    )
+    buffer = jnp.broadcast_to(empty, (span_count * slot_count, width)).at[position].set(payload)
     got = lax.all_to_all(
         buffer.reshape(span_count, slot_count, width), "span", split_axis=0, concat_axis=0, tiled=True
     ).reshape(span_count * slot_count, width)
     inputs = got[:, :FEAT]
-    wanted = got[:, FEAT : FEAT + out_width].astype(jnp.float32)
-    flags = got[:, FEAT + out_width].astype(jnp.float32)
+    wanted_raw = got[:, FEAT : FEAT + out_width].astype(jnp.float32)
+    filled = wanted_raw[:, :1] < EMPTY_MARK / 2
+    wanted = jnp.where(filled, wanted_raw, 0.0)
+    flags = filled[:, 0].astype(jnp.float32)
     row_scale = flags / jnp.maximum(jnp.sum(flags), 1.0)
     layer_one = weight_in[0]
     layer_two = weight_two[0]
@@ -257,14 +262,18 @@
     lanes = 128
     flat = jnp.concatenate([g.reshape(-1, lanes) for g in grads], axis=0)
     me = lax.axis_index("wall")
-    for bit in range(bits):
+    split_bits = min(3, bits)
+    for bit in range(split_bits):
         mine = (me >> bit) & 1
         halves = flat.reshape(2, flat.shape[0] // 2, lanes)
         keep = lax.dynamic_index_in_dim(halves, mine, 0, keepdims=False)
         send = lax.dynamic_index_in_dim(halves, 1 - mine, 0, keepdims=False)
         pairs = [(i, i ^ (1 << bit)) for i in range(size)]
         flat = keep + lax.ppermute(send, "wall", pairs)
-    for bit in reversed(range(bits)):
+    for bit in range(split_bits, bits):
+        pairs = [(i, i ^ (1 << bit)) for i in range(size)]
+        flat = flat + lax.ppermute(flat, "wall", pairs)
+    for bit in reversed(range(split_bits)):
         mine = (me >> bit) & 1
         pairs = [(i, i ^ (1 << bit)) for i in range(size)]
         other = lax.ppermute(flat, "wall", pairs)

time: 288 us -> 258 us (0.90)
  the two profiles are of different devices: /device:TPU:30 before, /device:TPU:120 now
where the time goes in v2:
time: 258 us; the launch traced here: 257 us
  waiting for transfers between devices  120 us (47%)
  starting transfers between devices  103 us (40%)
  matrix products  14.5 us (6%)
  local copies, waits for them, and re-layouts  10.8 us (4%)
  other arithmetic  6.36 us (2%)
    ppermute x3, starting transfers between devices, wall_sum(): flat = keep + lax.ppermute(send, 'wall', pairs)  52.3 us
    ppermute x2, waiting for transfers between devices, wall_sum(): flat = flat + lax.ppermute(flat, 'wall', pairs)  42.2 us
    all_to_all x1, waiting for transfers between devices, local(): lax.all_to_all(buffer.reshape(span_count, slot_count, width), 'span', spl...  31 us
    ppermute x3, waiting for transfers between devices, wall_sum(): flat = keep + lax.ppermute(send, 'wall', pairs)  25.2 us
    all_to_all x1, starting transfers between devices, local(): lax.all_to_all(buffer.reshape(span_count, slot_count, width), 'span', spl...  25.1 us
    ppermute x3, waiting for transfers between devices, wall_sum(): other = lax.ppermute(flat, 'wall', pairs)  21.9 us
    dot_general x22, matrix products, at_face(): jnp.tensordot(vector, field, axes=([0], [axis]), precision=lax.Precision....  9.5 us
    ppermute x3, starting transfers between devices, wall_sum(): other = lax.ppermute(flat, 'wall', pairs)  9.28 us
  transfers between devices with their start and end apart: 13, of which 9 were waited for; matrix products, arithmetic and copies ran while one was open for 5% of the time, Pallas kernels for 0%

profile of v2, /device:TPU:120, one launch (start us, length us, event | category | flops | bytes accessed | tf_op | source)
XLA Modules:
  0.0 257.4 jit_solution(14753337915459791275)
XLA Ops:
  0.7 1.3 slice_bitcast_fusion.15
  2.1 2.1 collective-permute-start.1
  4.1 2.4 collective-permute-start
  6.8 3.4 %collective-permute-start.2 = (f32[2,5,5,5,1,1,128]{6,5,4,3,2,1,0:T(1,128)S(1)}, f32[2,5,5,5,1,1,128]{6,5,4,3,2,1,0:T(1,128)S(1)}, u32[]{:S(2)}, u32[]{:S(2)}) collective-permute-start(f32[2,5,5,5,1,1,128]{6,5,4,3,2,1,0:T(1,128)S(1)} %get-tuple-element.43), channel_id=1, source_target_pairs={{0,1},{1,2},{2,3},{3,4},{4,5},{5,6},{6,7},{7,8},{8,9},{9,10},{10,1... | collective-permute-start | bytes 384008 | tf_op jit(solution)/shard_map/ppermute | solution.py:24
  10.2 4.6 %collective-permute-start.3 = (f32[2,5,5,5,1,1,128]{6,5,4,3,2,1,0:T(1,128)S(1)}, f32[2,5,5,5,1,1,128]{6,5,4,3,2,1,0:T(1,128)S(1)}, u32[]{:S(2)}, u32[]{:S(2)}) collective-permute-start(f32[2,5,5,5,1,1,128]{6,5,4,3,2,1,0:T(1,128)S(1)} %get-tuple-element.44), channel_id=1, source_target_pairs={{1,0},{2,1},{3,2},{4,3},{5,4},{6,5},{7,6},{8,7},{9,8},{10,9},{11,1... | collective-permute-start | bytes 384008 | tf_op jit(solution)/shard_map/ppermute | solution.py:25
  14.7 0.3 fusion.48
  19.3 0.3 fusion.50
  23.9 0.3 maximum_bitcast_fusion
  24.2 0.8 fusion.21
  25.1 0.8 fusion.23
  26.1 0.3 pad_maximum_fusion
  26.6 1.2 fusion
  27.8 1.2 fusion.2
  29.3 0.4 fusion.20
  30.3 0.7 gather_fusion
  31.1 0.7 broadcast_in_dim.41
  31.8 2.7 %scatter_custom_fusion = bf16[512,256]{1,0:T(8,128)(2,1)} fusion(bf16[512,256]{1,0:T(8,128)(2,1)} %broadcast_in_dim.41, s32[128]{0:T(128)S(1)} %fusion.101, bf16[128,128]{1,0:T(8,128)(2,1)S(1)} %copy-done.7, bf16[]{:T(256)} %constant.132, bf16[128,128]{1,0:T(8,128)(2,1)S(1)} %select_convert_fusion), kind=kCustom, calls=%fused_computation.137 | custom fusion | flops 131072 | bytes 328192 | tf_op jit(solution)/shard_map/scatter | solution.py:225
  34.5 25.1 %all-to-all-start = ((bf16[32,16,256]{2,1,0:T(8,128)(2,1)}), bf16[32,16,256]{2,1,0:T(8,128)(2,1)S(1)}, u32[]{:S(2)}, u32[]{:S(2)}) async-start(bf16[32,16,256]{2,1,0:T(8,128)(2,1)} %bitcast.135), calls=%async_computation | async-start | bytes 524288 | tf_op jit(solution)/shard_map/all_to_all | solution.py:226
  59.7 31.0 %all-to-all-done = bf16[32,16,256]{2,1,0:T(8,128)(2,1)S(1)} async-done(((bf16[32,16,256]{2,1,0:T(8,128)(2,1)}), bf16[32,16,256]{2,1,0:T(8,128)(2,1)S(1)}, u32[]{:S(2)}, u32[]{:S(2)}) %all-to-all-start) | async-done | bytes 262176 | tf_op jit(solution)/shard_map/all_to_all | solution.py:226
  90.8 0.6 convert_reduce_fusion
  92.6 0.5 copy-done.16
  93.7 0.6 copy-done.3
  95.4 0.3 fusion.9
  96.0 0.3 fusion.10
  96.6 0.5 fusion.12
  97.3 0.4 convolution_dynamic-update-slice_fusion
  97.7 1.9 collective-permute-start.4
  99.6 14.1 %collective-permute-done.4 = f32[1024,128]{1,0:T(8,128)S(1)} collective-permute-done((f32[1024,128]{1,0:T(8,128)S(1)}, f32[1024,128]{1,0:T(8,128)S(1)}, u32[]{:S(2)}, u32[]{:S(2)}) %collective-permute-start.4) | collective-permute-done | bytes 524320 | tf_op jit(solution)/shard_map/ppermute | solution.py:272
  113.8 48.5 %collective-permute-start.5 = (f32[512,128]{1,0:T(8,128)S(1)}, f32[512,128]{1,0:T(8,128)S(1)}, u32[]{:S(2)}, u32[]{:S(2)}) collective-permute-start(f32[512,128]{1,0:T(8,128)S(1)} %dynamic-slice_bitcast_fusion.1), channel_id=1, source_target_pairs={{0,2},{1,3},{2,0},{3,1},{4,6},{5,7},{6,4},{7,5},{8,10},{9,11},{10,... | collective-permute-start | bytes 786440 | tf_op jit(solution)/shard_map/ppermute | solution.py:272
  162.3 6.2 %collective-permute-done.5 = f32[512,128]{1,0:T(8,128)S(1)} collective-permute-done((f32[512,128]{1,0:T(8,128)S(1)}, f32[512,128]{1,0:T(8,128)S(1)}, u32[]{:S(2)}, u32[]{:S(2)}) %collective-permute-start.5) | collective-permute-done | bytes 262176 | tf_op jit(solution)/shard_map/ppermute | solution.py:272
  168.5 1.9 collective-permute-start.6
  170.5 4.9 %collective-permute-done.6 = f32[256,128]{1,0:T(8,128)S(1)} collective-permute-done((f32[256,128]{1,0:T(8,128)S(1)}, f32[256,128]{1,0:T(8,128)S(1)}, u32[]{:S(2)}, u32[]{:S(2)}) %collective-permute-start.6) | collective-permute-done | bytes 131104 | tf_op jit(solution)/shard_map/ppermute | solution.py:272
  175.4 1.9 collective-permute-start.7
  177.3 6.4 %collective-permute-done.7 = f32[256,128]{1,0:T(8,128)S(1)} collective-permute-done((f32[256,128]{1,0:T(8,128)S(1)}, f32[256,128]{1,0:T(8,128)S(1)}, u32[]{:S(2)}, u32[]{:S(2)}) %collective-permute-start.7) | collective-permute-done | bytes 131104 | tf_op jit(solution)/shard_map/ppermute | solution.py:275
  183.8 1.9 collective-permute-start.8
  185.7 35.8 %collective-permute-done.8 = f32[256,128]{1,0:T(8,128)S(1)} collective-permute-done((f32[256,128]{1,0:T(8,128)S(1)}, f32[256,128]{1,0:T(8,128)S(1)}, u32[]{:S(2)}, u32[]{:S(2)}) %collective-permute-start.8) | collective-permute-done | bytes 131104 | tf_op jit(solution)/shard_map/ppermute | solution.py:275
  221.5 2.1 collective-permute-start.9
  223.6 5.1 %collective-permute-done.9 = f32[256,128]{1,0:T(8,128)S(1)} collective-permute-done((f32[256,128]{1,0:T(8,128)S(1)}, f32[256,128]{1,0:T(8,128)S(1)}, u32[]{:S(2)}, u32[]{:S(2)}) %collective-permute-start.9) | collective-permute-done | bytes 131104 | tf_op jit(solution)/shard_map/ppermute | solution.py:279
  228.8 4.8 %collective-permute-start.10 = (f32[512,128]{1,0:T(8,128)S(1)}, f32[512,128]{1,0:T(8,128)S(1)}, u32[]{:S(2)}, u32[]{:S(2)}) collective-permute-start(f32[512,128]{1,0:T(8,128)S(1)} %pad_maximum_fusion.3), channel_id=1, source_target_pairs={{0,2},{1,3},{2,0},{3,1},{4,6},{5,7},{6,4},{7,5},{8,10},{9,11},{10,... | collective-permute-start | bytes 786440 | tf_op jit(solution)/shard_map/ppermute | solution.py:279
  233.6 5.9 %collective-permute-done.10 = f32[512,128]{1,0:T(8,128)S(1)} collective-permute-done((f32[512,128]{1,0:T(8,128)S(1)}, f32[512,128]{1,0:T(8,128)S(1)}, u32[]{:S(2)}, u32[]{:S(2)}) %collective-permute-start.10) | collective-permute-done | bytes 262176 | tf_op jit(solution)/shard_map/ppermute | solution.py:279
  239.6 2.4 collective-permute-start.11
  242.0 0.7 copy.79
  242.7 10.8 %collective-permute-done.11 = f32[1024,128]{1,0:T(8,128)S(1)} collective-permute-done((f32[1024,128]{1,0:T(8,128)S(1)}, f32[1024,128]{1,0:T(8,128)S(1)}, u32[]{:S(2)}, u32[]{:S(2)}) %collective-permute-start.11) | collective-permute-done | bytes 524320 | tf_op jit(solution)/shard_map/ppermute | solution.py:279
  253.6 0.7 slice_bitcast_fusion
  254.4 0.8 broadcast_in_dim_reshape.15
  255.2 0.7 broadcast_in_dim_reshape.12
  255.9 0.8 broadcast_in_dim_reshape.14
  256.6 0.8 broadcast_in_dim_reshape.13
  (137 shorter events, 13.0 us)
Async XLA Ops:
  0.6 92.7 %copy-start = (bf16[1,256,256]{2,1,0:T(8,128)(2,1)S(1)}, bf16[1,256,256]{2,1,0:T(8,128)(2,1)}, u32[]{:S(2)}) copy-start(bf16[1,256,256]{2,1,0:T(8,128)(2,1)} %param.22) | copy-start | bytes 393220
  0.6 14.1 %copy-start.4 = (f32[5,1,1,1,1]{0,1,4,3,2:T(1,128)S(1)}, f32[5,1,1,1,1]{0,1,4,3,2:T(1,128)}, u32[]{:S(2)}) copy-start(f32[5,1,1,1,1]{0,1,4,3,2:T(1,128)} %constant.118) | copy-start | bytes 64
  0.7 1.3 copy-start.1
  1.9 13.8 %copy-start.5 = (f32[5,1,1,1,1]{0,1,4,3,2:T(1,128)S(1)}, f32[5,1,1,1,1]{0,1,4,3,2:T(1,128)}, u32[]{:S(2)}) copy-start(f32[5,1,1,1,1]{0,1,4,3,2:T(1,128)} %constant.117) | copy-start | bytes 64
  2.1 14.6 %copy-start.2 = (f32[3,5,5,5,1,2,128]{6,5,4,3,2,1,0:T(2,128)S(1)}, f32[3,5,5,5,1,2,128]{6,5,4,3,2,1,0:T(2,128)}, u32[]{:S(2)}) copy-start(f32[3,5,5,5,1,2,128]{6,5,4,3,2,1,0:T(2,128)} %param.16) | copy-start | bytes 1152004
  2.1 24.0 %collective-permute-start.1 = (f32[2,5,5,5,1,2,128]{6,5,4,3,2,1,0:T(2,128)S(1)}, f32[2,5,5,5,1,2,128]{6,5,4,3,2,1,0:T(2,128)S(1)}, u32[]{:S(2)}, u32[]{:S(2)}) collective-permute-start(f32[2,5,5,5,1,2,128]{6,5,4,3,2,1,0:T(2,128)S(1)} %pad_maximum_fusion.4), channel_id=1, source_target_pairs={{32,0},{64,32},{96,64},{128,96},{160,128},{192,160},{224,192},{256... | collective-permute-start | bytes 768008 | tf_op jit(solution)/shard_map/ppermute | solution.py:25
  4.1 22.0 %collective-permute-start = (f32[2,5,5,5,1,2,128]{6,5,4,3,2,1,0:T(2,128)S(1)}, f32[2,5,5,5,1,2,128]{6,5,4,3,2,1,0:T(2,128)S(1)}, u32[]{:S(2)}, u32[]{:S(2)}) collective-permute-start(f32[2,5,5,5,1,2,128]{6,5,4,3,2,1,0:T(2,128)S(1)} %pad_maximum_fusion.4), channel_id=1, source_target_pairs={{0,32},{32,64},{64,96},{96,128},{128,160},{160,192},{192,224},{224... | collective-permute-start | bytes 768008 | tf_op jit(solution)/shard_map/ppermute | solution.py:24
  6.8 17.1 %collective-permute-start.2 = (f32[2,5,5,5,1,1,128]{6,5,4,3,2,1,0:T(1,128)S(1)}, f32[2,5,5,5,1,1,128]{6,5,4,3,2,1,0:T(1,128)S(1)}, u32[]{:S(2)}, u32[]{:S(2)}) collective-permute-start(f32[2,5,5,5,1,1,128]{6,5,4,3,2,1,0:T(1,128)S(1)} %get-tuple-element.43), channel_id=1, source_target_pairs={{0,1},{1,2},{2,3},{3,4},{4,5},{5,6},{6,7},{7,8},{8,9},{9,10},{10,1... | collective-permute-start | bytes 384008 | tf_op jit(solution)/shard_map/ppermute | solution.py:24
  10.2 13.7 %collective-permute-start.3 = (f32[2,5,5,5,1,1,128]{6,5,4,3,2,1,0:T(1,128)S(1)}, f32[2,5,5,5,1,1,128]{6,5,4,3,2,1,0:T(1,128)S(1)}, u32[]{:S(2)}, u32[]{:S(2)}) collective-permute-start(f32[2,5,5,5,1,1,128]{6,5,4,3,2,1,0:T(1,128)S(1)} %get-tuple-element.44), channel_id=1, source_target_pairs={{1,0},{2,1},{3,2},{4,3},{5,4},{6,5},{7,6},{8,7},{9,8},{10,9},{11,1... | collective-permute-start | bytes 384008 | tf_op jit(solution)/shard_map/ppermute | solution.py:25
  16.6 2.0 copy-start.6
  19.0 2.4 copy-start.19
  19.3 2.9 %copy-start.10 = (s32[128,1]{0,1:T(1,128)S(1)}, s32[128,1]{0,1:T(1,128)}, u32[]{:S(2)}) copy-start(s32[128,1]{0,1:T(1,128)} %param.18) | copy-start | bytes 1540
  22.3 1.9 copy-start.15
  23.8 1.3 copy-start.14
  25.9 0.7 copy-start.12
  26.6 1.2 copy-start.11
  27.8 1.4 copy-start.8
  27.8 1.4 copy-start.9
  29.3 1.8 copy-start.13
  29.7 2.1 copy-start.7
  30.3 61.8 %copy-start.17 = (bf16[1,128,256]{2,1,0:T(8,128)(2,1)S(1)}, bf16[1,128,256]{2,1,0:T(8,128)(2,1)}, u32[]{:S(2)}) copy-start(bf16[1,128,256]{2,1,0:T(8,128)(2,1)} %param.20) | copy-start | bytes 196612
  34.5 56.1 %all-to-all-start = ((bf16[32,16,256]{2,1,0:T(8,128)(2,1)}), bf16[32,16,256]{2,1,0:T(8,128)(2,1)S(1)}, u32[]{:S(2)}, u32[]{:S(2)}) async-start(bf16[32,16,256]{2,1,0:T(8,128)(2,1)} %bitcast.135), calls=%async_computation | async-start | bytes 524288 | tf_op jit(solution)/shard_map/all_to_all | solution.py:226
  92.1 0.9 copy-start.16
  93.4 0.9 copy-start.3
  93.4 1.1 copy-start.18
  97.7 16.0 %collective-permute-start.4 = (f32[1024,128]{1,0:T(8,128)S(1)}, f32[1024,128]{1,0:T(8,128)S(1)}, u32[]{:S(2)}, u32[]{:S(2)}) collective-permute-start(f32[1024,128]{1,0:T(8,128)S(1)} %dynamic-slice_bitcast_fusion), channel_id=1, source_target_pairs={{0,1},{1,0},{2,3},{3,2},{4,5},{5,4},{6,7},{7,6},{8,9},{9,8},{10,11... | collective-permute-start | bytes 1572872 | tf_op jit(solution)/shard_map/ppermute | solution.py:272
  113.8 54.7 %collective-permute-start.5 = (f32[512,128]{1,0:T(8,128)S(1)}, f32[512,128]{1,0:T(8,128)S(1)}, u32[]{:S(2)}, u32[]{:S(2)}) collective-permute-start(f32[512,128]{1,0:T(8,128)S(1)} %dynamic-slice_bitcast_fusion.1), channel_id=1, source_target_pairs={{0,2},{1,3},{2,0},{3,1},{4,6},{5,7},{6,4},{7,5},{8,10},{9,11},{10,... | collective-permute-start | bytes 786440 | tf_op jit(solution)/shard_map/ppermute | solution.py:272
  168.5 6.9 %collective-permute-start.6 = (f32[256,128]{1,0:T(8,128)S(1)}, f32[256,128]{1,0:T(8,128)S(1)}, u32[]{:S(2)}, u32[]{:S(2)}) collective-permute-start(f32[256,128]{1,0:T(8,128)S(1)} %dynamic-slice_bitcast_fusion.2), channel_id=1, source_target_pairs={{0,4},{1,5},{2,6},{3,7},{4,0},{5,1},{6,2},{7,3},{8,12},{9,13},{10,... | collective-permute-start | bytes 393224 | tf_op jit(solution)/shard_map/ppermute | solution.py:272
  175.4 8.4 %collective-permute-start.7 = (f32[256,128]{1,0:T(8,128)S(1)}, f32[256,128]{1,0:T(8,128)S(1)}, u32[]{:S(2)}, u32[]{:S(2)}) collective-permute-start(f32[256,128]{1,0:T(8,128)S(1)} %bitcast_add_fusion.4), channel_id=1, source_target_pairs={{0,8},{1,9},{2,10},{3,11},{4,12},{5,13},{6,14},{7,15},{8,0},{9,1},... | collective-permute-start | bytes 393224 | tf_op jit(solution)/shard_map/ppermute | solution.py:275
  183.8 37.7 %collective-permute-start.8 = (f32[256,128]{1,0:T(8,128)S(1)}, f32[256,128]{1,0:T(8,128)S(1)}, u32[]{:S(2)}, u32[]{:S(2)}) collective-permute-start(f32[256,128]{1,0:T(8,128)S(1)} %add.207), channel_id=1, source_target_pairs={{0,16},{1,17},{2,18},{3,19},{4,20},{5,21},{6,22},{7,23},{8,24},{9,... | collective-permute-start | bytes 393224 | tf_op jit(solution)/shard_map/ppermute | solution.py:275
  221.5 7.3 %collective-permute-start.9 = (f32[256,128]{1,0:T(8,128)S(1)}, f32[256,128]{1,0:T(8,128)S(1)}, u32[]{:S(2)}, u32[]{:S(2)}) collective-permute-start(f32[256,128]{1,0:T(8,128)S(1)} %add.208), channel_id=1, source_target_pairs={{0,4},{1,5},{2,6},{3,7},{4,0},{5,1},{6,2},{7,3},{8,12},{9,13},{10,... | collective-permute-start | bytes 393224 | tf_op jit(solution)/shard_map/ppermute | solution.py:279
  228.8 10.7 %collective-permute-start.10 = (f32[512,128]{1,0:T(8,128)S(1)}, f32[512,128]{1,0:T(8,128)S(1)}, u32[]{:S(2)}, u32[]{:S(2)}) collective-permute-start(f32[512,128]{1,0:T(8,128)S(1)} %pad_maximum_fusion.3), channel_id=1, source_target_pairs={{0,2},{1,3},{2,0},{3,1},{4,6},{5,7},{6,4},{7,5},{8,10},{9,11},{10,... | collective-permute-start | bytes 786440 | tf_op jit(solution)/shard_map/ppermute | solution.py:279
  239.6 14.0 %collective-permute-start.11 = (f32[1024,128]{1,0:T(8,128)S(1)}, f32[1024,128]{1,0:T(8,128)S(1)}, u32[]{:S(2)}, u32[]{:S(2)}) collective-permute-start(f32[1024,128]{1,0:T(8,128)S(1)} %pad_maximum_fusion.1), channel_id=1, source_target_pairs={{0,1},{1,0},{2,3},{3,2},{4,5},{5,4},{6,7},{7,6},{8,9},{9,8},{10,11... | collective-permute-start | bytes 1572872 | tf_op jit(solution)/shard_map/ppermute | solution.py:279

commit v3 on v2

--- a/solution.py
+++ b/solution.py
@@ -256,30 +256,37 @@
 
 def wall_sum(grads):
     size = lax.axis_size("wall")
-    bits = size.bit_length() - 1
-    if (1 << bits) != size:
+    groups = wall_groups(size)
+    if groups is None:
         return lax.psum(grads, "wall")
     lanes = 128
     flat = jnp.concatenate([g.reshape(-1, lanes) for g in grads], axis=0)
     me = lax.axis_index("wall")
-    split_bits = min(3, bits)
-    for bit in range(split_bits):
-        mine = (me >> bit) & 1
-        halves = flat.reshape(2, flat.shape[0] // 2, lanes)
-        keep = lax.dynamic_index_in_dim(halves, mine, 0, keepdims=False)
-        send = lax.dynamic_index_in_dim(halves, 1 - mine, 0, keepdims=False)
-        pairs = [(i, i ^ (1 << bit)) for i in range(size)]
-        flat = keep + lax.ppermute(send, "wall", pairs)
-    for bit in range(split_bits, bits):
-        pairs = [(i, i ^ (1 << bit)) for i in range(size)]
-        flat = flat + lax.ppermute(flat, "wall", pairs)
-    for bit in reversed(range(split_bits)):
-        mine = (me >> bit) & 1
-        pairs = [(i, i ^ (1 << bit)) for i in range(size)]
-        other = lax.ppermute(flat, "wall", pairs)
-        low = jnp.where(mine == 0, flat, other)
-        high = jnp.where(mine == 0, other, flat)
-        flat = jnp.concatenate([low, high], axis=0)
+    scatter_groups = [(off, count) for off, count in groups if count > 2]
+    exchange_groups = [(off, count) for off, count in groups if count <= 2]
+    for off, count in scatter_groups:
+        coord = (me >> off) & (count - 1)
+        parts = flat.reshape(count, flat.shape[0] // count, lanes)
+        total = lax.dynamic_index_in_dim(parts, coord, 0, keepdims=False)
+        for shift in range(1, count):
+            send = lax.dynamic_index_in_dim(parts, (coord + shift) % count, 0, keepdims=False)
+            total = total + lax.ppermute(send, "wall", group_pairs(size, off, count, shift))
+        flat = total
+    for off, count in exchange_groups:
+        flat = flat + lax.ppermute(flat, "wall", group_pairs(size, off, count, 1))
+    for off, count in reversed(scatter_groups):
+        coord = (me >> off) & (count - 1)
+        got = [flat] + [
+            lax.ppermute(flat, "wall", group_pairs(size, off, count, shift)) for shift in range(1, count)
+        ]
+        stacked = jnp.stack(got)
+        flat = jnp.concatenate(
+            [
+                lax.dynamic_index_in_dim(stacked, (coord - part) % count, 0, keepdims=False)
+                for part in range(count)
+            ],
+            axis=0,
+        )
     out = []
     at = 0
     for g in grads:
@@ -289,6 +296,21 @@
     return tuple(out)
 
 
+def wall_groups(size):
+    if size != 32:
+        return None
+    return [(0, 4), (2, 4), (4, 2)]
+
+
+def group_pairs(size, off, count, shift):
+    pairs = []
+    for i in range(size):
+        coord = (i >> off) & (count - 1)
+        dest = i - (coord << off) + (((coord + shift) % count) << off)
+        pairs.append((i, dest))
+    return pairs
+
+
 def solution(mesh):
     in_specs = (
         P(None, None, None, "span", "wall", None),

time: 258 us -> 240 us (0.930)
  the two profiles are of different devices: /device:TPU:120 before, /device:TPU:32 now
where the time goes in v3:
time: 240 us; the launch traced here: 239 us
  starting transfers between devices  113 us (47%)
  waiting for transfers between devices  91.2 us (38%)
  matrix products  14.5 us (6%)
  local copies, waits for them, and re-layouts  10.9 us (5%)
  other arithmetic  6.24 us (3%)
  between operations  2.7 us (1%)
    ppermute x6, starting transfers between devices, wall_sum(): lax.ppermute(send, 'wall', group_pairs(size, off, count, shift))  57.1 us
    all_to_all x1, waiting for transfers between devices, local(): lax.all_to_all(buffer.reshape(span_count, slot_count, width), 'span', spl...  42.3 us
    ppermute x1, waiting for transfers between devices, wall_sum(): flat = flat + lax.ppermute(flat, 'wall', group_pairs(size, off, count, 1))  27.9 us
    all_to_all x1, starting transfers between devices, local(): lax.all_to_all(buffer.reshape(span_count, slot_count, width), 'span', spl...  26.1 us
    ppermute x6, starting transfers between devices, wall_sum(): lax.ppermute(flat, 'wall', group_pairs(size, off, count, shift))  18.9 us
    ppermute x6, waiting for transfers between devices, wall_sum(): lax.ppermute(send, 'wall', group_pairs(size, off, count, shift))  12.2 us
    dot_general x22, matrix products, at_face(): jnp.tensordot(vector, field, axes=([0], [axis]), precision=lax.Precision....  9.48 us
    ppermute x6, waiting for transfers between devices, wall_sum(): lax.ppermute(flat, 'wall', group_pairs(size, off, count, shift))  8.75 us
  transfers between devices with their start and end apart: 18, of which 9 were waited for; matrix products, arithmetic and copies ran while one was open for 5% of the time, Pallas kernels for 0%

profile of v3, /device:TPU:32, one launch (start us, length us, event | category | flops | bytes accessed | tf_op | source)
XLA Modules:
  0.0 238.8 jit_solution(1624334658991943714)
XLA Ops:
  0.7 1.3 slice_bitcast_fusion.14
  2.1 2.1 collective-permute-start.1
  4.1 2.4 %collective-permute-start = (f32[2,5,5,5,1,2,128]{6,5,4,3,2,1,0:T(2,128)S(1)}, f32[2,5,5,5,1,2,128]{6,5,4,3,2,1,0:T(2,128)S(1)}, u32[]{:S(2)}, u32[]{:S(2)}) collective-permute-start(f32[2,5,5,5,1,2,128]{6,5,4,3,2,1,0:T(2,128)S(1)} %pad_maximum_fusion.7), channel_id=1, source_target_pairs={{0,32},{32,64},{64,96},{96,128},{128,160},{160,192},{192,224},{224... | collective-permute-start | bytes 768008 | tf_op jit(solution)/shard_map/ppermute | solution.py:24
  6.8 3.4 %collective-permute-start.2 = (f32[2,5,5,5,1,1,128]{6,5,4,3,2,1,0:T(1,128)S(1)}, f32[2,5,5,5,1,1,128]{6,5,4,3,2,1,0:T(1,128)S(1)}, u32[]{:S(2)}, u32[]{:S(2)}) collective-permute-start(f32[2,5,5,5,1,1,128]{6,5,4,3,2,1,0:T(1,128)S(1)} %get-tuple-element.55), channel_id=1, source_target_pairs={{0,1},{1,2},{2,3},{3,4},{4,5},{5,6},{6,7},{7,8},{8,9},{9,10},{10,1... | collective-permute-start | bytes 384008 | tf_op jit(solution)/shard_map/ppermute | solution.py:24
  10.2 1.3 collective-permute-start.3
  20.6 0.3 maximum_bitcast_fusion
  21.0 0.8 fusion.21
  21.8 0.8 fusion.23
  23.3 1.2 fusion
  24.6 1.2 fusion.2
  26.0 0.4 fusion.20
  27.0 0.7 gather_fusion
  27.8 0.7 broadcast_in_dim.26
  28.6 2.7 %scatter_custom_fusion = bf16[512,256]{1,0:T(8,128)(2,1)} fusion(bf16[512,256]{1,0:T(8,128)(2,1)} %broadcast_in_dim.26, s32[128]{0:T(128)S(1)} %fusion.105, bf16[128,128]{1,0:T(8,128)(2,1)S(1)} %copy-done.7, bf16[]{:T(256)} %constant.222, bf16[128,128]{1,0:T(8,128)(2,1)S(1)} %select_convert_fusion), kind=kCustom, calls=%fused_computation.139 | custom fusion | flops 131072 | bytes 328192 | tf_op jit(solution)/shard_map/scatter | solution.py:225
  31.2 26.1 %all-to-all-start = ((bf16[32,16,256]{2,1,0:T(8,128)(2,1)}), bf16[32,16,256]{2,1,0:T(8,128)(2,1)S(1)}, u32[]{:S(2)}, u32[]{:S(2)}) async-start(bf16[32,16,256]{2,1,0:T(8,128)(2,1)} %bitcast.135), calls=%async_computation | async-start | bytes 524288 | tf_op jit(solution)/shard_map/all_to_all | solution.py:226
  57.3 42.3 %all-to-all-done = bf16[32,16,256]{2,1,0:T(8,128)(2,1)S(1)} async-done(((bf16[32,16,256]{2,1,0:T(8,128)(2,1)}), bf16[32,16,256]{2,1,0:T(8,128)(2,1)S(1)}, u32[]{:S(2)}, u32[]{:S(2)}) %all-to-all-start) | async-done | bytes 262176 | tf_op jit(solution)/shard_map/all_to_all | solution.py:226
  99.8 0.6 convert_reduce_fusion
  101.6 0.4 copy-done.16
  102.7 0.6 copy-done.3
  105.6 0.5 fusion.12
  106.3 0.4 convolution_dynamic-update-slice_fusion
  106.7 1.9 collective-permute-start.4
  108.6 5.1 %collective-permute-start.6 = (f32[512,128]{1,0:T(8,128)S(1)}, f32[512,128]{1,0:T(8,128)S(1)}, u32[]{:S(2)}, u32[]{:S(2)}) collective-permute-start(f32[512,128]{1,0:T(8,128)S(1)} %get-tuple-element.33), channel_id=1, source_target_pairs={{0,3},{1,0},{2,1},{3,2},{4,7},{5,4},{6,5},{7,6},{8,11},{9,8},{10,9... | collective-permute-start | bytes 786440 | tf_op jit(solution)/shard_map/ppermute | solution.py:273
  113.8 1.9 collective-permute-start.5
  115.7 1.1 collective-permute-done.4
  116.9 6.8 %collective-permute-done.6 = f32[512,128]{1,0:T(8,128)S(1)} collective-permute-done((f32[512,128]{1,0:T(8,128)S(1)}, f32[512,128]{1,0:T(8,128)S(1)}, u32[]{:S(2)}, u32[]{:S(2)}) %collective-permute-start.6) | collective-permute-done | bytes 262176 | tf_op jit(solution)/shard_map/ppermute | solution.py:273
  123.8 1.9 collective-permute-start.7
  125.7 42.8 %collective-permute-start.9 = (f32[128,128]{1,0:T(8,128)S(1)}, f32[128,128]{1,0:T(8,128)S(1)}, u32[]{:S(2)}, u32[]{:S(2)}) collective-permute-start(f32[128,128]{1,0:T(8,128)S(1)} %get-tuple-element.53), channel_id=1, source_target_pairs={{0,12},{1,13},{2,14},{3,15},{4,0},{5,1},{6,2},{7,3},{8,4},{9,5},{1... | collective-permute-start | bytes 196616 | tf_op jit(solution)/shard_map/ppermute | solution.py:273
  168.5 3.4 %collective-permute-start.8 = (f32[128,128]{1,0:T(8,128)S(1)}, f32[128,128]{1,0:T(8,128)S(1)}, u32[]{:S(2)}, u32[]{:S(2)}) collective-permute-start(f32[128,128]{1,0:T(8,128)S(1)} %get-tuple-element.54), channel_id=1, source_target_pairs={{0,8},{1,9},{2,10},{3,11},{4,12},{5,13},{6,14},{7,15},{8,0},{9,1},... | collective-permute-start | bytes 196616 | tf_op jit(solution)/shard_map/ppermute | solution.py:273
  171.9 4.3 %collective-permute-done.8 = f32[128,128]{1,0:T(8,128)S(1)} collective-permute-done((f32[128,128]{1,0:T(8,128)S(1)}, f32[128,128]{1,0:T(8,128)S(1)}, u32[]{:S(2)}, u32[]{:S(2)}) %collective-permute-start.8) | collective-permute-done | bytes 65568 | tf_op jit(solution)/shard_map/ppermute | solution.py:273
  176.2 2.1 collective-permute-start.10
  178.3 27.9 %collective-permute-done.10 = f32[128,128]{1,0:T(8,128)S(1)} collective-permute-done((f32[128,128]{1,0:T(8,128)S(1)}, f32[128,128]{1,0:T(8,128)S(1)}, u32[]{:S(2)}, u32[]{:S(2)}) %collective-permute-start.10) | collective-permute-done | bytes 65568 | tf_op jit(solution)/shard_map/ppermute | solution.py:276
  206.2 2.2 collective-permute-start.13
  208.4 3.6 %collective-permute-start.12 = (f32[128,128]{1,0:T(8,128)S(1)}, f32[128,128]{1,0:T(8,128)S(1)}, u32[]{:S(2)}, u32[]{:S(2)}) collective-permute-start(f32[128,128]{1,0:T(8,128)S(1)} %add.323), channel_id=1, source_target_pairs={{0,8},{1,9},{2,10},{3,11},{4,12},{5,13},{6,14},{7,15},{8,0},{9,1},... | collective-permute-start | bytes 196616 | tf_op jit(solution)/shard_map/ppermute | solution.py:280
  212.0 3.3 %collective-permute-start.11 = (f32[128,128]{1,0:T(8,128)S(1)}, f32[128,128]{1,0:T(8,128)S(1)}, u32[]{:S(2)}, u32[]{:S(2)}) collective-permute-start(f32[128,128]{1,0:T(8,128)S(1)} %add.323), channel_id=1, source_target_pairs={{0,4},{1,5},{2,6},{3,7},{4,8},{5,9},{6,10},{7,11},{8,12},{9,13},{1... | collective-permute-start | bytes 196616 | tf_op jit(solution)/shard_map/ppermute | solution.py:280
  215.5 0.6 collective-permute-done.12
  216.1 3.3 %collective-permute-done.11 = f32[128,128]{1,0:T(8,128)S(1)} collective-permute-done((f32[128,128]{1,0:T(8,128)S(1)}, f32[128,128]{1,0:T(8,128)S(1)}, u32[]{:S(2)}, u32[]{:S(2)}) %collective-permute-start.11) | collective-permute-done | bytes 65568 | tf_op jit(solution)/shard_map/ppermute | solution.py:280
  219.5 1.9 collective-permute-start.15
  221.4 5.2 %collective-permute-start.14 = (f32[512,128]{1,0:T(8,128)S(1)}, f32[512,128]{1,0:T(8,128)S(1)}, u32[]{:S(2)}, u32[]{:S(2)}) collective-permute-start(f32[512,128]{1,0:T(8,128)S(1)} %get-tuple-element.47), channel_id=1, source_target_pairs={{0,1},{1,2},{2,3},{3,0},{4,5},{5,6},{6,7},{7,4},{8,9},{9,10},{10,1... | collective-permute-start | bytes 786440 | tf_op jit(solution)/shard_map/ppermute | solution.py:280
  226.6 2.7 %collective-permute-start.16 = (f32[512,128]{1,0:T(8,128)S(1)}, f32[512,128]{1,0:T(8,128)S(1)}, u32[]{:S(2)}, u32[]{:S(2)}) collective-permute-start(f32[512,128]{1,0:T(8,128)S(1)} %get-tuple-element.47), channel_id=1, source_target_pairs={{0,3},{1,0},{2,1},{3,2},{4,7},{5,4},{6,5},{7,6},{8,11},{9,8},{10,9... | collective-permute-start | bytes 786440 | tf_op jit(solution)/shard_map/ppermute | solution.py:280
  229.4 0.7 copy.79
  230.1 2.0 collective-permute-done.14
  232.1 2.8 %collective-permute-done.16 = f32[512,128]{1,0:T(8,128)S(1)} collective-permute-done((f32[512,128]{1,0:T(8,128)S(1)}, f32[512,128]{1,0:T(8,128)S(1)}, u32[]{:S(2)}, u32[]{:S(2)}) %collective-permute-start.16) | collective-permute-done | bytes 262176 | tf_op jit(solution)/shard_map/ppermute | solution.py:280
  235.0 0.7 constant_dynamic-slice_fusion.1
  235.8 0.8 broadcast_in_dim_reshape.15
  236.5 0.7 broadcast_in_dim_reshape.12
  237.2 0.8 broadcast_in_dim_reshape.14
  238.0 0.8 broadcast_in_dim_reshape.13
  (143 shorter events, 14.6 us)
Async XLA Ops:
  0.6 101.7 %copy-start = (bf16[1,256,256]{2,1,0:T(8,128)(2,1)S(1)}, bf16[1,256,256]{2,1,0:T(8,128)(2,1)}, u32[]{:S(2)}) copy-start(bf16[1,256,256]{2,1,0:T(8,128)(2,1)} %param.22) | copy-start | bytes 393220
  0.6 10.8 %copy-start.4 = (f32[5,1,1,1,1]{0,1,4,3,2:T(1,128)S(1)}, f32[5,1,1,1,1]{0,1,4,3,2:T(1,128)}, u32[]{:S(2)}) copy-start(f32[5,1,1,1,1]{0,1,4,3,2:T(1,128)} %constant.205) | copy-start | bytes 64
  0.7 1.3 copy-start.1
  1.9 10.5 %copy-start.5 = (f32[5,1,1,1,1]{0,1,4,3,2:T(1,128)S(1)}, f32[5,1,1,1,1]{0,1,4,3,2:T(1,128)}, u32[]{:S(2)}) copy-start(f32[5,1,1,1,1]{0,1,4,3,2:T(1,128)} %constant.204) | copy-start | bytes 64
  2.1 11.3 %copy-start.2 = (f32[3,5,5,5,1,2,128]{6,5,4,3,2,1,0:T(2,128)S(1)}, f32[3,5,5,5,1,2,128]{6,5,4,3,2,1,0:T(2,128)}, u32[]{:S(2)}) copy-start(f32[3,5,5,5,1,2,128]{6,5,4,3,2,1,0:T(2,128)} %param.16) | copy-start | bytes 1152004
  2.1 20.7 %collective-permute-start.1 = (f32[2,5,5,5,1,2,128]{6,5,4,3,2,1,0:T(2,128)S(1)}, f32[2,5,5,5,1,2,128]{6,5,4,3,2,1,0:T(2,128)S(1)}, u32[]{:S(2)}, u32[]{:S(2)}) collective-permute-start(f32[2,5,5,5,1,2,128]{6,5,4,3,2,1,0:T(2,128)S(1)} %pad_maximum_fusion.7), channel_id=1, source_target_pairs={{32,0},{64,32},{96,64},{128,96},{160,128},{192,160},{224,192},{256... | collective-permute-start | bytes 768008 | tf_op jit(solution)/shard_map/ppermute | solution.py:25
  4.1 18.7 %collective-permute-start = (f32[2,5,5,5,1,2,128]{6,5,4,3,2,1,0:T(2,128)S(1)}, f32[2,5,5,5,1,2,128]{6,5,4,3,2,1,0:T(2,128)S(1)}, u32[]{:S(2)}, u32[]{:S(2)}) collective-permute-start(f32[2,5,5,5,1,2,128]{6,5,4,3,2,1,0:T(2,128)S(1)} %pad_maximum_fusion.7), channel_id=1, source_target_pairs={{0,32},{32,64},{64,96},{96,128},{128,160},{160,192},{192,224},{224... | collective-permute-start | bytes 768008 | tf_op jit(solution)/shard_map/ppermute | solution.py:24
  6.8 13.8 %collective-permute-start.2 = (f32[2,5,5,5,1,1,128]{6,5,4,3,2,1,0:T(1,128)S(1)}, f32[2,5,5,5,1,1,128]{6,5,4,3,2,1,0:T(1,128)S(1)}, u32[]{:S(2)}, u32[]{:S(2)}) collective-permute-start(f32[2,5,5,5,1,1,128]{6,5,4,3,2,1,0:T(1,128)S(1)} %get-tuple-element.55), channel_id=1, source_target_pairs={{0,1},{1,2},{2,3},{3,4},{4,5},{5,6},{6,7},{7,8},{8,9},{9,10},{10,1... | collective-permute-start | bytes 384008 | tf_op jit(solution)/shard_map/ppermute | solution.py:24
  10.2 10.4 %collective-permute-start.3 = (f32[2,5,5,5,1,1,128]{6,5,4,3,2,1,0:T(1,128)S(1)}, f32[2,5,5,5,1,1,128]{6,5,4,3,2,1,0:T(1,128)S(1)}, u32[]{:S(2)}, u32[]{:S(2)}) collective-permute-start(f32[2,5,5,5,1,1,128]{6,5,4,3,2,1,0:T(1,128)S(1)} %get-tuple-element.56), channel_id=1, source_target_pairs={{1,0},{2,1},{3,2},{4,3},{5,4},{6,5},{7,6},{8,7},{9,8},{10,9},{11,1... | collective-permute-start | bytes 384008 | tf_op jit(solution)/shard_map/ppermute | solution.py:25
  13.4 2.0 copy-start.6
  15.7 2.4 %copy-start.19 = (s32[128]{0:T(128)S(1)}, s32[128]{0:T(128)}, u32[]{:S(2)}) copy-start(s32[128]{0:T(128)} %param.17) | copy-start | bytes 1540
  16.1 2.9 %copy-start.10 = (s32[128,1]{0,1:T(1,128)S(1)}, s32[128,1]{0,1:T(1,128)}, u32[]{:S(2)}) copy-start(s32[128,1]{0,1:T(1,128)} %param.18) | copy-start | bytes 1540
  19.0 1.9 copy-start.15
  20.5 1.3 copy-start.14
  22.7 0.7 copy-start.12
  23.3 1.2 copy-start.11
  24.5 1.4 copy-start.8
  24.5 1.4 copy-start.9
  26.0 1.8 copy-start.13
  26.4 2.1 copy-start.7
  27.7 73.4 %copy-start.17 = (bf16[1,128,256]{2,1,0:T(8,128)(2,1)S(1)}, bf16[1,128,256]{2,1,0:T(8,128)(2,1)}, u32[]{:S(2)}) copy-start(bf16[1,128,256]{2,1,0:T(8,128)(2,1)} %param.20) | copy-start | bytes 196612
  31.2 68.4 %all-to-all-start = ((bf16[32,16,256]{2,1,0:T(8,128)(2,1)}), bf16[32,16,256]{2,1,0:T(8,128)(2,1)S(1)}, u32[]{:S(2)}, u32[]{:S(2)}) async-start(bf16[32,16,256]{2,1,0:T(8,128)(2,1)} %bitcast.135), calls=%async_computation | async-start | bytes 524288 | tf_op jit(solution)/shard_map/all_to_all | solution.py:226
  101.1 0.9 copy-start.16
  102.4 0.9 copy-start.3
  102.4 1.1 copy-start.18
  106.7 10.2 %collective-permute-start.4 = (f32[512,128]{1,0:T(8,128)S(1)}, f32[512,128]{1,0:T(8,128)S(1)}, u32[]{:S(2)}, u32[]{:S(2)}) collective-permute-start(f32[512,128]{1,0:T(8,128)S(1)} %get-tuple-element.32), channel_id=1, source_target_pairs={{0,1},{1,2},{2,3},{3,0},{4,5},{5,6},{6,7},{7,4},{8,9},{9,10},{10,1... | collective-permute-start | bytes 786440 | tf_op jit(solution)/shard_map/ppermute | solution.py:273
  108.6 15.0 %collective-permute-start.6 = (f32[512,128]{1,0:T(8,128)S(1)}, f32[512,128]{1,0:T(8,128)S(1)}, u32[]{:S(2)}, u32[]{:S(2)}) collective-permute-start(f32[512,128]{1,0:T(8,128)S(1)} %get-tuple-element.33), channel_id=1, source_target_pairs={{0,3},{1,0},{2,1},{3,2},{4,7},{5,4},{6,5},{7,6},{8,11},{9,8},{10,9... | collective-permute-start | bytes 786440 | tf_op jit(solution)/shard_map/ppermute | solution.py:273
  113.8 9.9 %collective-permute-start.5 = (f32[512,128]{1,0:T(8,128)S(1)}, f32[512,128]{1,0:T(8,128)S(1)}, u32[]{:S(2)}, u32[]{:S(2)}) collective-permute-start(f32[512,128]{1,0:T(8,128)S(1)} %get-tuple-element.34), channel_id=1, source_target_pairs={{0,2},{1,3},{2,0},{3,1},{4,6},{5,7},{6,4},{7,5},{8,10},{9,11},{10,... | collective-permute-start | bytes 786440 | tf_op jit(solution)/shard_map/ppermute | solution.py:273
  123.8 48.1 %collective-permute-start.7 = (f32[128,128]{1,0:T(8,128)S(1)}, f32[128,128]{1,0:T(8,128)S(1)}, u32[]{:S(2)}, u32[]{:S(2)}) collective-permute-start(f32[128,128]{1,0:T(8,128)S(1)} %get-tuple-element.52), channel_id=1, source_target_pairs={{0,4},{1,5},{2,6},{3,7},{4,8},{5,9},{6,10},{7,11},{8,12},{9,13},{1... | collective-permute-start | bytes 196616 | tf_op jit(solution)/shard_map/ppermute | solution.py:273
  125.7 46.2 %collective-permute-start.9 = (f32[128,128]{1,0:T(8,128)S(1)}, f32[128,128]{1,0:T(8,128)S(1)}, u32[]{:S(2)}, u32[]{:S(2)}) collective-permute-start(f32[128,128]{1,0:T(8,128)S(1)} %get-tuple-element.53), channel_id=1, source_target_pairs={{0,12},{1,13},{2,14},{3,15},{4,0},{5,1},{6,2},{7,3},{8,4},{9,5},{1... | collective-permute-start | bytes 196616 | tf_op jit(solution)/shard_map/ppermute | solution.py:273
  168.5 7.7 %collective-permute-start.8 = (f32[128,128]{1,0:T(8,128)S(1)}, f32[128,128]{1,0:T(8,128)S(1)}, u32[]{:S(2)}, u32[]{:S(2)}) collective-permute-start(f32[128,128]{1,0:T(8,128)S(1)} %get-tuple-element.54), channel_id=1, source_target_pairs={{0,8},{1,9},{2,10},{3,11},{4,12},{5,13},{6,14},{7,15},{8,0},{9,1},... | collective-permute-start | bytes 196616 | tf_op jit(solution)/shard_map/ppermute | solution.py:273
  176.2 30.1 %collective-permute-start.10 = (f32[128,128]{1,0:T(8,128)S(1)}, f32[128,128]{1,0:T(8,128)S(1)}, u32[]{:S(2)}, u32[]{:S(2)}) collective-permute-start(f32[128,128]{1,0:T(8,128)S(1)} %fusion.96), channel_id=1, source_target_pairs={{0,16},{1,17},{2,18},{3,19},{4,20},{5,21},{6,22},{7,23},{8,24},{9,... | collective-permute-start | bytes 196616 | tf_op jit(solution)/shard_map/ppermute | solution.py:276
  206.2 9.2 %collective-permute-start.13 = (f32[128,128]{1,0:T(8,128)S(1)}, f32[128,128]{1,0:T(8,128)S(1)}, u32[]{:S(2)}, u32[]{:S(2)}) collective-permute-start(f32[128,128]{1,0:T(8,128)S(1)} %add.323), channel_id=1, source_target_pairs={{0,12},{1,13},{2,14},{3,15},{4,0},{5,1},{6,2},{7,3},{8,4},{9,5},{1... | collective-permute-start | bytes 196616 | tf_op jit(solution)/shard_map/ppermute | solution.py:280
  208.4 7.7 %collective-permute-start.12 = (f32[128,128]{1,0:T(8,128)S(1)}, f32[128,128]{1,0:T(8,128)S(1)}, u32[]{:S(2)}, u32[]{:S(2)}) collective-permute-start(f32[128,128]{1,0:T(8,128)S(1)} %add.323), channel_id=1, source_target_pairs={{0,8},{1,9},{2,10},{3,11},{4,12},{5,13},{6,14},{7,15},{8,0},{9,1},... | collective-permute-start | bytes 196616 | tf_op jit(solution)/shard_map/ppermute | solution.py:280
  212.0 7.4 %collective-permute-start.11 = (f32[128,128]{1,0:T(8,128)S(1)}, f32[128,128]{1,0:T(8,128)S(1)}, u32[]{:S(2)}, u32[]{:S(2)}) collective-permute-start(f32[128,128]{1,0:T(8,128)S(1)} %add.323), channel_id=1, source_target_pairs={{0,4},{1,5},{2,6},{3,7},{4,8},{5,9},{6,10},{7,11},{8,12},{9,13},{1... | collective-permute-start | bytes 196616 | tf_op jit(solution)/shard_map/ppermute | solution.py:280
  219.5 10.6 %collective-permute-start.15 = (f32[512,128]{1,0:T(8,128)S(1)}, f32[512,128]{1,0:T(8,128)S(1)}, u32[]{:S(2)}, u32[]{:S(2)}) collective-permute-start(f32[512,128]{1,0:T(8,128)S(1)} %get-tuple-element.47), channel_id=1, source_target_pairs={{0,2},{1,3},{2,0},{3,1},{4,6},{5,7},{6,4},{7,5},{8,10},{9,11},{10,... | collective-permute-start | bytes 786440 | tf_op jit(solution)/shard_map/ppermute | solution.py:280
  221.4 10.7 %collective-permute-start.14 = (f32[512,128]{1,0:T(8,128)S(1)}, f32[512,128]{1,0:T(8,128)S(1)}, u32[]{:S(2)}, u32[]{:S(2)}) collective-permute-start(f32[512,128]{1,0:T(8,128)S(1)} %get-tuple-element.47), channel_id=1, source_target_pairs={{0,1},{1,2},{2,3},{3,0},{4,5},{5,6},{6,7},{7,4},{8,9},{9,10},{10,1... | collective-permute-start | bytes 786440 | tf_op jit(solution)/shard_map/ppermute | solution.py:280
  226.6 8.3 %collective-permute-start.16 = (f32[512,128]{1,0:T(8,128)S(1)}, f32[512,128]{1,0:T(8,128)S(1)}, u32[]{:S(2)}, u32[]{:S(2)}) collective-permute-start(f32[512,128]{1,0:T(8,128)S(1)} %get-tuple-element.47), channel_id=1, source_target_pairs={{0,3},{1,0},{2,1},{3,2},{4,7},{5,4},{6,5},{7,6},{8,11},{9,8},{10,9... | collective-permute-start | bytes 786440 | tf_op jit(solution)/shard_map/ppermute | solution.py:280

commit v4 on v3

--- a/solution.py
+++ b/solution.py
@@ -217,17 +217,17 @@
     slots = jnp.sum((jnp.cumsum(onehot, axis=0) - 1) * onehot, axis=1)
     position = dest * slot_count + slots
     out_width = targets.shape[1]
-    payload = jnp.concatenate([rows, targets], axis=1)
-    width = payload.shape[1]
-    empty = jnp.concatenate(
-        [jnp.zeros((1, FEAT), jnp.bfloat16), jnp.full((1, out_width), EMPTY_MARK, jnp.bfloat16)], axis=1
-    )
-    buffer = jnp.broadcast_to(empty, (span_count * slot_count, width)).at[position].set(payload)
-    got = lax.all_to_all(
-        buffer.reshape(span_count, slot_count, width), "span", split_axis=0, concat_axis=0, tiled=True
-    ).reshape(span_count * slot_count, width)
-    inputs = got[:, :FEAT]
-    wanted_raw = got[:, FEAT : FEAT + out_width].astype(jnp.float32)
+    target_buffer = (
+        jnp.full((span_count * slot_count, out_width), EMPTY_MARK, jnp.bfloat16).at[position].set(targets)
+    )
+    got_targets = lax.all_to_all(
+        target_buffer.reshape(span_count, slot_count, out_width), "span", split_axis=0, concat_axis=0, tiled=True
+    ).reshape(span_count * slot_count, out_width)
+    row_buffer = jnp.zeros((span_count * slot_count, FEAT), jnp.bfloat16).at[position].set(rows)
+    inputs = lax.all_to_all(
+        row_buffer.reshape(span_count, slot_count, FEAT), "span", split_axis=0, concat_axis=0, tiled=True
+    ).reshape(span_count * slot_count, FEAT)
+    wanted_raw = got_targets.astype(jnp.float32)
     filled = wanted_raw[:, :1] < EMPTY_MARK / 2
     wanted = jnp.where(filled, wanted_raw, 0.0)
     flags = filled[:, 0].astype(jnp.float32)

time: 240 us -> 247 us (1.029)
  starting transfers between devices: 113 us -> 138 us
  waiting for transfers between devices: 91.2 us -> 70.4 us
  matrix products: 14.5 us -> 18.7 us
    all_to_all x1 -> x2, waiting for transfers between devices: 42.3 us -> 22.3 us  [the longest x1 22.3 us: local(): lax.all_to_all(row_buffer.reshape(span_count, slot_count, FEAT), 'span',...]
    all_to_all x1 -> x2, starting transfers between devices: 26.1 us -> 45.9 us  [the longest x1 26.2 us: local(): lax.all_to_all(target_buffer.reshape(span_count, slot_count, out_width),...]
    dot_general x22, matrix products: 9.48 us -> 13.7 us  [at_face(): jnp.tensordot(vector, field, axes=([0], [axis]), precision=lax.Precision....]
    ppermute x6, starting transfers between devices: 57.1 us -> 61 us  [wall_sum(): lax.ppermute(send, 'wall', group_pairs(size, off, count, shift))]
  transfers between devices with their start and end apart: 18 -> 19, of which waited for: 9 -> 9; matrix products, arithmetic and copies ran while one was open for 5% -> 10% of each run, Pallas kernels for 0% -> 0%
where the time goes in v4:
time: 247 us; the launch traced here: 246 us
  starting transfers between devices  138 us (56%)
  waiting for transfers between devices  70.4 us (29%)
  matrix products  18.7 us (8%)
  local copies, waits for them, and re-layouts  11.1 us (4%)
  other arithmetic  5.46 us (2%)
  between operations  2.73 us (1%)
    ppermute x6, starting transfers between devices, wall_sum(): lax.ppermute(send, 'wall', group_pairs(size, off, count, shift))  61 us
    ppermute x1, waiting for transfers between devices, wall_sum(): flat = flat + lax.ppermute(flat, 'wall', group_pairs(size, off, count, 1))  27.6 us
    all_to_all x1, starting transfers between devices, local(): lax.all_to_all(target_buffer.reshape(span_count, slot_count, out_width),...  26.2 us
    all_to_all x1, waiting for transfers between devices, local(): lax.all_to_all(row_buffer.reshape(span_count, slot_count, FEAT), 'span',...  22.3 us
    ppermute x6, starting transfers between devices, wall_sum(): lax.ppermute(flat, 'wall', group_pairs(size, off, count, shift))  20 us
    all_to_all x1, starting transfers between devices, local(): lax.all_to_all(row_buffer.reshape(span_count, slot_count, FEAT), 'span',...  19.8 us
    dot_general x22, matrix products, at_face(): jnp.tensordot(vector, field, axes=([0], [axis]), precision=lax.Precision....  13.7 us
    ppermute x6, waiting for transfers between devices, wall_sum(): lax.ppermute(send, 'wall', group_pairs(size, off, count, shift))  11.5 us
  transfers between devices with their start and end apart: 19, of which 9 were waited for; matrix products, arithmetic and copies ran while one was open for 10% of the time, Pallas kernels for 0%

profile of v4, /device:TPU:32, one launch (start us, length us, event | category | flops | bytes accessed | tf_op | source)
XLA Modules:
  0.0 246.4 jit_solution(1292554832932235297)
XLA Ops:
  0.7 1.2 slice_bitcast_fusion.14
  2.1 1.9 collective-permute-start.1
  4.0 2.4 collective-permute-start
  6.9 1.7 scatter_custom_fusion.1
  8.6 26.2 %all-to-all-start.1 = ((bf16[32,16,128]{2,1,0:T(8,128)(2,1)}), bf16[32,16,128]{2,1,0:T(8,128)(2,1)S(1)}, u32[]{:S(2)}, u32[]{:S(2)}) async-start(bf16[32,16,128]{2,1,0:T(8,128)(2,1)} %bitcast.137), calls=%async_computation.1 | async-start | bytes 262144 | tf_op jit(solution)/shard_map/all_to_all | solution.py:223
  35.0 3.4 %collective-permute-start.2 = (f32[2,5,5,5,1,1,128]{6,5,4,3,2,1,0:T(1,128)S(1)}, f32[2,5,5,5,1,1,128]{6,5,4,3,2,1,0:T(1,128)S(1)}, u32[]{:S(2)}, u32[]{:S(2)}) collective-permute-start(f32[2,5,5,5,1,1,128]{6,5,4,3,2,1,0:T(1,128)S(1)} %get-tuple-element.55), channel_id=1, source_target_pairs={{0,1},{1,2},{2,3},{3,4},{4,5},{5,6},{6,7},{7,8},{8,9},{9,10},{10,1... | collective-permute-start | bytes 384008 | tf_op jit(solution)/shard_map/ppermute | solution.py:24
  38.4 1.3 collective-permute-start.3
  40.4 0.9 fusion.56
  41.6 0.9 fusion.58
  43.0 0.9 fusion.39
  43.9 0.9 fusion.37
  44.8 0.9 fusion.33
  45.7 0.9 fusion.31
  48.9 0.9 fusion.70
  53.0 0.8 fusion.21
  53.9 0.8 fusion.23
  55.4 1.2 fusion.2
  56.7 1.2 fusion
  59.0 1.8 scatter_custom_fusion
  60.8 19.8 %all-to-all-start = ((bf16[32,16,128]{2,1,0:T(8,128)(2,1)}), bf16[32,16,128]{2,1,0:T(8,128)(2,1)S(1)}, u32[]{:S(2)}, u32[]{:S(2)}) async-start(bf16[32,16,128]{2,1,0:T(8,128)(2,1)} %bitcast.135), calls=%async_computation | async-start | bytes 262144 | tf_op jit(solution)/shard_map/all_to_all | solution.py:227
  80.8 0.6 convert_reduce_fusion
  82.3 22.3 %all-to-all-done = bf16[32,16,128]{2,1,0:T(8,128)(2,1)S(1)} async-done(((bf16[32,16,128]{2,1,0:T(8,128)(2,1)}), bf16[32,16,128]{2,1,0:T(8,128)(2,1)S(1)}, u32[]{:S(2)}, u32[]{:S(2)}) %all-to-all-start) | async-done | bytes 131104 | tf_op jit(solution)/shard_map/all_to_all | solution.py:227
  110.1 3.8 %collective-permute-start.4 = (f32[512,128]{1,0:T(8,128)S(1)}, f32[512,128]{1,0:T(8,128)S(1)}, u32[]{:S(2)}, u32[]{:S(2)}) collective-permute-start(f32[512,128]{1,0:T(8,128)S(1)} %get-tuple-element.32), channel_id=1, source_target_pairs={{0,1},{1,2},{2,3},{3,0},{4,5},{5,6},{6,7},{7,4},{8,9},{9,10},{10,1... | collective-permute-start | bytes 786440 | tf_op jit(solution)/shard_map/ppermute | solution.py:273
  114.0 3.2 %collective-permute-start.6 = (f32[512,128]{1,0:T(8,128)S(1)}, f32[512,128]{1,0:T(8,128)S(1)}, u32[]{:S(2)}, u32[]{:S(2)}) collective-permute-start(f32[512,128]{1,0:T(8,128)S(1)} %get-tuple-element.33), channel_id=1, source_target_pairs={{0,3},{1,0},{2,1},{3,2},{4,7},{5,4},{6,5},{7,6},{8,11},{9,8},{10,9... | collective-permute-start | bytes 786440 | tf_op jit(solution)/shard_map/ppermute | solution.py:273
  117.2 4.1 %collective-permute-start.5 = (f32[512,128]{1,0:T(8,128)S(1)}, f32[512,128]{1,0:T(8,128)S(1)}, u32[]{:S(2)}, u32[]{:S(2)}) collective-permute-start(f32[512,128]{1,0:T(8,128)S(1)} %get-tuple-element.34), channel_id=1, source_target_pairs={{0,2},{1,3},{2,0},{3,1},{4,6},{5,7},{6,4},{7,5},{8,10},{9,11},{10,... | collective-permute-start | bytes 786440 | tf_op jit(solution)/shard_map/ppermute | solution.py:273
  121.8 6.8 %collective-permute-done.6 = f32[512,128]{1,0:T(8,128)S(1)} collective-permute-done((f32[512,128]{1,0:T(8,128)S(1)}, f32[512,128]{1,0:T(8,128)S(1)}, u32[]{:S(2)}, u32[]{:S(2)}) %collective-permute-start.6) | collective-permute-done | bytes 262176 | tf_op jit(solution)/shard_map/ppermute | solution.py:273
  128.7 4.4 %collective-permute-start.7 = (f32[128,128]{1,0:T(8,128)S(1)}, f32[128,128]{1,0:T(8,128)S(1)}, u32[]{:S(2)}, u32[]{:S(2)}) collective-permute-start(f32[128,128]{1,0:T(8,128)S(1)} %get-tuple-element.52), channel_id=1, source_target_pairs={{0,4},{1,5},{2,6},{3,7},{4,8},{5,9},{6,10},{7,11},{8,12},{9,13},{1... | collective-permute-start | bytes 196616 | tf_op jit(solution)/shard_map/ppermute | solution.py:273
  133.1 42.1 %collective-permute-start.9 = (f32[128,128]{1,0:T(8,128)S(1)}, f32[128,128]{1,0:T(8,128)S(1)}, u32[]{:S(2)}, u32[]{:S(2)}) collective-permute-start(f32[128,128]{1,0:T(8,128)S(1)} %get-tuple-element.53), channel_id=1, source_target_pairs={{0,12},{1,13},{2,14},{3,15},{4,0},{5,1},{6,2},{7,3},{8,4},{9,5},{1... | collective-permute-start | bytes 196616 | tf_op jit(solution)/shard_map/ppermute | solution.py:273
  175.2 3.4 %collective-permute-start.8 = (f32[128,128]{1,0:T(8,128)S(1)}, f32[128,128]{1,0:T(8,128)S(1)}, u32[]{:S(2)}, u32[]{:S(2)}) collective-permute-start(f32[128,128]{1,0:T(8,128)S(1)} %get-tuple-element.54), channel_id=1, source_target_pairs={{0,8},{1,9},{2,10},{3,11},{4,12},{5,13},{6,14},{7,15},{8,0},{9,1},... | collective-permute-start | bytes 196616 | tf_op jit(solution)/shard_map/ppermute | solution.py:273
  178.6 4.3 %collective-permute-done.8 = f32[128,128]{1,0:T(8,128)S(1)} collective-permute-done((f32[128,128]{1,0:T(8,128)S(1)}, f32[128,128]{1,0:T(8,128)S(1)}, u32[]{:S(2)}, u32[]{:S(2)}) %collective-permute-start.8) | collective-permute-done | bytes 65568 | tf_op jit(solution)/shard_map/ppermute | solution.py:273
  182.9 1.9 collective-permute-start.10
  184.8 27.6 %collective-permute-done.10 = f32[128,128]{1,0:T(8,128)S(1)} collective-permute-done((f32[128,128]{1,0:T(8,128)S(1)}, f32[128,128]{1,0:T(8,128)S(1)}, u32[]{:S(2)}, u32[]{:S(2)}) %collective-permute-start.10) | collective-permute-done | bytes 65568 | tf_op jit(solution)/shard_map/ppermute | solution.py:276
  212.4 3.9 %collective-permute-start.13 = (f32[128,128]{1,0:T(8,128)S(1)}, f32[128,128]{1,0:T(8,128)S(1)}, u32[]{:S(2)}, u32[]{:S(2)}) collective-permute-start(f32[128,128]{1,0:T(8,128)S(1)} %add.320), channel_id=1, source_target_pairs={{0,12},{1,13},{2,14},{3,15},{4,0},{5,1},{6,2},{7,3},{8,4},{9,5},{1... | collective-permute-start | bytes 196616 | tf_op jit(solution)/shard_map/ppermute | solution.py:280
  216.3 1.9 collective-permute-start.12
  218.3 2.8 %collective-permute-start.11 = (f32[128,128]{1,0:T(8,128)S(1)}, f32[128,128]{1,0:T(8,128)S(1)}, u32[]{:S(2)}, u32[]{:S(2)}) collective-permute-start(f32[128,128]{1,0:T(8,128)S(1)} %add.320), channel_id=1, source_target_pairs={{0,4},{1,5},{2,6},{3,7},{4,8},{5,9},{6,10},{7,11},{8,12},{9,13},{1... | collective-permute-start | bytes 196616 | tf_op jit(solution)/shard_map/ppermute | solution.py:280
  221.1 2.9 %collective-permute-done.12 = f32[128,128]{1,0:T(8,128)S(1)} collective-permute-done((f32[128,128]{1,0:T(8,128)S(1)}, f32[128,128]{1,0:T(8,128)S(1)}, u32[]{:S(2)}, u32[]{:S(2)}) %collective-permute-start.12) | collective-permute-done | bytes 65568 | tf_op jit(solution)/shard_map/ppermute | solution.py:280
  224.0 1.6 collective-permute-done.11
  225.7 3.3 %collective-permute-start.15 = (f32[512,128]{1,0:T(8,128)S(1)}, f32[512,128]{1,0:T(8,128)S(1)}, u32[]{:S(2)}, u32[]{:S(2)}) collective-permute-start(f32[512,128]{1,0:T(8,128)S(1)} %get-tuple-element.47), channel_id=1, source_target_pairs={{0,2},{1,3},{2,0},{3,1},{4,6},{5,7},{6,4},{7,5},{8,10},{9,11},{10,... | collective-permute-start | bytes 786440 | tf_op jit(solution)/shard_map/ppermute | solution.py:280
  229.1 5.1 %collective-permute-start.14 = (f32[512,128]{1,0:T(8,128)S(1)}, f32[512,128]{1,0:T(8,128)S(1)}, u32[]{:S(2)}, u32[]{:S(2)}) collective-permute-start(f32[512,128]{1,0:T(8,128)S(1)} %get-tuple-element.47), channel_id=1, source_target_pairs={{0,1},{1,2},{2,3},{3,0},{4,5},{5,6},{6,7},{7,4},{8,9},{9,10},{10,1... | collective-permute-start | bytes 786440 | tf_op jit(solution)/shard_map/ppermute | solution.py:280
  234.2 3.0 %collective-permute-start.16 = (f32[512,128]{1,0:T(8,128)S(1)}, f32[512,128]{1,0:T(8,128)S(1)}, u32[]{:S(2)}, u32[]{:S(2)}) collective-permute-start(f32[512,128]{1,0:T(8,128)S(1)} %get-tuple-element.47), channel_id=1, source_target_pairs={{0,3},{1,0},{2,1},{3,2},{4,7},{5,4},{6,5},{7,6},{8,11},{9,8},{10,9... | collective-permute-start | bytes 786440 | tf_op jit(solution)/shard_map/ppermute | solution.py:280
  237.3 0.7 copy.79
  238.0 1.6 collective-permute-done.14
  239.6 2.9 %collective-permute-done.16 = f32[512,128]{1,0:T(8,128)S(1)} collective-permute-done((f32[512,128]{1,0:T(8,128)S(1)}, f32[512,128]{1,0:T(8,128)S(1)}, u32[]{:S(2)}, u32[]{:S(2)}) %collective-permute-start.16) | collective-permute-done | bytes 262176 | tf_op jit(solution)/shard_map/ppermute | solution.py:280
  242.5 0.7 constant_dynamic-slice_fusion.1
  243.3 0.8 broadcast_in_dim_reshape.15
  244.1 0.7 broadcast_in_dim_reshape.12
  244.8 0.8 broadcast_in_dim_reshape.14
  245.6 0.8 broadcast_in_dim_reshape.13
  (153 shorter events, 15.6 us)
Async XLA Ops:
  0.6 105.2 %copy-start = (bf16[1,256,256]{2,1,0:T(8,128)(2,1)S(1)}, bf16[1,256,256]{2,1,0:T(8,128)(2,1)}, u32[]{:S(2)}) copy-start(bf16[1,256,256]{2,1,0:T(8,128)(2,1)} %param.22) | copy-start | bytes 393220
  0.6 1.3 copy-start.1
  0.7 5.8 %copy-start.16 = (s32[128,1]{0,1:T(1,128)S(1)}, s32[128,1]{0,1:T(1,128)}, u32[]{:S(2)}) copy-start(s32[128,1]{0,1:T(1,128)} %param.18) | copy-start | bytes 1540
  1.9 37.8 %copy-start.12 = (f32[5,1,1,1,1]{0,1,4,3,2:T(1,128)S(1)}, f32[5,1,1,1,1]{0,1,4,3,2:T(1,128)}, u32[]{:S(2)}) copy-start(f32[5,1,1,1,1]{0,1,4,3,2:T(1,128)} %constant.206) | copy-start | bytes 64
  2.1 39.2 %copy-start.11 = (f32[5,1,1,1,1]{0,1,4,3,2:T(1,128)S(1)}, f32[5,1,1,1,1]{0,1,4,3,2:T(1,128)}, u32[]{:S(2)}) copy-start(f32[5,1,1,1,1]{0,1,4,3,2:T(1,128)} %constant.205) | copy-start | bytes 64
  2.1 52.8 %collective-permute-start.1 = (f32[2,5,5,5,1,2,128]{6,5,4,3,2,1,0:T(2,128)S(1)}, f32[2,5,5,5,1,2,128]{6,5,4,3,2,1,0:T(2,128)S(1)}, u32[]{:S(2)}, u32[]{:S(2)}) collective-permute-start(f32[2,5,5,5,1,2,128]{6,5,4,3,2,1,0:T(2,128)S(1)} %pad_maximum_fusion.7), channel_id=1, source_target_pairs={{32,0},{64,32},{96,64},{128,96},{160,128},{192,160},{224,192},{256... | collective-permute-start | bytes 768008 | tf_op jit(solution)/shard_map/ppermute | solution.py:25
  4.0 50.9 %collective-permute-start = (f32[2,5,5,5,1,2,128]{6,5,4,3,2,1,0:T(2,128)S(1)}, f32[2,5,5,5,1,2,128]{6,5,4,3,2,1,0:T(2,128)S(1)}, u32[]{:S(2)}, u32[]{:S(2)}) collective-permute-start(f32[2,5,5,5,1,2,128]{6,5,4,3,2,1,0:T(2,128)S(1)} %pad_maximum_fusion.7), channel_id=1, source_target_pairs={{0,32},{32,64},{64,96},{96,128},{128,160},{160,192},{192,224},{224... | collective-permute-start | bytes 768008 | tf_op jit(solution)/shard_map/ppermute | solution.py:24
  8.6 34.2 %copy-start.2 = (f32[3,5,5,5,1,2,128]{6,5,4,3,2,1,0:T(2,128)S(1)}, f32[3,5,5,5,1,2,128]{6,5,4,3,2,1,0:T(2,128)}, u32[]{:S(2)}) copy-start(f32[3,5,5,5,1,2,128]{6,5,4,3,2,1,0:T(2,128)} %param.16) | copy-start | bytes 1152004
  8.6 52.2 %all-to-all-start.1 = ((bf16[32,16,128]{2,1,0:T(8,128)(2,1)}), bf16[32,16,128]{2,1,0:T(8,128)(2,1)S(1)}, u32[]{:S(2)}, u32[]{:S(2)}) async-start(bf16[32,16,128]{2,1,0:T(8,128)(2,1)} %bitcast.137), calls=%async_computation.1 | async-start | bytes 262144 | tf_op jit(solution)/shard_map/all_to_all | solution.py:223
  35.0 17.6 %collective-permute-start.2 = (f32[2,5,5,5,1,1,128]{6,5,4,3,2,1,0:T(1,128)S(1)}, f32[2,5,5,5,1,1,128]{6,5,4,3,2,1,0:T(1,128)S(1)}, u32[]{:S(2)}, u32[]{:S(2)}) collective-permute-start(f32[2,5,5,5,1,1,128]{6,5,4,3,2,1,0:T(1,128)S(1)} %get-tuple-element.55), channel_id=1, source_target_pairs={{0,1},{1,2},{2,3},{3,4},{4,5},{5,6},{6,7},{7,8},{8,9},{9,10},{10,1... | collective-permute-start | bytes 384008 | tf_op jit(solution)/shard_map/ppermute | solution.py:24
  38.4 14.2 %collective-permute-start.3 = (f32[2,5,5,5,1,1,128]{6,5,4,3,2,1,0:T(1,128)S(1)}, f32[2,5,5,5,1,1,128]{6,5,4,3,2,1,0:T(1,128)S(1)}, u32[]{:S(2)}, u32[]{:S(2)}) collective-permute-start(f32[2,5,5,5,1,1,128]{6,5,4,3,2,1,0:T(1,128)S(1)} %get-tuple-element.56), channel_id=1, source_target_pairs={{1,0},{2,1},{3,2},{4,3},{5,4},{6,5},{7,6},{8,7},{9,8},{10,9},{11,1... | collective-permute-start | bytes 384008 | tf_op jit(solution)/shard_map/ppermute | solution.py:25
  42.8 4.5 %copy-start.13 = (f32[5,5,1,1,1]{1,0,4,3,2:T(8,128)S(1)}, f32[5,5,1,1,1]{1,0,4,3,2:T(8,128)}, u32[]{:S(2)}) copy-start(f32[5,5,1,1,1]{1,0,4,3,2:T(8,128)} %constant.203) | copy-start | bytes 304
  47.6 3.0 %copy-start.24 = (s32[128]{0:T(128)S(1)}, s32[128]{0:T(128)}, u32[]{:S(2)}) copy-start(s32[128]{0:T(128)} %param.17) | copy-start | bytes 1540
  48.5 3.6 %copy-start.10 = (f32[1,5,5,2,128]{4,0,3,2,1:T(1,128)S(1)}, f32[1,5,5,2,128]{4,0,3,2,1:T(1,128)}, u32[]{:S(2)}) copy-start(f32[1,5,5,2,128]{4,0,3,2,1:T(1,128)} %fusion.31) | copy-start | bytes 76804
  48.5 3.7 %copy-start.9 = (f32[1,5,5,2,128]{4,0,3,2,1:T(1,128)S(1)}, f32[1,5,5,2,128]{4,0,3,2,1:T(1,128)}, u32[]{:S(2)}) copy-start(f32[1,5,5,2,128]{4,0,3,2,1:T(1,128)} %fusion.33) | copy-start | bytes 76804
  50.8 2.2 copy-start.20
  52.5 1.3 copy-start.19
  53.0 1.7 copy-start.6
  53.0 1.7 copy-start.8
  53.0 1.8 copy-start.5
  53.0 1.8 copy-start.7
  54.7 0.7 copy-start.18
  55.4 1.3 copy-start.17
  56.6 1.4 copy-start.4
  56.6 1.4 copy-start.14
  56.7 1.4 copy-start.15
  58.6 46.0 %copy-start.22 = (bf16[1,128,256]{2,1,0:T(8,128)(2,1)S(1)}, bf16[1,128,256]{2,1,0:T(8,128)(2,1)}, u32[]{:S(2)}) copy-start(bf16[1,128,256]{2,1,0:T(8,128)(2,1)} %param.20) | copy-start | bytes 196612
  60.8 43.8 %all-to-all-start = ((bf16[32,16,128]{2,1,0:T(8,128)(2,1)}), bf16[32,16,128]{2,1,0:T(8,128)(2,1)S(1)}, u32[]{:S(2)}, u32[]{:S(2)}) async-start(bf16[32,16,128]{2,1,0:T(8,128)(2,1)} %bitcast.135), calls=%async_computation | async-start | bytes 262144 | tf_op jit(solution)/shard_map/all_to_all | solution.py:227
  104.6 0.9 copy-start.21
  105.8 0.9 copy-start.3
  105.8 1.1 copy-start.23
  110.1 11.7 %collective-permute-start.4 = (f32[512,128]{1,0:T(8,128)S(1)}, f32[512,128]{1,0:T(8,128)S(1)}, u32[]{:S(2)}, u32[]{:S(2)}) collective-permute-start(f32[512,128]{1,0:T(8,128)S(1)} %get-tuple-element.32), channel_id=1, source_target_pairs={{0,1},{1,2},{2,3},{3,0},{4,5},{5,6},{6,7},{7,4},{8,9},{9,10},{10,1... | collective-permute-start | bytes 786440 | tf_op jit(solution)/shard_map/ppermute | solution.py:273
  114.0 14.7 %collective-permute-start.6 = (f32[512,128]{1,0:T(8,128)S(1)}, f32[512,128]{1,0:T(8,128)S(1)}, u32[]{:S(2)}, u32[]{:S(2)}) collective-permute-start(f32[512,128]{1,0:T(8,128)S(1)} %get-tuple-element.33), channel_id=1, source_target_pairs={{0,3},{1,0},{2,1},{3,2},{4,7},{5,4},{6,5},{7,6},{8,11},{9,8},{10,9... | collective-permute-start | bytes 786440 | tf_op jit(solution)/shard_map/ppermute | solution.py:273
  117.2 11.4 %collective-permute-start.5 = (f32[512,128]{1,0:T(8,128)S(1)}, f32[512,128]{1,0:T(8,128)S(1)}, u32[]{:S(2)}, u32[]{:S(2)}) collective-permute-start(f32[512,128]{1,0:T(8,128)S(1)} %get-tuple-element.34), channel_id=1, source_target_pairs={{0,2},{1,3},{2,0},{3,1},{4,6},{5,7},{6,4},{7,5},{8,10},{9,11},{10,... | collective-permute-start | bytes 786440 | tf_op jit(solution)/shard_map/ppermute | solution.py:273
  128.7 49.9 %collective-permute-start.7 = (f32[128,128]{1,0:T(8,128)S(1)}, f32[128,128]{1,0:T(8,128)S(1)}, u32[]{:S(2)}, u32[]{:S(2)}) collective-permute-start(f32[128,128]{1,0:T(8,128)S(1)} %get-tuple-element.52), channel_id=1, source_target_pairs={{0,4},{1,5},{2,6},{3,7},{4,8},{5,9},{6,10},{7,11},{8,12},{9,13},{1... | collective-permute-start | bytes 196616 | tf_op jit(solution)/shard_map/ppermute | solution.py:273
  133.1 45.5 %collective-permute-start.9 = (f32[128,128]{1,0:T(8,128)S(1)}, f32[128,128]{1,0:T(8,128)S(1)}, u32[]{:S(2)}, u32[]{:S(2)}) collective-permute-start(f32[128,128]{1,0:T(8,128)S(1)} %get-tuple-element.53), channel_id=1, source_target_pairs={{0,12},{1,13},{2,14},{3,15},{4,0},{5,1},{6,2},{7,3},{8,4},{9,5},{1... | collective-permute-start | bytes 196616 | tf_op jit(solution)/shard_map/ppermute | solution.py:273
  175.2 7.7 %collective-permute-start.8 = (f32[128,128]{1,0:T(8,128)S(1)}, f32[128,128]{1,0:T(8,128)S(1)}, u32[]{:S(2)}, u32[]{:S(2)}) collective-permute-start(f32[128,128]{1,0:T(8,128)S(1)} %get-tuple-element.54), channel_id=1, source_target_pairs={{0,8},{1,9},{2,10},{3,11},{4,12},{5,13},{6,14},{7,15},{8,0},{9,1},... | collective-permute-start | bytes 196616 | tf_op jit(solution)/shard_map/ppermute | solution.py:273
  182.9 29.5 %collective-permute-start.10 = (f32[128,128]{1,0:T(8,128)S(1)}, f32[128,128]{1,0:T(8,128)S(1)}, u32[]{:S(2)}, u32[]{:S(2)}) collective-permute-start(f32[128,128]{1,0:T(8,128)S(1)} %fusion.89), channel_id=1, source_target_pairs={{0,16},{1,17},{2,18},{3,19},{4,20},{5,21},{6,22},{7,23},{8,24},{9,... | collective-permute-start | bytes 196616 | tf_op jit(solution)/shard_map/ppermute | solution.py:276
  212.4 8.7 %collective-permute-start.13 = (f32[128,128]{1,0:T(8,128)S(1)}, f32[128,128]{1,0:T(8,128)S(1)}, u32[]{:S(2)}, u32[]{:S(2)}) collective-permute-start(f32[128,128]{1,0:T(8,128)S(1)} %add.320), channel_id=1, source_target_pairs={{0,12},{1,13},{2,14},{3,15},{4,0},{5,1},{6,2},{7,3},{8,4},{9,5},{1... | collective-permute-start | bytes 196616 | tf_op jit(solution)/shard_map/ppermute | solution.py:280
  216.3 7.7 %collective-permute-start.12 = (f32[128,128]{1,0:T(8,128)S(1)}, f32[128,128]{1,0:T(8,128)S(1)}, u32[]{:S(2)}, u32[]{:S(2)}) collective-permute-start(f32[128,128]{1,0:T(8,128)S(1)} %add.320), channel_id=1, source_target_pairs={{0,8},{1,9},{2,10},{3,11},{4,12},{5,13},{6,14},{7,15},{8,0},{9,1},... | collective-permute-start | bytes 196616 | tf_op jit(solution)/shard_map/ppermute | solution.py:280
  218.3 7.4 %collective-permute-start.11 = (f32[128,128]{1,0:T(8,128)S(1)}, f32[128,128]{1,0:T(8,128)S(1)}, u32[]{:S(2)}, u32[]{:S(2)}) collective-permute-start(f32[128,128]{1,0:T(8,128)S(1)} %add.320), channel_id=1, source_target_pairs={{0,4},{1,5},{2,6},{3,7},{4,8},{5,9},{6,10},{7,11},{8,12},{9,13},{1... | collective-permute-start | bytes 196616 | tf_op jit(solution)/shard_map/ppermute | solution.py:280
  225.7 12.2 %collective-permute-start.15 = (f32[512,128]{1,0:T(8,128)S(1)}, f32[512,128]{1,0:T(8,128)S(1)}, u32[]{:S(2)}, u32[]{:S(2)}) collective-permute-start(f32[512,128]{1,0:T(8,128)S(1)} %get-tuple-element.47), channel_id=1, source_target_pairs={{0,2},{1,3},{2,0},{3,1},{4,6},{5,7},{6,4},{7,5},{8,10},{9,11},{10,... | collective-permute-start | bytes 786440 | tf_op jit(solution)/shard_map/ppermute | solution.py:280
  229.1 10.5 %collective-permute-start.14 = (f32[512,128]{1,0:T(8,128)S(1)}, f32[512,128]{1,0:T(8,128)S(1)}, u32[]{:S(2)}, u32[]{:S(2)}) collective-permute-start(f32[512,128]{1,0:T(8,128)S(1)} %get-tuple-element.47), channel_id=1, source_target_pairs={{0,1},{1,2},{2,3},{3,0},{4,5},{5,6},{6,7},{7,4},{8,9},{9,10},{10,1... | collective-permute-start | bytes 786440 | tf_op jit(solution)/shard_map/ppermute | solution.py:280
  234.2 8.3 %collective-permute-start.16 = (f32[512,128]{1,0:T(8,128)S(1)}, f32[512,128]{1,0:T(8,128)S(1)}, u32[]{:S(2)}, u32[]{:S(2)}) collective-permute-start(f32[512,128]{1,0:T(8,128)S(1)} %get-tuple-element.47), channel_id=1, source_target_pairs={{0,3},{1,0},{2,1},{3,2},{4,7},{5,4},{6,5},{7,6},{8,11},{9,8},{10,9... | collective-permute-start | bytes 786440 | tf_op jit(solution)/shard_map/ppermute | solution.py:280

commit v5 on v3

--- a/solution.py
+++ b/solution.py
@@ -169,12 +169,11 @@
     count = field.shape[3 + direction]
     face_axis = 3 + direction
     stacked = jnp.stack([field, speed])
-    if direction == 0:
-        padded = extended(stacked, (("span", 4),), 1)
-    else:
-        padded = extended(stacked, (("wall", 5),), 1)
-    padded_left = at_face(tables[1], padded, 1 + direction)
-    padded_right = at_face(tables[2], padded, 1 + direction)
+    own_left = at_face(tables[1], stacked, 1 + direction)
+    own_right = at_face(tables[2], stacked, 1 + direction)
+    axis = "span" if direction == 0 else "wall"
+    padded_left = extended(own_left, ((axis, face_axis),), 1)
+    padded_right = extended(own_right, ((axis, face_axis),), 1)
     before = lax.slice_in_dim(padded_right, 0, count, axis=face_axis)
     after = lax.slice_in_dim(padded_left, 2, count + 2, axis=face_axis)
     return ((before[0], before[1]), (after[0], after[1]))

time: 240 us -> 216 us (0.900)
  the two profiles are of different devices: /device:TPU:32 before, /device:TPU:2 now
where the time goes in v5:
time: 216 us; the launch traced here: 215 us
  starting transfers between devices  106 us (49%)
  waiting for transfers between devices  73.4 us (34%)
  local copies, waits for them, and re-layouts  15 us (7%)
  matrix products  12.4 us (6%)
  other arithmetic  5.53 us (3%)
  between operations  2.61 us (1%)
    ppermute x6, starting transfers between devices, wall_sum(): lax.ppermute(send, 'wall', group_pairs(size, off, count, shift))  37.5 us
    all_to_all x1, waiting for transfers between devices, local(): lax.all_to_all(buffer.reshape(span_count, slot_count, width), 'span', spl...  32.9 us
    ppermute x1, starting transfers between devices, wall_sum(): flat = flat + lax.ppermute(flat, 'wall', group_pairs(size, off, count, 1))  16 us
    ppermute x6, starting transfers between devices, wall_sum(): lax.ppermute(flat, 'wall', group_pairs(size, off, count, shift))  16 us
    all_to_all x1, starting transfers between devices, local(): lax.all_to_all(buffer.reshape(span_count, slot_count, width), 'span', spl...  15.8 us
    ppermute x6, waiting for transfers between devices, wall_sum(): lax.ppermute(send, 'wall', group_pairs(size, off, count, shift))  14.7 us
    ppermute x2, starting transfers between devices, extended(): after = lax.ppermute(first, axis, down)  14.2 us
    ppermute x1, waiting for transfers between devices, wall_sum(): flat = flat + lax.ppermute(flat, 'wall', group_pairs(size, off, count, 1))  13.8 us
  transfers between devices with their start and end apart: 18, of which 11 were waited for; matrix products, arithmetic and copies ran while one was open for 5% of the time, Pallas kernels for 0%

profile of v5, /device:TPU:2, one launch (start us, length us, event | category | flops | bytes accessed | tf_op | source)
XLA Modules:
  0.0 214.9 jit_solution(18356997037802125116)
XLA Ops:
  0.7 1.2 slice_bitcast_fusion.10
  2.1 0.6 copy-done.11
  3.3 3.4 %collective-permute-start.2 = (f32[2,5,5,1,1,128]{5,0,4,3,2,1:T(2,128)S(1)}, f32[2,5,5,1,1,128]{5,0,4,3,2,1:T(2,128)S(1)}, u32[]{:S(2)}, u32[]{:S(2)}) collective-permute-start(f32[2,5,5,1,1,128]{5,0,4,3,2,1:T(2,128)S(1)} %slice.139), channel_id=1, source_target_pairs={{0,1},{1,2},{2,3},{3,4},{4,5},{5,6},{6,7},{7,8},{8,9},{9,10},{10,1... | collective-permute-start | bytes 76808 | tf_op jit(solution)/shard_map/ppermute | solution.py:24
  6.8 0.5 fusion.20
  7.3 13.0 %collective-permute-start.3 = (f32[2,5,5,1,1,128]{5,0,4,3,2,1:T(2,128)S(1)}, f32[2,5,5,1,1,128]{5,0,4,3,2,1:T(2,128)S(1)}, u32[]{:S(2)}, u32[]{:S(2)}) collective-permute-start(f32[2,5,5,1,1,128]{5,0,4,3,2,1:T(2,128)S(1)} %slice.140), channel_id=1, source_target_pairs={{1,0},{2,1},{3,2},{4,3},{5,4},{6,5},{7,6},{8,7},{9,8},{10,9},{11,1... | collective-permute-start | bytes 76808 | tf_op jit(solution)/shard_map/ppermute | solution.py:25
  20.7 1.3 collective-permute-start.1
  22.5 3.0 %collective-permute-start = (f32[2,5,5,1,2,128]{5,4,3,2,1,0:T(2,128)S(1)}, f32[2,5,5,1,2,128]{5,4,3,2,1,0:T(2,128)S(1)}, u32[]{:S(2)}, u32[]{:S(2)}) collective-permute-start(f32[2,5,5,1,2,128]{5,4,3,2,1,0:T(2,128)S(1)} %bitcast.414), channel_id=1, source_target_pairs={{0,32},{32,64},{64,96},{96,128},{128,160},{160,192},{192,224},{224... | collective-permute-start | bytes 153608 | tf_op jit(solution)/shard_map/ppermute | solution.py:24
  25.6 0.6 copy-done.5
  34.4 0.7 copy-done.10
  37.1 0.6 copy-done.8
  38.5 0.7 gather_fusion
  39.3 0.6 copy-done.13
  39.9 0.7 broadcast_in_dim.26
  40.7 2.7 %scatter_custom_fusion = bf16[512,256]{1,0:T(8,128)(2,1)} fusion(bf16[512,256]{1,0:T(8,128)(2,1)} %broadcast_in_dim.26, s32[128]{0:T(128)S(1)} %fusion.104, bf16[128,128]{1,0:T(8,128)(2,1)S(1)} %copy-done.7, bf16[]{:T(256)} %constant.220, bf16[128,128]{1,0:T(8,128)(2,1)S(1)} %select_convert_fusion), kind=kCustom, calls=%fused_computation.134 | custom fusion | flops 131072 | bytes 328192 | tf_op jit(solution)/shard_map/scatter | solution.py:224
  43.3 15.8 %all-to-all-start = ((bf16[32,16,256]{2,1,0:T(8,128)(2,1)}), bf16[32,16,256]{2,1,0:T(8,128)(2,1)S(1)}, u32[]{:S(2)}, u32[]{:S(2)}) async-start(bf16[32,16,256]{2,1,0:T(8,128)(2,1)} %bitcast.141), calls=%async_computation | async-start | bytes 524288 | tf_op jit(solution)/shard_map/all_to_all | solution.py:225
  59.2 32.9 %all-to-all-done = bf16[32,16,256]{2,1,0:T(8,128)(2,1)S(1)} async-done(((bf16[32,16,256]{2,1,0:T(8,128)(2,1)}), bf16[32,16,256]{2,1,0:T(8,128)(2,1)S(1)}, u32[]{:S(2)}, u32[]{:S(2)}) %all-to-all-start) | async-done | bytes 262176 | tf_op jit(solution)/shard_map/all_to_all | solution.py:225
  92.3 0.6 convert_reduce_fusion
  95.2 0.6 copy-done.3
  96.0 0.6 copy-done.16
  99.7 3.4 %collective-permute-start.4 = (f32[512,128]{1,0:T(8,128)S(1)}, f32[512,128]{1,0:T(8,128)S(1)}, u32[]{:S(2)}, u32[]{:S(2)}) collective-permute-start(f32[512,128]{1,0:T(8,128)S(1)} %get-tuple-element.32), channel_id=1, source_target_pairs={{0,1},{1,2},{2,3},{3,0},{4,5},{5,6},{6,7},{7,4},{8,9},{9,10},{10,1... | collective-permute-start | bytes 786440 | tf_op jit(solution)/shard_map/ppermute | solution.py:272
  103.1 2.4 %collective-permute-start.6 = (f32[512,128]{1,0:T(8,128)S(1)}, f32[512,128]{1,0:T(8,128)S(1)}, u32[]{:S(2)}, u32[]{:S(2)}) collective-permute-start(f32[512,128]{1,0:T(8,128)S(1)} %get-tuple-element.33), channel_id=1, source_target_pairs={{0,3},{1,0},{2,1},{3,2},{4,7},{5,4},{6,5},{7,6},{8,11},{9,8},{10,9... | collective-permute-start | bytes 786440 | tf_op jit(solution)/shard_map/ppermute | solution.py:272
  105.6 4.1 %collective-permute-start.5 = (f32[512,128]{1,0:T(8,128)S(1)}, f32[512,128]{1,0:T(8,128)S(1)}, u32[]{:S(2)}, u32[]{:S(2)}) collective-permute-start(f32[512,128]{1,0:T(8,128)S(1)} %get-tuple-element.34), channel_id=1, source_target_pairs={{0,2},{1,3},{2,0},{3,1},{4,6},{5,7},{6,4},{7,5},{8,10},{9,11},{10,... | collective-permute-start | bytes 786440 | tf_op jit(solution)/shard_map/ppermute | solution.py:272
  109.7 1.0 collective-permute-done.4
  110.8 3.1 %collective-permute-done.6 = f32[512,128]{1,0:T(8,128)S(1)} collective-permute-done((f32[512,128]{1,0:T(8,128)S(1)}, f32[512,128]{1,0:T(8,128)S(1)}, u32[]{:S(2)}, u32[]{:S(2)}) %collective-permute-start.6) | collective-permute-done | bytes 262176 | tf_op jit(solution)/shard_map/ppermute | solution.py:272
  113.9 6.3 %collective-permute-done.5 = f32[512,128]{1,0:T(8,128)S(1)} collective-permute-done((f32[512,128]{1,0:T(8,128)S(1)}, f32[512,128]{1,0:T(8,128)S(1)}, u32[]{:S(2)}, u32[]{:S(2)}) %collective-permute-start.5) | collective-permute-done | bytes 262176 | tf_op jit(solution)/shard_map/ppermute | solution.py:272
  120.2 4.3 %collective-permute-start.7 = (f32[128,128]{1,0:T(8,128)S(1)}, f32[128,128]{1,0:T(8,128)S(1)}, u32[]{:S(2)}, u32[]{:S(2)}) collective-permute-start(f32[128,128]{1,0:T(8,128)S(1)} %get-tuple-element.52), channel_id=1, source_target_pairs={{0,4},{1,5},{2,6},{3,7},{4,8},{5,9},{6,10},{7,11},{8,12},{9,13},{1... | collective-permute-start | bytes 196616 | tf_op jit(solution)/shard_map/ppermute | solution.py:272
  124.6 19.9 %collective-permute-start.9 = (f32[128,128]{1,0:T(8,128)S(1)}, f32[128,128]{1,0:T(8,128)S(1)}, u32[]{:S(2)}, u32[]{:S(2)}) collective-permute-start(f32[128,128]{1,0:T(8,128)S(1)} %get-tuple-element.53), channel_id=1, source_target_pairs={{0,12},{1,13},{2,14},{3,15},{4,0},{5,1},{6,2},{7,3},{8,4},{9,5},{1... | collective-permute-start | bytes 196616 | tf_op jit(solution)/shard_map/ppermute | solution.py:272
  144.5 3.4 %collective-permute-start.8 = (f32[128,128]{1,0:T(8,128)S(1)}, f32[128,128]{1,0:T(8,128)S(1)}, u32[]{:S(2)}, u32[]{:S(2)}) collective-permute-start(f32[128,128]{1,0:T(8,128)S(1)} %get-tuple-element.54), channel_id=1, source_target_pairs={{0,8},{1,9},{2,10},{3,11},{4,12},{5,13},{6,14},{7,15},{8,0},{9,1},... | collective-permute-start | bytes 196616 | tf_op jit(solution)/shard_map/ppermute | solution.py:272
  147.9 4.3 %collective-permute-done.8 = f32[128,128]{1,0:T(8,128)S(1)} collective-permute-done((f32[128,128]{1,0:T(8,128)S(1)}, f32[128,128]{1,0:T(8,128)S(1)}, u32[]{:S(2)}, u32[]{:S(2)}) %collective-permute-start.8) | collective-permute-done | bytes 65568 | tf_op jit(solution)/shard_map/ppermute | solution.py:272
  152.1 16.0 %collective-permute-start.10 = (f32[128,128]{1,0:T(8,128)S(1)}, f32[128,128]{1,0:T(8,128)S(1)}, u32[]{:S(2)}, u32[]{:S(2)}) collective-permute-start(f32[128,128]{1,0:T(8,128)S(1)} %fusion.97), channel_id=1, source_target_pairs={{0,16},{1,17},{2,18},{3,19},{4,20},{5,21},{6,22},{7,23},{8,24},{9,... | collective-permute-start | bytes 196616 | tf_op jit(solution)/shard_map/ppermute | solution.py:275
  168.1 13.8 %collective-permute-done.10 = f32[128,128]{1,0:T(8,128)S(1)} collective-permute-done((f32[128,128]{1,0:T(8,128)S(1)}, f32[128,128]{1,0:T(8,128)S(1)}, u32[]{:S(2)}, u32[]{:S(2)}) %collective-permute-start.10) | collective-permute-done | bytes 65568 | tf_op jit(solution)/shard_map/ppermute | solution.py:275
  181.9 3.5 %collective-permute-start.13 = (f32[128,128]{1,0:T(8,128)S(1)}, f32[128,128]{1,0:T(8,128)S(1)}, u32[]{:S(2)}, u32[]{:S(2)}) collective-permute-start(f32[128,128]{1,0:T(8,128)S(1)} %add.323), channel_id=1, source_target_pairs={{0,12},{1,13},{2,14},{3,15},{4,0},{5,1},{6,2},{7,3},{8,4},{9,5},{1... | collective-permute-start | bytes 196616 | tf_op jit(solution)/shard_map/ppermute | solution.py:279
  185.4 1.9 collective-permute-start.12
  187.4 2.8 %collective-permute-start.11 = (f32[128,128]{1,0:T(8,128)S(1)}, f32[128,128]{1,0:T(8,128)S(1)}, u32[]{:S(2)}, u32[]{:S(2)}) collective-permute-start(f32[128,128]{1,0:T(8,128)S(1)} %add.323), channel_id=1, source_target_pairs={{0,4},{1,5},{2,6},{3,7},{4,8},{5,9},{6,10},{7,11},{8,12},{9,13},{1... | collective-permute-start | bytes 196616 | tf_op jit(solution)/shard_map/ppermute | solution.py:279
  190.2 3.2 %collective-permute-done.12 = f32[128,128]{1,0:T(8,128)S(1)} collective-permute-done((f32[128,128]{1,0:T(8,128)S(1)}, f32[128,128]{1,0:T(8,128)S(1)}, u32[]{:S(2)}, u32[]{:S(2)}) %collective-permute-start.12) | collective-permute-done | bytes 65568 | tf_op jit(solution)/shard_map/ppermute | solution.py:279
  193.4 1.3 collective-permute-done.11
  194.8 1.9 collective-permute-start.15
  196.8 3.1 %collective-permute-start.14 = (f32[512,128]{1,0:T(8,128)S(1)}, f32[512,128]{1,0:T(8,128)S(1)}, u32[]{:S(2)}, u32[]{:S(2)}) collective-permute-start(f32[512,128]{1,0:T(8,128)S(1)} %get-tuple-element.47), channel_id=1, source_target_pairs={{0,1},{1,2},{2,3},{3,0},{4,5},{5,6},{6,7},{7,4},{8,9},{9,10},{10,1... | collective-permute-start | bytes 786440 | tf_op jit(solution)/shard_map/ppermute | solution.py:279
  199.9 2.7 %collective-permute-start.16 = (f32[512,128]{1,0:T(8,128)S(1)}, f32[512,128]{1,0:T(8,128)S(1)}, u32[]{:S(2)}, u32[]{:S(2)}) collective-permute-start(f32[512,128]{1,0:T(8,128)S(1)} %get-tuple-element.47), channel_id=1, source_target_pairs={{0,3},{1,0},{2,1},{3,2},{4,7},{5,4},{6,5},{7,6},{8,11},{9,8},{10,9... | collective-permute-start | bytes 786440 | tf_op jit(solution)/shard_map/ppermute | solution.py:279
  202.7 0.7 copy.86
  203.4 2.2 %collective-permute-done.15 = f32[512,128]{1,0:T(8,128)S(1)} collective-permute-done((f32[512,128]{1,0:T(8,128)S(1)}, f32[512,128]{1,0:T(8,128)S(1)}, u32[]{:S(2)}, u32[]{:S(2)}) %collective-permute-start.15) | collective-permute-done | bytes 262176 | tf_op jit(solution)/shard_map/ppermute | solution.py:279
  205.6 1.9 collective-permute-done.14
  207.6 3.4 %collective-permute-done.16 = f32[512,128]{1,0:T(8,128)S(1)} collective-permute-done((f32[512,128]{1,0:T(8,128)S(1)}, f32[512,128]{1,0:T(8,128)S(1)}, u32[]{:S(2)}, u32[]{:S(2)}) %collective-permute-start.16) | collective-permute-done | bytes 262176 | tf_op jit(solution)/shard_map/ppermute | solution.py:279
  211.0 0.7 constant_dynamic-slice_fusion.1
  211.8 0.8 broadcast_in_dim_reshape.15
  212.6 0.7 broadcast_in_dim_reshape.12
  213.3 0.8 broadcast_in_dim_reshape.14
  214.1 0.8 broadcast_in_dim_reshape.13
  (141 shorter events, 17.8 us)
Async XLA Ops:
  0.6 94.2 %copy-start = (bf16[1,256,256]{2,1,0:T(8,128)(2,1)S(1)}, bf16[1,256,256]{2,1,0:T(8,128)(2,1)}, u32[]{:S(2)}) copy-start(bf16[1,256,256]{2,1,0:T(8,128)(2,1)} %param.22) | copy-start | bytes 393220
  0.6 1.3 copy-start.1
  2.1 0.7 copy-start.11
  3.3 3.4 %copy-start.12 = (f32[5,1,1,1,1,1]{0,1,5,4,3,2:T(1,128)S(1)}, f32[5,1,1,1,1,1]{0,1,5,4,3,2:T(1,128)}, u32[]{:S(2)}) copy-start(f32[5,1,1,1,1,1]{0,1,5,4,3,2:T(1,128)} %constant.206) | copy-start | bytes 64
  3.3 33.4 %collective-permute-start.2 = (f32[2,5,5,1,1,128]{5,0,4,3,2,1:T(2,128)S(1)}, f32[2,5,5,1,1,128]{5,0,4,3,2,1:T(2,128)S(1)}, u32[]{:S(2)}, u32[]{:S(2)}) collective-permute-start(f32[2,5,5,1,1,128]{5,0,4,3,2,1:T(2,128)S(1)} %slice.139), channel_id=1, source_target_pairs={{0,1},{1,2},{2,3},{3,4},{4,5},{5,6},{6,7},{7,8},{8,9},{9,10},{10,1... | collective-permute-start | bytes 76808 | tf_op jit(solution)/shard_map/ppermute | solution.py:24
  7.3 29.5 %collective-permute-start.3 = (f32[2,5,5,1,1,128]{5,0,4,3,2,1:T(2,128)S(1)}, f32[2,5,5,1,1,128]{5,0,4,3,2,1:T(2,128)S(1)}, u32[]{:S(2)}, u32[]{:S(2)}) collective-permute-start(f32[2,5,5,1,1,128]{5,0,4,3,2,1:T(2,128)S(1)} %slice.140), channel_id=1, source_target_pairs={{1,0},{2,1},{3,2},{4,3},{5,4},{6,5},{7,6},{8,7},{9,8},{10,9},{11,1... | collective-permute-start | bytes 76808 | tf_op jit(solution)/shard_map/ppermute | solution.py:25
  20.7 16.2 %collective-permute-start.1 = (f32[2,5,5,1,2,128]{5,4,3,2,1,0:T(2,128)S(1)}, f32[2,5,5,1,2,128]{5,4,3,2,1,0:T(2,128)S(1)}, u32[]{:S(2)}, u32[]{:S(2)}) collective-permute-start(f32[2,5,5,1,2,128]{5,4,3,2,1,0:T(2,128)S(1)} %bitcast.415), channel_id=1, source_target_pairs={{32,0},{64,32},{96,64},{128,96},{160,128},{192,160},{224,192},{256... | collective-permute-start | bytes 153608 | tf_op jit(solution)/shard_map/ppermute | solution.py:25
  22.5 3.1 %copy-start.17 = (s32[128]{0:T(128)S(1)}, s32[128]{0:T(128)}, u32[]{:S(2)}) copy-start(s32[128]{0:T(128)} %param.17) | copy-start | bytes 1540
  22.5 14.5 %collective-permute-start = (f32[2,5,5,1,2,128]{5,4,3,2,1,0:T(2,128)S(1)}, f32[2,5,5,1,2,128]{5,4,3,2,1,0:T(2,128)S(1)}, u32[]{:S(2)}, u32[]{:S(2)}) collective-permute-start(f32[2,5,5,1,2,128]{5,4,3,2,1,0:T(2,128)S(1)} %bitcast.414), channel_id=1, source_target_pairs={{0,32},{32,64},{64,96},{96,128},{128,160},{160,192},{192,224},{224... | collective-permute-start | bytes 153608 | tf_op jit(solution)/shard_map/ppermute | solution.py:24
  25.6 0.7 copy-start.5
  26.9 0.7 copy-start.4
  27.6 1.0 copy-start.2
  30.3 0.7 copy-start.6
  34.4 0.7 copy-start.10
  37.0 0.7 copy-start.8
  37.1 0.7 copy-start.9
  39.2 0.7 copy-start.13
  39.9 0.8 copy-start.7
  43.3 48.8 %all-to-all-start = ((bf16[32,16,256]{2,1,0:T(8,128)(2,1)}), bf16[32,16,256]{2,1,0:T(8,128)(2,1)S(1)}, u32[]{:S(2)}, u32[]{:S(2)}) async-start(bf16[32,16,256]{2,1,0:T(8,128)(2,1)} %bitcast.141), calls=%async_computation | async-start | bytes 524288 | tf_op jit(solution)/shard_map/all_to_all | solution.py:225
  92.1 1.5 copy-start.15
  93.6 0.9 copy-start.14
  94.8 0.9 copy-start.3
  95.7 0.8 copy-start.16
  99.7 11.0 %collective-permute-start.4 = (f32[512,128]{1,0:T(8,128)S(1)}, f32[512,128]{1,0:T(8,128)S(1)}, u32[]{:S(2)}, u32[]{:S(2)}) collective-permute-start(f32[512,128]{1,0:T(8,128)S(1)} %get-tuple-element.32), channel_id=1, source_target_pairs={{0,1},{1,2},{2,3},{3,0},{4,5},{5,6},{6,7},{7,4},{8,9},{9,10},{10,1... | collective-permute-start | bytes 786440 | tf_op jit(solution)/shard_map/ppermute | solution.py:272
  103.1 10.7 %collective-permute-start.6 = (f32[512,128]{1,0:T(8,128)S(1)}, f32[512,128]{1,0:T(8,128)S(1)}, u32[]{:S(2)}, u32[]{:S(2)}) collective-permute-start(f32[512,128]{1,0:T(8,128)S(1)} %get-tuple-element.33), channel_id=1, source_target_pairs={{0,3},{1,0},{2,1},{3,2},{4,7},{5,4},{6,5},{7,6},{8,11},{9,8},{10,9... | collective-permute-start | bytes 786440 | tf_op jit(solution)/shard_map/ppermute | solution.py:272
  105.6 14.6 %collective-permute-start.5 = (f32[512,128]{1,0:T(8,128)S(1)}, f32[512,128]{1,0:T(8,128)S(1)}, u32[]{:S(2)}, u32[]{:S(2)}) collective-permute-start(f32[512,128]{1,0:T(8,128)S(1)} %get-tuple-element.34), channel_id=1, source_target_pairs={{0,2},{1,3},{2,0},{3,1},{4,6},{5,7},{6,4},{7,5},{8,10},{9,11},{10,... | collective-permute-start | bytes 786440 | tf_op jit(solution)/shard_map/ppermute | solution.py:272
  120.2 27.6 %collective-permute-start.7 = (f32[128,128]{1,0:T(8,128)S(1)}, f32[128,128]{1,0:T(8,128)S(1)}, u32[]{:S(2)}, u32[]{:S(2)}) collective-permute-start(f32[128,128]{1,0:T(8,128)S(1)} %get-tuple-element.52), channel_id=1, source_target_pairs={{0,4},{1,5},{2,6},{3,7},{4,8},{5,9},{6,10},{7,11},{8,12},{9,13},{1... | collective-permute-start | bytes 196616 | tf_op jit(solution)/shard_map/ppermute | solution.py:272
  124.6 23.3 %collective-permute-start.9 = (f32[128,128]{1,0:T(8,128)S(1)}, f32[128,128]{1,0:T(8,128)S(1)}, u32[]{:S(2)}, u32[]{:S(2)}) collective-permute-start(f32[128,128]{1,0:T(8,128)S(1)} %get-tuple-element.53), channel_id=1, source_target_pairs={{0,12},{1,13},{2,14},{3,15},{4,0},{5,1},{6,2},{7,3},{8,4},{9,5},{1... | collective-permute-start | bytes 196616 | tf_op jit(solution)/shard_map/ppermute | solution.py:272
  144.5 7.7 %collective-permute-start.8 = (f32[128,128]{1,0:T(8,128)S(1)}, f32[128,128]{1,0:T(8,128)S(1)}, u32[]{:S(2)}, u32[]{:S(2)}) collective-permute-start(f32[128,128]{1,0:T(8,128)S(1)} %get-tuple-element.54), channel_id=1, source_target_pairs={{0,8},{1,9},{2,10},{3,11},{4,12},{5,13},{6,14},{7,15},{8,0},{9,1},... | collective-permute-start | bytes 196616 | tf_op jit(solution)/shard_map/ppermute | solution.py:272
  152.1 29.8 %collective-permute-start.10 = (f32[128,128]{1,0:T(8,128)S(1)}, f32[128,128]{1,0:T(8,128)S(1)}, u32[]{:S(2)}, u32[]{:S(2)}) collective-permute-start(f32[128,128]{1,0:T(8,128)S(1)} %fusion.97), channel_id=1, source_target_pairs={{0,16},{1,17},{2,18},{3,19},{4,20},{5,21},{6,22},{7,23},{8,24},{9,... | collective-permute-start | bytes 196616 | tf_op jit(solution)/shard_map/ppermute | solution.py:275
  181.9 8.3 %collective-permute-start.13 = (f32[128,128]{1,0:T(8,128)S(1)}, f32[128,128]{1,0:T(8,128)S(1)}, u32[]{:S(2)}, u32[]{:S(2)}) collective-permute-start(f32[128,128]{1,0:T(8,128)S(1)} %add.323), channel_id=1, source_target_pairs={{0,12},{1,13},{2,14},{3,15},{4,0},{5,1},{6,2},{7,3},{8,4},{9,5},{1... | collective-permute-start | bytes 196616 | tf_op jit(solution)/shard_map/ppermute | solution.py:279
  185.4 8.0 %collective-permute-start.12 = (f32[128,128]{1,0:T(8,128)S(1)}, f32[128,128]{1,0:T(8,128)S(1)}, u32[]{:S(2)}, u32[]{:S(2)}) collective-permute-start(f32[128,128]{1,0:T(8,128)S(1)} %add.323), channel_id=1, source_target_pairs={{0,8},{1,9},{2,10},{3,11},{4,12},{5,13},{6,14},{7,15},{8,0},{9,1},... | collective-permute-start | bytes 196616 | tf_op jit(solution)/shard_map/ppermute | solution.py:279
  187.4 7.4 %collective-permute-start.11 = (f32[128,128]{1,0:T(8,128)S(1)}, f32[128,128]{1,0:T(8,128)S(1)}, u32[]{:S(2)}, u32[]{:S(2)}) collective-permute-start(f32[128,128]{1,0:T(8,128)S(1)} %add.323), channel_id=1, source_target_pairs={{0,4},{1,5},{2,6},{3,7},{4,8},{5,9},{6,10},{7,11},{8,12},{9,13},{1... | collective-permute-start | bytes 196616 | tf_op jit(solution)/shard_map/ppermute | solution.py:279
  194.8 10.8 %collective-permute-start.15 = (f32[512,128]{1,0:T(8,128)S(1)}, f32[512,128]{1,0:T(8,128)S(1)}, u32[]{:S(2)}, u32[]{:S(2)}) collective-permute-start(f32[512,128]{1,0:T(8,128)S(1)} %get-tuple-element.47), channel_id=1, source_target_pairs={{0,2},{1,3},{2,0},{3,1},{4,6},{5,7},{6,4},{7,5},{8,10},{9,11},{10,... | collective-permute-start | bytes 786440 | tf_op jit(solution)/shard_map/ppermute | solution.py:279
  196.8 10.8 %collective-permute-start.14 = (f32[512,128]{1,0:T(8,128)S(1)}, f32[512,128]{1,0:T(8,128)S(1)}, u32[]{:S(2)}, u32[]{:S(2)}) collective-permute-start(f32[512,128]{1,0:T(8,128)S(1)} %get-tuple-element.47), channel_id=1, source_target_pairs={{0,1},{1,2},{2,3},{3,0},{4,5},{5,6},{6,7},{7,4},{8,9},{9,10},{10,1... | collective-permute-start | bytes 786440 | tf_op jit(solution)/shard_map/ppermute | solution.py:279
  199.9 11.0 %collective-permute-start.16 = (f32[512,128]{1,0:T(8,128)S(1)}, f32[512,128]{1,0:T(8,128)S(1)}, u32[]{:S(2)}, u32[]{:S(2)}) collective-permute-start(f32[512,128]{1,0:T(8,128)S(1)} %get-tuple-element.47), channel_id=1, source_target_pairs={{0,3},{1,0},{2,1},{3,2},{4,7},{5,4},{6,5},{7,6},{8,11},{9,8},{10,9... | collective-permute-start | bytes 786440 | tf_op jit(solution)/shard_map/ppermute | solution.py:279

commit v6 on v5

--- a/solution.py
+++ b/solution.py
@@ -12,6 +12,7 @@
 
 step_scale = 0.04
 EMPTY_MARK = 1024.0
+LINK_DTYPE = jnp.bfloat16
 
 
 def extended(x, sides, width):
@@ -269,14 +270,16 @@
         total = lax.dynamic_index_in_dim(parts, coord, 0, keepdims=False)
         for shift in range(1, count):
             send = lax.dynamic_index_in_dim(parts, (coord + shift) % count, 0, keepdims=False)
-            total = total + lax.ppermute(send, "wall", group_pairs(size, off, count, shift))
+            got = lax.ppermute(send.astype(LINK_DTYPE), "wall", group_pairs(size, off, count, shift))
+            total = total + got.astype(jnp.float32)
         flat = total
     for off, count in exchange_groups:
         flat = flat + lax.ppermute(flat, "wall", group_pairs(size, off, count, 1))
     for off, count in reversed(scatter_groups):
         coord = (me >> off) & (count - 1)
-        got = [flat] + [
-            lax.ppermute(flat, "wall", group_pairs(size, off, count, shift)) for shift in range(1, count)
+        sent = flat.astype(LINK_DTYPE)
+        got = [sent] + [
+            lax.ppermute(sent, "wall", group_pairs(size, off, count, shift)) for shift in range(1, count)
         ]
         stacked = jnp.stack(got)
         flat = jnp.concatenate(
@@ -286,6 +289,7 @@
             ],
             axis=0,
         )
+    flat = flat.astype(jnp.float32)
     out = []
     at = 0
     for g in grads:

time: 216 us -> 209 us (0.968)
  waiting for transfers between devices: 73.4 us -> 60.9 us
  starting transfers between devices: 106 us -> 111 us
    ppermute x12, waiting for transfers between devices: 26.8 us -> 17.3 us  [the longest x6 8.96 us: wall_sum(): lax.ppermute(send.astype(LINK_DTYPE), 'wall', group_pairs(size, off, coun...]
    ppermute x12, starting transfers between devices: 53.4 us -> 58.1 us  [the longest x6 37.2 us: wall_sum(): lax.ppermute(send.astype(LINK_DTYPE), 'wall', group_pairs(size, off, coun...]
    ppermute x1, waiting for transfers between devices: 13.8 us -> 10.7 us  [wall_sum(): flat = flat + lax.ppermute(flat, 'wall', group_pairs(size, off, count, 1))]
    unnamed x43 -> x45, local copies, waits for them, and re-layouts: 6.45 us -> 6.78 us
  transfers between devices with their start and end apart: 18 -> 18, of which waited for: 11 -> 8; matrix products, arithmetic and copies ran while one was open for 5% -> 5% of each run, Pallas kernels for 0% -> 0%
where the time goes in v6:
time: 209 us; the launch traced here: 208 us
  starting transfers between devices  111 us (53%)
  waiting for transfers between devices  60.9 us (29%)
  local copies, waits for them, and re-layouts  14.7 us (7%)
  matrix products  13.1 us (6%)
  other arithmetic  6.2 us (3%)
  between operations  2.63 us (1%)
    ppermute x6, starting transfers between devices, wall_sum(): lax.ppermute(send.astype(LINK_DTYPE), 'wall', group_pairs(size, off, coun...  37.2 us
    all_to_all x1, waiting for transfers between devices, local(): lax.all_to_all(buffer.reshape(span_count, slot_count, width), 'span', spl...  32.9 us
    ppermute x6, starting transfers between devices, wall_sum(): lax.ppermute(sent, 'wall', group_pairs(size, off, count, shift))  20.8 us
    ppermute x1, starting transfers between devices, wall_sum(): flat = flat + lax.ppermute(flat, 'wall', group_pairs(size, off, count, 1))  16.3 us
    all_to_all x1, starting transfers between devices, local(): lax.all_to_all(buffer.reshape(span_count, slot_count, width), 'span', spl...  15.8 us
    ppermute x2, starting transfers between devices, extended(): after = lax.ppermute(first, axis, down)  14.2 us
    ppermute x1, waiting for transfers between devices, wall_sum(): flat = flat + lax.ppermute(flat, 'wall', group_pairs(size, off, count, 1))  10.7 us
    ppermute x6, waiting for transfers between devices, wall_sum(): lax.ppermute(send.astype(LINK_DTYPE), 'wall', group_pairs(size, off, coun...  8.96 us
  transfers between devices with their start and end apart: 18, of which 8 were waited for; matrix products, arithmetic and copies ran while one was open for 5% of the time, Pallas kernels for 0%

profile of v6, /device:TPU:2, one launch (start us, length us, event | category | flops | bytes accessed | tf_op | source)
XLA Modules:
  0.0 208.3 jit_solution(1438640770450352493)
XLA Ops:
  0.7 1.2 slice_bitcast_fusion.10
  2.1 0.6 copy-done.11
  3.3 3.4 %collective-permute-start.2 = (f32[2,5,5,1,1,128]{5,0,4,3,2,1:T(2,128)S(1)}, f32[2,5,5,1,1,128]{5,0,4,3,2,1:T(2,128)S(1)}, u32[]{:S(2)}, u32[]{:S(2)}) collective-permute-start(f32[2,5,5,1,1,128]{5,0,4,3,2,1:T(2,128)S(1)} %slice.134), channel_id=1, source_target_pairs={{0,1},{1,2},{2,3},{3,4},{4,5},{5,6},{6,7},{7,8},{8,9},{9,10},{10,1... | collective-permute-start | bytes 76808 | tf_op jit(solution)/shard_map/ppermute | solution.py:25
  6.8 0.5 fusion.20
  7.3 13.0 %collective-permute-start.3 = (f32[2,5,5,1,1,128]{5,0,4,3,2,1:T(2,128)S(1)}, f32[2,5,5,1,1,128]{5,0,4,3,2,1:T(2,128)S(1)}, u32[]{:S(2)}, u32[]{:S(2)}) collective-permute-start(f32[2,5,5,1,1,128]{5,0,4,3,2,1:T(2,128)S(1)} %slice.135), channel_id=1, source_target_pairs={{1,0},{2,1},{3,2},{4,3},{5,4},{6,5},{7,6},{8,7},{9,8},{10,9},{11,1... | collective-permute-start | bytes 76808 | tf_op jit(solution)/shard_map/ppermute | solution.py:26
  20.3 0.5 fusion.24
  20.7 1.3 collective-permute-start.1
  22.5 3.0 %collective-permute-start = (f32[2,5,5,1,2,128]{5,4,3,2,1,0:T(2,128)S(1)}, f32[2,5,5,1,2,128]{5,4,3,2,1,0:T(2,128)S(1)}, u32[]{:S(2)}, u32[]{:S(2)}) collective-permute-start(f32[2,5,5,1,2,128]{5,4,3,2,1,0:T(2,128)S(1)} %bitcast.413), channel_id=1, source_target_pairs={{0,32},{32,64},{64,96},{96,128},{128,160},{160,192},{192,224},{224... | collective-permute-start | bytes 153608 | tf_op jit(solution)/shard_map/ppermute | solution.py:25
  25.6 0.6 copy-done.5
  34.4 0.7 copy-done.10
  37.1 0.6 copy-done.8
  38.5 0.7 gather_fusion
  39.3 0.6 copy-done.13
  39.9 0.7 broadcast_in_dim.41
  40.7 2.7 %scatter_custom_fusion = bf16[512,256]{1,0:T(8,128)(2,1)} fusion(bf16[512,256]{1,0:T(8,128)(2,1)} %broadcast_in_dim.41, s32[128]{0:T(128)S(1)} %fusion.110, bf16[128,128]{1,0:T(8,128)(2,1)S(1)} %copy-done.7, bf16[]{:T(256)} %constant.213, bf16[128,128]{1,0:T(8,128)(2,1)S(1)} %select_convert_fusion), kind=kCustom, calls=%fused_computation.137 | custom fusion | flops 131072 | bytes 328192 | tf_op jit(solution)/shard_map/scatter | solution.py:225
  43.3 15.8 %all-to-all-start = ((bf16[32,16,256]{2,1,0:T(8,128)(2,1)}), bf16[32,16,256]{2,1,0:T(8,128)(2,1)S(1)}, u32[]{:S(2)}, u32[]{:S(2)}) async-start(bf16[32,16,256]{2,1,0:T(8,128)(2,1)} %bitcast.141), calls=%async_computation | async-start | bytes 524288 | tf_op jit(solution)/shard_map/all_to_all | solution.py:226
  59.2 32.9 %all-to-all-done = bf16[32,16,256]{2,1,0:T(8,128)(2,1)S(1)} async-done(((bf16[32,16,256]{2,1,0:T(8,128)(2,1)}), bf16[32,16,256]{2,1,0:T(8,128)(2,1)S(1)}, u32[]{:S(2)}, u32[]{:S(2)}) %all-to-all-start) | async-done | bytes 262176 | tf_op jit(solution)/shard_map/all_to_all | solution.py:226
  92.3 0.6 convert_reduce_fusion
  93.6 1.0 multiply_convert_fusion.3
  95.4 0.6 copy-done.3
  96.2 0.6 copy-done.16
  98.9 0.8 copy-done.18
  100.8 3.4 %collective-permute-start.4 = (bf16[512,128]{1,0:T(8,128)(2,1)S(1)}, bf16[512,128]{1,0:T(8,128)(2,1)S(1)}, u32[]{:S(2)}, u32[]{:S(2)}) collective-permute-start(bf16[512,128]{1,0:T(8,128)(2,1)S(1)} %get-tuple-element.29), channel_id=1, source_target_pairs={{0,1},{1,2},{2,3},{3,0},{4,5},{5,6},{6,7},{7,4},{8,9},{9,10},{10,1... | collective-permute-start | bytes 393224 | tf_op jit(solution)/shard_map/ppermute | solution.py:273
  104.2 2.4 %collective-permute-start.6 = (bf16[512,128]{1,0:T(8,128)(2,1)S(1)}, bf16[512,128]{1,0:T(8,128)(2,1)S(1)}, u32[]{:S(2)}, u32[]{:S(2)}) collective-permute-start(bf16[512,128]{1,0:T(8,128)(2,1)S(1)} %get-tuple-element.30), channel_id=1, source_target_pairs={{0,3},{1,0},{2,1},{3,2},{4,7},{5,4},{6,5},{7,6},{8,11},{9,8},{10,9... | collective-permute-start | bytes 393224 | tf_op jit(solution)/shard_map/ppermute | solution.py:273
  106.7 4.0 %collective-permute-start.5 = (bf16[512,128]{1,0:T(8,128)(2,1)S(1)}, bf16[512,128]{1,0:T(8,128)(2,1)S(1)}, u32[]{:S(2)}, u32[]{:S(2)}) collective-permute-start(bf16[512,128]{1,0:T(8,128)(2,1)S(1)} %get-tuple-element.31), channel_id=1, source_target_pairs={{0,2},{1,3},{2,0},{3,1},{4,6},{5,7},{6,4},{7,5},{8,10},{9,11},{10,... | collective-permute-start | bytes 393224 | tf_op jit(solution)/shard_map/ppermute | solution.py:273
  110.8 1.4 collective-permute-done.6
  112.1 3.7 %collective-permute-done.5 = bf16[512,128]{1,0:T(8,128)(2,1)S(1)} collective-permute-done((bf16[512,128]{1,0:T(8,128)(2,1)S(1)}, bf16[512,128]{1,0:T(8,128)(2,1)S(1)}, u32[]{:S(2)}, u32[]{:S(2)}) %collective-permute-start.5) | collective-permute-done | bytes 131104 | tf_op jit(solution)/shard_map/ppermute | solution.py:273
  115.9 4.4 %collective-permute-start.7 = (bf16[128,128]{1,0:T(8,128)(2,1)S(1)}, bf16[128,128]{1,0:T(8,128)(2,1)S(1)}, u32[]{:S(2)}, u32[]{:S(2)}) collective-permute-start(bf16[128,128]{1,0:T(8,128)(2,1)S(1)} %get-tuple-element.46), channel_id=1, source_target_pairs={{0,4},{1,5},{2,6},{3,7},{4,8},{5,9},{6,10},{7,11},{8,12},{9,13},{1... | collective-permute-start | bytes 98312 | tf_op jit(solution)/shard_map/ppermute | solution.py:273
  120.3 19.6 %collective-permute-start.9 = (bf16[128,128]{1,0:T(8,128)(2,1)S(1)}, bf16[128,128]{1,0:T(8,128)(2,1)S(1)}, u32[]{:S(2)}, u32[]{:S(2)}) collective-permute-start(bf16[128,128]{1,0:T(8,128)(2,1)S(1)} %get-tuple-element.47), channel_id=1, source_target_pairs={{0,12},{1,13},{2,14},{3,15},{4,0},{5,1},{6,2},{7,3},{8,4},{9,5},{1... | collective-permute-start | bytes 98312 | tf_op jit(solution)/shard_map/ppermute | solution.py:273
  139.9 3.4 %collective-permute-start.8 = (bf16[128,128]{1,0:T(8,128)(2,1)S(1)}, bf16[128,128]{1,0:T(8,128)(2,1)S(1)}, u32[]{:S(2)}, u32[]{:S(2)}) collective-permute-start(bf16[128,128]{1,0:T(8,128)(2,1)S(1)} %get-tuple-element.48), channel_id=1, source_target_pairs={{0,8},{1,9},{2,10},{3,11},{4,12},{5,13},{6,14},{7,15},{8,0},{9,1},... | collective-permute-start | bytes 98312 | tf_op jit(solution)/shard_map/ppermute | solution.py:273
  143.3 3.9 %collective-permute-done.8 = bf16[128,128]{1,0:T(8,128)(2,1)S(1)} collective-permute-done((bf16[128,128]{1,0:T(8,128)(2,1)S(1)}, bf16[128,128]{1,0:T(8,128)(2,1)S(1)}, u32[]{:S(2)}, u32[]{:S(2)}) %collective-permute-start.8) | collective-permute-done | bytes 32800 | tf_op jit(solution)/shard_map/ppermute | solution.py:273
  147.2 16.3 %collective-permute-start.10 = (f32[128,128]{1,0:T(8,128)S(1)}, f32[128,128]{1,0:T(8,128)S(1)}, u32[]{:S(2)}, u32[]{:S(2)}) collective-permute-start(f32[128,128]{1,0:T(8,128)S(1)} %fusion.100), channel_id=1, source_target_pairs={{0,16},{1,17},{2,18},{3,19},{4,20},{5,21},{6,22},{7,23},{8,24},{9,... | collective-permute-start | bytes 196616 | tf_op jit(solution)/shard_map/ppermute | solution.py:277
  163.5 10.7 %collective-permute-done.10 = f32[128,128]{1,0:T(8,128)S(1)} collective-permute-done((f32[128,128]{1,0:T(8,128)S(1)}, f32[128,128]{1,0:T(8,128)S(1)}, u32[]{:S(2)}, u32[]{:S(2)}) %collective-permute-start.10) | collective-permute-done | bytes 65568 | tf_op jit(solution)/shard_map/ppermute | solution.py:277
  174.2 6.3 %collective-permute-start.13 = (bf16[128,128]{1,0:T(8,128)(2,1)S(1)}, bf16[128,128]{1,0:T(8,128)(2,1)S(1)}, u32[]{:S(2)}, u32[]{:S(2)}) collective-permute-start(bf16[128,128]{1,0:T(8,128)(2,1)S(1)} %add_convert_fusion), channel_id=1, source_target_pairs={{0,12},{1,13},{2,14},{3,15},{4,0},{5,1},{6,2},{7,3},{8,4},{9,5},{1... | collective-permute-start | bytes 98312 | tf_op jit(solution)/shard_map/ppermute | solution.py:282
  180.6 1.9 collective-permute-start.12
  182.5 2.8 %collective-permute-start.11 = (bf16[128,128]{1,0:T(8,128)(2,1)S(1)}, bf16[128,128]{1,0:T(8,128)(2,1)S(1)}, u32[]{:S(2)}, u32[]{:S(2)}) collective-permute-start(bf16[128,128]{1,0:T(8,128)(2,1)S(1)} %add_convert_fusion), channel_id=1, source_target_pairs={{0,4},{1,5},{2,6},{3,7},{4,8},{5,9},{6,10},{7,11},{8,12},{9,13},{1... | collective-permute-start | bytes 98312 | tf_op jit(solution)/shard_map/ppermute | solution.py:282
  185.4 2.5 %collective-permute-done.12 = bf16[128,128]{1,0:T(8,128)(2,1)S(1)} collective-permute-done((bf16[128,128]{1,0:T(8,128)(2,1)S(1)}, bf16[128,128]{1,0:T(8,128)(2,1)S(1)}, u32[]{:S(2)}, u32[]{:S(2)}) %collective-permute-start.12) | collective-permute-done | bytes 32800 | tf_op jit(solution)/shard_map/ppermute | solution.py:282
  187.9 1.6 collective-permute-done.11
  189.6 3.3 %collective-permute-start.15 = (bf16[512,128]{1,0:T(8,128)(2,1)S(1)}, bf16[512,128]{1,0:T(8,128)(2,1)S(1)}, u32[]{:S(2)}, u32[]{:S(2)}) collective-permute-start(bf16[512,128]{1,0:T(8,128)(2,1)S(1)} %get-tuple-element.50), channel_id=1, source_target_pairs={{0,2},{1,3},{2,0},{3,1},{4,6},{5,7},{6,4},{7,5},{8,10},{9,11},{10,... | collective-permute-start | bytes 393224 | tf_op jit(solution)/shard_map/ppermute | solution.py:282
  192.9 4.6 %collective-permute-start.14 = (bf16[512,128]{1,0:T(8,128)(2,1)S(1)}, bf16[512,128]{1,0:T(8,128)(2,1)S(1)}, u32[]{:S(2)}, u32[]{:S(2)}) collective-permute-start(bf16[512,128]{1,0:T(8,128)(2,1)S(1)} %get-tuple-element.50), channel_id=1, source_target_pairs={{0,1},{1,2},{2,3},{3,0},{4,5},{5,6},{6,7},{7,4},{8,9},{9,10},{10,1... | collective-permute-start | bytes 393224 | tf_op jit(solution)/shard_map/ppermute | solution.py:282
  197.5 1.9 collective-permute-start.16
  199.5 0.7 copy.86
  200.2 4.1 %collective-permute-done.16 = bf16[512,128]{1,0:T(8,128)(2,1)S(1)} collective-permute-done((bf16[512,128]{1,0:T(8,128)(2,1)S(1)}, bf16[512,128]{1,0:T(8,128)(2,1)S(1)}, u32[]{:S(2)}, u32[]{:S(2)}) %collective-permute-start.16) | collective-permute-done | bytes 131104 | tf_op jit(solution)/shard_map/ppermute | solution.py:282
  204.5 0.7 convert_bitcast_fusion
  205.2 0.7 broadcast_in_dim_reshape.12
  206.0 0.8 broadcast_in_dim_reshape.15
  206.8 0.8 broadcast_in_dim_reshape.14
  207.5 0.8 broadcast_in_dim_reshape.13
  (144 shorter events, 16.6 us)
Async XLA Ops:
  0.6 94.5 %copy-start = (bf16[1,256,256]{2,1,0:T(8,128)(2,1)S(1)}, bf16[1,256,256]{2,1,0:T(8,128)(2,1)}, u32[]{:S(2)}) copy-start(bf16[1,256,256]{2,1,0:T(8,128)(2,1)} %param.22) | copy-start | bytes 393220
  0.6 1.3 copy-start.1
  2.1 0.7 copy-start.11
  3.3 3.4 %copy-start.12 = (f32[5,1,1,1,1,1]{0,1,5,4,3,2:T(1,128)S(1)}, f32[5,1,1,1,1,1]{0,1,5,4,3,2:T(1,128)}, u32[]{:S(2)}) copy-start(f32[5,1,1,1,1,1]{0,1,5,4,3,2:T(1,128)} %constant.210) | copy-start | bytes 64
  3.3 33.4 %collective-permute-start.2 = (f32[2,5,5,1,1,128]{5,0,4,3,2,1:T(2,128)S(1)}, f32[2,5,5,1,1,128]{5,0,4,3,2,1:T(2,128)S(1)}, u32[]{:S(2)}, u32[]{:S(2)}) collective-permute-start(f32[2,5,5,1,1,128]{5,0,4,3,2,1:T(2,128)S(1)} %slice.134), channel_id=1, source_target_pairs={{0,1},{1,2},{2,3},{3,4},{4,5},{5,6},{6,7},{7,8},{8,9},{9,10},{10,1... | collective-permute-start | bytes 76808 | tf_op jit(solution)/shard_map/ppermute | solution.py:25
  7.3 29.5 %collective-permute-start.3 = (f32[2,5,5,1,1,128]{5,0,4,3,2,1:T(2,128)S(1)}, f32[2,5,5,1,1,128]{5,0,4,3,2,1:T(2,128)S(1)}, u32[]{:S(2)}, u32[]{:S(2)}) collective-permute-start(f32[2,5,5,1,1,128]{5,0,4,3,2,1:T(2,128)S(1)} %slice.135), channel_id=1, source_target_pairs={{1,0},{2,1},{3,2},{4,3},{5,4},{6,5},{7,6},{8,7},{9,8},{10,9},{11,1... | collective-permute-start | bytes 76808 | tf_op jit(solution)/shard_map/ppermute | solution.py:26
  20.7 16.2 %collective-permute-start.1 = (f32[2,5,5,1,2,128]{5,4,3,2,1,0:T(2,128)S(1)}, f32[2,5,5,1,2,128]{5,4,3,2,1,0:T(2,128)S(1)}, u32[]{:S(2)}, u32[]{:S(2)}) collective-permute-start(f32[2,5,5,1,2,128]{5,4,3,2,1,0:T(2,128)S(1)} %bitcast.414), channel_id=1, source_target_pairs={{32,0},{64,32},{96,64},{128,96},{160,128},{192,160},{224,192},{256... | collective-permute-start | bytes 153608 | tf_op jit(solution)/shard_map/ppermute | solution.py:26
  22.5 3.1 %copy-start.17 = (s32[128]{0:T(128)S(1)}, s32[128]{0:T(128)}, u32[]{:S(2)}) copy-start(s32[128]{0:T(128)} %param.17) | copy-start | bytes 1540
  22.5 14.5 %collective-permute-start = (f32[2,5,5,1,2,128]{5,4,3,2,1,0:T(2,128)S(1)}, f32[2,5,5,1,2,128]{5,4,3,2,1,0:T(2,128)S(1)}, u32[]{:S(2)}, u32[]{:S(2)}) collective-permute-start(f32[2,5,5,1,2,128]{5,4,3,2,1,0:T(2,128)S(1)} %bitcast.413), channel_id=1, source_target_pairs={{0,32},{32,64},{64,96},{96,128},{128,160},{160,192},{192,224},{224... | collective-permute-start | bytes 153608 | tf_op jit(solution)/shard_map/ppermute | solution.py:25
  25.6 0.7 copy-start.5
  26.9 0.7 copy-start.4
  27.6 1.0 copy-start.2
  30.3 0.7 copy-start.6
  34.4 0.7 copy-start.10
  37.0 0.7 copy-start.8
  37.1 0.7 copy-start.9
  39.2 0.7 copy-start.13
  39.9 0.8 copy-start.7
  43.3 48.8 %all-to-all-start = ((bf16[32,16,256]{2,1,0:T(8,128)(2,1)}), bf16[32,16,256]{2,1,0:T(8,128)(2,1)S(1)}, u32[]{:S(2)}, u32[]{:S(2)}) async-start(bf16[32,16,256]{2,1,0:T(8,128)(2,1)} %bitcast.141), calls=%async_computation | async-start | bytes 524288 | tf_op jit(solution)/shard_map/all_to_all | solution.py:226
  92.1 1.5 copy-start.15
  93.6 1.2 copy-start.14
  95.1 0.9 copy-start.3
  96.0 0.8 copy-start.16
  98.7 1.0 copy-start.18
  100.8 10.0 %collective-permute-start.4 = (bf16[512,128]{1,0:T(8,128)(2,1)S(1)}, bf16[512,128]{1,0:T(8,128)(2,1)S(1)}, u32[]{:S(2)}, u32[]{:S(2)}) collective-permute-start(bf16[512,128]{1,0:T(8,128)(2,1)S(1)} %get-tuple-element.29), channel_id=1, source_target_pairs={{0,1},{1,2},{2,3},{3,0},{4,5},{5,6},{6,7},{7,4},{8,9},{9,10},{10,1... | collective-permute-start | bytes 393224 | tf_op jit(solution)/shard_map/ppermute | solution.py:273
  104.2 7.9 %collective-permute-start.6 = (bf16[512,128]{1,0:T(8,128)(2,1)S(1)}, bf16[512,128]{1,0:T(8,128)(2,1)S(1)}, u32[]{:S(2)}, u32[]{:S(2)}) collective-permute-start(bf16[512,128]{1,0:T(8,128)(2,1)S(1)} %get-tuple-element.30), channel_id=1, source_target_pairs={{0,3},{1,0},{2,1},{3,2},{4,7},{5,4},{6,5},{7,6},{8,11},{9,8},{10,9... | collective-permute-start | bytes 393224 | tf_op jit(solution)/shard_map/ppermute | solution.py:273
  106.7 9.1 %collective-permute-start.5 = (bf16[512,128]{1,0:T(8,128)(2,1)S(1)}, bf16[512,128]{1,0:T(8,128)(2,1)S(1)}, u32[]{:S(2)}, u32[]{:S(2)}) collective-permute-start(bf16[512,128]{1,0:T(8,128)(2,1)S(1)} %get-tuple-element.31), channel_id=1, source_target_pairs={{0,2},{1,3},{2,0},{3,1},{4,6},{5,7},{6,4},{7,5},{8,10},{9,11},{10,... | collective-permute-start | bytes 393224 | tf_op jit(solution)/shard_map/ppermute | solution.py:273
  115.9 27.4 %collective-permute-start.7 = (bf16[128,128]{1,0:T(8,128)(2,1)S(1)}, bf16[128,128]{1,0:T(8,128)(2,1)S(1)}, u32[]{:S(2)}, u32[]{:S(2)}) collective-permute-start(bf16[128,128]{1,0:T(8,128)(2,1)S(1)} %get-tuple-element.46), channel_id=1, source_target_pairs={{0,4},{1,5},{2,6},{3,7},{4,8},{5,9},{6,10},{7,11},{8,12},{9,13},{1... | collective-permute-start | bytes 98312 | tf_op jit(solution)/shard_map/ppermute | solution.py:273
  120.3 23.0 %collective-permute-start.9 = (bf16[128,128]{1,0:T(8,128)(2,1)S(1)}, bf16[128,128]{1,0:T(8,128)(2,1)S(1)}, u32[]{:S(2)}, u32[]{:S(2)}) collective-permute-start(bf16[128,128]{1,0:T(8,128)(2,1)S(1)} %get-tuple-element.47), channel_id=1, source_target_pairs={{0,12},{1,13},{2,14},{3,15},{4,0},{5,1},{6,2},{7,3},{8,4},{9,5},{1... | collective-permute-start | bytes 98312 | tf_op jit(solution)/shard_map/ppermute | solution.py:273
  139.9 7.3 %collective-permute-start.8 = (bf16[128,128]{1,0:T(8,128)(2,1)S(1)}, bf16[128,128]{1,0:T(8,128)(2,1)S(1)}, u32[]{:S(2)}, u32[]{:S(2)}) collective-permute-start(bf16[128,128]{1,0:T(8,128)(2,1)S(1)} %get-tuple-element.48), channel_id=1, source_target_pairs={{0,8},{1,9},{2,10},{3,11},{4,12},{5,13},{6,14},{7,15},{8,0},{9,1},... | collective-permute-start | bytes 98312 | tf_op jit(solution)/shard_map/ppermute | solution.py:273
  147.2 27.0 %collective-permute-start.10 = (f32[128,128]{1,0:T(8,128)S(1)}, f32[128,128]{1,0:T(8,128)S(1)}, u32[]{:S(2)}, u32[]{:S(2)}) collective-permute-start(f32[128,128]{1,0:T(8,128)S(1)} %fusion.100), channel_id=1, source_target_pairs={{0,16},{1,17},{2,18},{3,19},{4,20},{5,21},{6,22},{7,23},{8,24},{9,... | collective-permute-start | bytes 196616 | tf_op jit(solution)/shard_map/ppermute | solution.py:277
  174.2 11.1 %collective-permute-start.13 = (bf16[128,128]{1,0:T(8,128)(2,1)S(1)}, bf16[128,128]{1,0:T(8,128)(2,1)S(1)}, u32[]{:S(2)}, u32[]{:S(2)}) collective-permute-start(bf16[128,128]{1,0:T(8,128)(2,1)S(1)} %add_convert_fusion), channel_id=1, source_target_pairs={{0,12},{1,13},{2,14},{3,15},{4,0},{5,1},{6,2},{7,3},{8,4},{9,5},{1... | collective-permute-start | bytes 98312 | tf_op jit(solution)/shard_map/ppermute | solution.py:282
  180.6 7.3 %collective-permute-start.12 = (bf16[128,128]{1,0:T(8,128)(2,1)S(1)}, bf16[128,128]{1,0:T(8,128)(2,1)S(1)}, u32[]{:S(2)}, u32[]{:S(2)}) collective-permute-start(bf16[128,128]{1,0:T(8,128)(2,1)S(1)} %add_convert_fusion), channel_id=1, source_target_pairs={{0,8},{1,9},{2,10},{3,11},{4,12},{5,13},{6,14},{7,15},{8,0},{9,1},... | collective-permute-start | bytes 98312 | tf_op jit(solution)/shard_map/ppermute | solution.py:282
  182.5 7.0 %collective-permute-start.11 = (bf16[128,128]{1,0:T(8,128)(2,1)S(1)}, bf16[128,128]{1,0:T(8,128)(2,1)S(1)}, u32[]{:S(2)}, u32[]{:S(2)}) collective-permute-start(bf16[128,128]{1,0:T(8,128)(2,1)S(1)} %add_convert_fusion), channel_id=1, source_target_pairs={{0,4},{1,5},{2,6},{3,7},{4,8},{5,9},{6,10},{7,11},{8,12},{9,13},{1... | collective-permute-start | bytes 98312 | tf_op jit(solution)/shard_map/ppermute | solution.py:282
  189.6 10.6 %collective-permute-start.15 = (bf16[512,128]{1,0:T(8,128)(2,1)S(1)}, bf16[512,128]{1,0:T(8,128)(2,1)S(1)}, u32[]{:S(2)}, u32[]{:S(2)}) collective-permute-start(bf16[512,128]{1,0:T(8,128)(2,1)S(1)} %get-tuple-element.50), channel_id=1, source_target_pairs={{0,2},{1,3},{2,0},{3,1},{4,6},{5,7},{6,4},{7,5},{8,10},{9,11},{10,... | collective-permute-start | bytes 393224 | tf_op jit(solution)/shard_map/ppermute | solution.py:282
  192.9 7.3 %collective-permute-start.14 = (bf16[512,128]{1,0:T(8,128)(2,1)S(1)}, bf16[512,128]{1,0:T(8,128)(2,1)S(1)}, u32[]{:S(2)}, u32[]{:S(2)}) collective-permute-start(bf16[512,128]{1,0:T(8,128)(2,1)S(1)} %get-tuple-element.50), channel_id=1, source_target_pairs={{0,1},{1,2},{2,3},{3,0},{4,5},{5,6},{6,7},{7,4},{8,9},{9,10},{10,1... | collective-permute-start | bytes 393224 | tf_op jit(solution)/shard_map/ppermute | solution.py:282
  197.5 6.9 %collective-permute-start.16 = (bf16[512,128]{1,0:T(8,128)(2,1)S(1)}, bf16[512,128]{1,0:T(8,128)(2,1)S(1)}, u32[]{:S(2)}, u32[]{:S(2)}) collective-permute-start(bf16[512,128]{1,0:T(8,128)(2,1)S(1)} %get-tuple-element.50), channel_id=1, source_target_pairs={{0,3},{1,0},{2,1},{3,2},{4,7},{5,4},{6,5},{7,6},{8,11},{9,8},{10,9... | collective-permute-start | bytes 393224 | tf_op jit(solution)/shard_map/ppermute | solution.py:282

commit v7 on v6

--- a/solution.py
+++ b/solution.py
@@ -270,8 +270,7 @@
         total = lax.dynamic_index_in_dim(parts, coord, 0, keepdims=False)
         for shift in range(1, count):
             send = lax.dynamic_index_in_dim(parts, (coord + shift) % count, 0, keepdims=False)
-            got = lax.ppermute(send.astype(LINK_DTYPE), "wall", group_pairs(size, off, count, shift))
-            total = total + got.astype(jnp.float32)
+            total = total + lax.ppermute(send, "wall", group_pairs(size, off, count, shift))
         flat = total
     for off, count in exchange_groups:
         flat = flat + lax.ppermute(flat, "wall", group_pairs(size, off, count, 1))

time: 209 us -> 213 us (1.019)
  the two profiles are of different devices: /device:TPU:2 before, /device:TPU:64 now
where the time goes in v7:
time: 213 us; the launch traced here: 212 us
  starting transfers between devices  119 us (56%)
  waiting for transfers between devices  57.3 us (27%)
  local copies, waits for them, and re-layouts  14.3 us (7%)
  matrix products  12.4 us (6%)
  other arithmetic  6.2 us (3%)
  between operations  2.62 us (1%)
    ppermute x6, starting transfers between devices, wall_sum(): lax.ppermute(send, 'wall', group_pairs(size, off, count, shift))  39.5 us
    all_to_all x1, waiting for transfers between devices, local(): lax.all_to_all(buffer.reshape(span_count, slot_count, width), 'span', spl...  32.3 us
    ppermute x6, starting transfers between devices, wall_sum(): lax.ppermute(sent, 'wall', group_pairs(size, off, count, shift))  27.4 us
    all_to_all x1, starting transfers between devices, local(): lax.all_to_all(buffer.reshape(span_count, slot_count, width), 'span', spl...  25.6 us
    ppermute x1, starting transfers between devices, wall_sum(): flat = flat + lax.ppermute(flat, 'wall', group_pairs(size, off, count, 1))  17.4 us
    ppermute x6, waiting for transfers between devices, wall_sum(): lax.ppermute(send, 'wall', group_pairs(size, off, count, shift))  10.6 us
    ppermute x1, waiting for transfers between devices, wall_sum(): flat = flat + lax.ppermute(flat, 'wall', group_pairs(size, off, count, 1))  7.49 us
    dot_general x22, matrix products, at_face(): jnp.tensordot(vector, field, axes=([0], [axis]), precision=lax.Precision....  7.38 us
  transfers between devices with their start and end apart: 18, of which 9 were waited for; matrix products, arithmetic and copies ran while one was open for 5% of the time, Pallas kernels for 0%

profile of v7, /device:TPU:64, one launch (start us, length us, event | category | flops | bytes accessed | tf_op | source)
XLA Modules:
  0.0 211.8 jit_solution(14910854285052183326)
XLA Ops:
  0.7 1.2 slice_bitcast_fusion.10
  2.1 0.6 copy-done.11
  3.3 3.4 %collective-permute-start.2 = (f32[2,5,5,1,1,128]{5,0,4,3,2,1:T(2,128)S(1)}, f32[2,5,5,1,1,128]{5,0,4,3,2,1:T(2,128)S(1)}, u32[]{:S(2)}, u32[]{:S(2)}) collective-permute-start(f32[2,5,5,1,1,128]{5,0,4,3,2,1:T(2,128)S(1)} %slice.134), channel_id=1, source_target_pairs={{0,1},{1,2},{2,3},{3,4},{4,5},{5,6},{6,7},{7,8},{8,9},{9,10},{10,1... | collective-permute-start | bytes 76808 | tf_op jit(solution)/shard_map/ppermute | solution.py:25
  6.8 0.5 fusion.20
  7.3 1.3 collective-permute-start.3
  8.6 0.5 fusion.24
  9.1 1.9 collective-permute-start.1
  11.0 0.5 fusion.26
  11.5 2.4 %collective-permute-start = (f32[2,5,5,1,2,128]{5,4,3,2,1,0:T(2,128)S(1)}, f32[2,5,5,1,2,128]{5,4,3,2,1,0:T(2,128)S(1)}, u32[]{:S(2)}, u32[]{:S(2)}) collective-permute-start(f32[2,5,5,1,2,128]{5,4,3,2,1,0:T(2,128)S(1)} %bitcast.413), channel_id=1, source_target_pairs={{0,32},{32,64},{64,96},{96,128},{128,160},{160,192},{192,224},{224... | collective-permute-start | bytes 153608 | tf_op jit(solution)/shard_map/ppermute | solution.py:25
  14.0 0.6 copy-done.5
  22.8 0.7 copy-done.10
  25.5 0.6 copy-done.8
  26.9 0.7 gather_fusion
  27.7 0.6 copy-done.13
  28.2 0.7 broadcast_in_dim.41
  29.0 2.7 %scatter_custom_fusion = bf16[512,256]{1,0:T(8,128)(2,1)} fusion(bf16[512,256]{1,0:T(8,128)(2,1)} %broadcast_in_dim.41, s32[128]{0:T(128)S(1)} %fusion.104, bf16[128,128]{1,0:T(8,128)(2,1)S(1)} %copy-done.7, bf16[]{:T(256)} %constant.213, bf16[128,128]{1,0:T(8,128)(2,1)S(1)} %select_convert_fusion), kind=kCustom, calls=%fused_computation.134 | custom fusion | flops 131072 | bytes 328192 | tf_op jit(solution)/shard_map/scatter | solution.py:225
  31.7 25.6 %all-to-all-start = ((bf16[32,16,256]{2,1,0:T(8,128)(2,1)}), bf16[32,16,256]{2,1,0:T(8,128)(2,1)S(1)}, u32[]{:S(2)}, u32[]{:S(2)}) async-start(bf16[32,16,256]{2,1,0:T(8,128)(2,1)} %bitcast.141), calls=%async_computation | async-start | bytes 524288 | tf_op jit(solution)/shard_map/all_to_all | solution.py:226
  57.3 32.3 %all-to-all-done = bf16[32,16,256]{2,1,0:T(8,128)(2,1)S(1)} async-done(((bf16[32,16,256]{2,1,0:T(8,128)(2,1)}), bf16[32,16,256]{2,1,0:T(8,128)(2,1)S(1)}, u32[]{:S(2)}, u32[]{:S(2)}) %all-to-all-start) | async-done | bytes 262176 | tf_op jit(solution)/shard_map/all_to_all | solution.py:226
  89.8 0.6 convert_reduce_fusion
  92.6 0.6 copy-done.3
  93.4 0.6 copy-done.16
  96.1 0.5 fusion.8
  97.2 4.6 %collective-permute-start.4 = (f32[512,128]{1,0:T(8,128)S(1)}, f32[512,128]{1,0:T(8,128)S(1)}, u32[]{:S(2)}, u32[]{:S(2)}) collective-permute-start(f32[512,128]{1,0:T(8,128)S(1)} %get-tuple-element.29), channel_id=1, source_target_pairs={{0,1},{1,2},{2,3},{3,0},{4,5},{5,6},{6,7},{7,4},{8,9},{9,10},{10,1... | collective-permute-start | bytes 786440 | tf_op jit(solution)/shard_map/ppermute | solution.py:273
  101.8 3.2 %collective-permute-start.6 = (f32[512,128]{1,0:T(8,128)S(1)}, f32[512,128]{1,0:T(8,128)S(1)}, u32[]{:S(2)}, u32[]{:S(2)}) collective-permute-start(f32[512,128]{1,0:T(8,128)S(1)} %get-tuple-element.30), channel_id=1, source_target_pairs={{0,3},{1,0},{2,1},{3,2},{4,7},{5,4},{6,5},{7,6},{8,11},{9,8},{10,9... | collective-permute-start | bytes 786440 | tf_op jit(solution)/shard_map/ppermute | solution.py:273
  105.0 4.2 %collective-permute-start.5 = (f32[512,128]{1,0:T(8,128)S(1)}, f32[512,128]{1,0:T(8,128)S(1)}, u32[]{:S(2)}, u32[]{:S(2)}) collective-permute-start(f32[512,128]{1,0:T(8,128)S(1)} %get-tuple-element.31), channel_id=1, source_target_pairs={{0,2},{1,3},{2,0},{3,1},{4,6},{5,7},{6,4},{7,5},{8,10},{9,11},{10,... | collective-permute-start | bytes 786440 | tf_op jit(solution)/shard_map/ppermute | solution.py:273
  109.2 3.5 %collective-permute-done.6 = f32[512,128]{1,0:T(8,128)S(1)} collective-permute-done((f32[512,128]{1,0:T(8,128)S(1)}, f32[512,128]{1,0:T(8,128)S(1)}, u32[]{:S(2)}, u32[]{:S(2)}) %collective-permute-start.6) | collective-permute-done | bytes 262176 | tf_op jit(solution)/shard_map/ppermute | solution.py:273
  112.7 2.9 %collective-permute-done.5 = f32[512,128]{1,0:T(8,128)S(1)} collective-permute-done((f32[512,128]{1,0:T(8,128)S(1)}, f32[512,128]{1,0:T(8,128)S(1)}, u32[]{:S(2)}, u32[]{:S(2)}) %collective-permute-start.5) | collective-permute-done | bytes 262176 | tf_op jit(solution)/shard_map/ppermute | solution.py:273
  115.7 5.8 %collective-permute-start.7 = (f32[128,128]{1,0:T(8,128)S(1)}, f32[128,128]{1,0:T(8,128)S(1)}, u32[]{:S(2)}, u32[]{:S(2)}) collective-permute-start(f32[128,128]{1,0:T(8,128)S(1)} %get-tuple-element.46), channel_id=1, source_target_pairs={{0,4},{1,5},{2,6},{3,7},{4,8},{5,9},{6,10},{7,11},{8,12},{9,13},{1... | collective-permute-start | bytes 196616 | tf_op jit(solution)/shard_map/ppermute | solution.py:273
  121.5 18.4 %collective-permute-start.9 = (f32[128,128]{1,0:T(8,128)S(1)}, f32[128,128]{1,0:T(8,128)S(1)}, u32[]{:S(2)}, u32[]{:S(2)}) collective-permute-start(f32[128,128]{1,0:T(8,128)S(1)} %get-tuple-element.47), channel_id=1, source_target_pairs={{0,12},{1,13},{2,14},{3,15},{4,0},{5,1},{6,2},{7,3},{8,4},{9,5},{1... | collective-permute-start | bytes 196616 | tf_op jit(solution)/shard_map/ppermute | solution.py:273
  139.9 3.4 %collective-permute-start.8 = (f32[128,128]{1,0:T(8,128)S(1)}, f32[128,128]{1,0:T(8,128)S(1)}, u32[]{:S(2)}, u32[]{:S(2)}) collective-permute-start(f32[128,128]{1,0:T(8,128)S(1)} %get-tuple-element.48), channel_id=1, source_target_pairs={{0,8},{1,9},{2,10},{3,11},{4,12},{5,13},{6,14},{7,15},{8,0},{9,1},... | collective-permute-start | bytes 196616 | tf_op jit(solution)/shard_map/ppermute | solution.py:273
  143.3 4.3 %collective-permute-done.8 = f32[128,128]{1,0:T(8,128)S(1)} collective-permute-done((f32[128,128]{1,0:T(8,128)S(1)}, f32[128,128]{1,0:T(8,128)S(1)}, u32[]{:S(2)}, u32[]{:S(2)}) %collective-permute-start.8) | collective-permute-done | bytes 65568 | tf_op jit(solution)/shard_map/ppermute | solution.py:273
  147.6 17.4 %collective-permute-start.10 = (f32[128,128]{1,0:T(8,128)S(1)}, f32[128,128]{1,0:T(8,128)S(1)}, u32[]{:S(2)}, u32[]{:S(2)}) collective-permute-start(f32[128,128]{1,0:T(8,128)S(1)} %fusion.97), channel_id=1, source_target_pairs={{0,16},{1,17},{2,18},{3,19},{4,20},{5,21},{6,22},{7,23},{8,24},{9,... | collective-permute-start | bytes 196616 | tf_op jit(solution)/shard_map/ppermute | solution.py:276
  165.0 7.5 %collective-permute-done.10 = f32[128,128]{1,0:T(8,128)S(1)} collective-permute-done((f32[128,128]{1,0:T(8,128)S(1)}, f32[128,128]{1,0:T(8,128)S(1)}, u32[]{:S(2)}, u32[]{:S(2)}) %collective-permute-start.10) | collective-permute-done | bytes 65568 | tf_op jit(solution)/shard_map/ppermute | solution.py:276
  172.5 10.7 %collective-permute-start.13 = (bf16[128,128]{1,0:T(8,128)(2,1)S(1)}, bf16[128,128]{1,0:T(8,128)(2,1)S(1)}, u32[]{:S(2)}, u32[]{:S(2)}) collective-permute-start(bf16[128,128]{1,0:T(8,128)(2,1)S(1)} %add_convert_fusion), channel_id=1, source_target_pairs={{0,12},{1,13},{2,14},{3,15},{4,0},{5,1},{6,2},{7,3},{8,4},{9,5},{1... | collective-permute-start | bytes 98312 | tf_op jit(solution)/shard_map/ppermute | solution.py:281
  183.2 1.9 collective-permute-start.12
  185.2 3.0 %collective-permute-start.11 = (bf16[128,128]{1,0:T(8,128)(2,1)S(1)}, bf16[128,128]{1,0:T(8,128)(2,1)S(1)}, u32[]{:S(2)}, u32[]{:S(2)}) collective-permute-start(bf16[128,128]{1,0:T(8,128)(2,1)S(1)} %add_convert_fusion), channel_id=1, source_target_pairs={{0,4},{1,5},{2,6},{3,7},{4,8},{5,9},{6,10},{7,11},{8,12},{9,13},{1... | collective-permute-start | bytes 98312 | tf_op jit(solution)/shard_map/ppermute | solution.py:281
  188.3 2.3 %collective-permute-done.12 = bf16[128,128]{1,0:T(8,128)(2,1)S(1)} collective-permute-done((bf16[128,128]{1,0:T(8,128)(2,1)S(1)}, bf16[128,128]{1,0:T(8,128)(2,1)S(1)}, u32[]{:S(2)}, u32[]{:S(2)}) %collective-permute-start.12) | collective-permute-done | bytes 32800 | tf_op jit(solution)/shard_map/ppermute | solution.py:281
  190.6 1.6 collective-permute-done.11
  192.3 3.5 %collective-permute-start.15 = (bf16[512,128]{1,0:T(8,128)(2,1)S(1)}, bf16[512,128]{1,0:T(8,128)(2,1)S(1)}, u32[]{:S(2)}, u32[]{:S(2)}) collective-permute-start(bf16[512,128]{1,0:T(8,128)(2,1)S(1)} %get-tuple-element.50), channel_id=1, source_target_pairs={{0,2},{1,3},{2,0},{3,1},{4,6},{5,7},{6,4},{7,5},{8,10},{9,11},{10,... | collective-permute-start | bytes 393224 | tf_op jit(solution)/shard_map/ppermute | solution.py:281
  195.7 5.3 %collective-permute-start.14 = (bf16[512,128]{1,0:T(8,128)(2,1)S(1)}, bf16[512,128]{1,0:T(8,128)(2,1)S(1)}, u32[]{:S(2)}, u32[]{:S(2)}) collective-permute-start(bf16[512,128]{1,0:T(8,128)(2,1)S(1)} %get-tuple-element.50), channel_id=1, source_target_pairs={{0,1},{1,2},{2,3},{3,0},{4,5},{5,6},{6,7},{7,4},{8,9},{9,10},{10,1... | collective-permute-start | bytes 393224 | tf_op jit(solution)/shard_map/ppermute | solution.py:281
  201.0 3.1 %collective-permute-start.16 = (bf16[512,128]{1,0:T(8,128)(2,1)S(1)}, bf16[512,128]{1,0:T(8,128)(2,1)S(1)}, u32[]{:S(2)}, u32[]{:S(2)}) collective-permute-start(bf16[512,128]{1,0:T(8,128)(2,1)S(1)} %get-tuple-element.50), channel_id=1, source_target_pairs={{0,3},{1,0},{2,1},{3,2},{4,7},{5,4},{6,5},{7,6},{8,11},{9,8},{10,9... | collective-permute-start | bytes 393224 | tf_op jit(solution)/shard_map/ppermute | solution.py:281
  204.2 0.7 copy.86
  205.1 2.8 %collective-permute-done.16 = bf16[512,128]{1,0:T(8,128)(2,1)S(1)} collective-permute-done((bf16[512,128]{1,0:T(8,128)(2,1)S(1)}, bf16[512,128]{1,0:T(8,128)(2,1)S(1)}, u32[]{:S(2)}, u32[]{:S(2)}) %collective-permute-start.16) | collective-permute-done | bytes 131104 | tf_op jit(solution)/shard_map/ppermute | solution.py:281
  208.0 0.7 convert_bitcast_fusion
  208.7 0.7 broadcast_in_dim_reshape.12
  209.5 0.8 broadcast_in_dim_reshape.15
  210.3 0.8 broadcast_in_dim_reshape.14
  211.0 0.8 broadcast_in_dim_reshape.13
  (142 shorter events, 16.6 us)
Async XLA Ops:
  0.6 91.7 %copy-start = (bf16[1,256,256]{2,1,0:T(8,128)(2,1)S(1)}, bf16[1,256,256]{2,1,0:T(8,128)(2,1)}, u32[]{:S(2)}) copy-start(bf16[1,256,256]{2,1,0:T(8,128)(2,1)} %param.22) | copy-start | bytes 393220
  0.6 1.3 copy-start.1
  2.1 0.7 copy-start.11
  3.3 3.4 %copy-start.12 = (f32[5,1,1,1,1,1]{0,1,5,4,3,2:T(1,128)S(1)}, f32[5,1,1,1,1,1]{0,1,5,4,3,2:T(1,128)}, u32[]{:S(2)}) copy-start(f32[5,1,1,1,1,1]{0,1,5,4,3,2:T(1,128)} %constant.210) | copy-start | bytes 64
  3.3 21.7 %collective-permute-start.2 = (f32[2,5,5,1,1,128]{5,0,4,3,2,1:T(2,128)S(1)}, f32[2,5,5,1,1,128]{5,0,4,3,2,1:T(2,128)S(1)}, u32[]{:S(2)}, u32[]{:S(2)}) collective-permute-start(f32[2,5,5,1,1,128]{5,0,4,3,2,1:T(2,128)S(1)} %slice.134), channel_id=1, source_target_pairs={{0,1},{1,2},{2,3},{3,4},{4,5},{5,6},{6,7},{7,8},{8,9},{9,10},{10,1... | collective-permute-start | bytes 76808 | tf_op jit(solution)/shard_map/ppermute | solution.py:25
  7.3 17.9 %collective-permute-start.3 = (f32[2,5,5,1,1,128]{5,0,4,3,2,1:T(2,128)S(1)}, f32[2,5,5,1,1,128]{5,0,4,3,2,1:T(2,128)S(1)}, u32[]{:S(2)}, u32[]{:S(2)}) collective-permute-start(f32[2,5,5,1,1,128]{5,0,4,3,2,1:T(2,128)S(1)} %slice.135), channel_id=1, source_target_pairs={{1,0},{2,1},{3,2},{4,3},{5,4},{6,5},{7,6},{8,7},{9,8},{10,9},{11,1... | collective-permute-start | bytes 76808 | tf_op jit(solution)/shard_map/ppermute | solution.py:26
  9.1 16.2 %collective-permute-start.1 = (f32[2,5,5,1,2,128]{5,4,3,2,1,0:T(2,128)S(1)}, f32[2,5,5,1,2,128]{5,4,3,2,1,0:T(2,128)S(1)}, u32[]{:S(2)}, u32[]{:S(2)}) collective-permute-start(f32[2,5,5,1,2,128]{5,4,3,2,1,0:T(2,128)S(1)} %bitcast.414), channel_id=1, source_target_pairs={{32,0},{64,32},{96,64},{128,96},{160,128},{192,160},{224,192},{256... | collective-permute-start | bytes 153608 | tf_op jit(solution)/shard_map/ppermute | solution.py:26
  11.5 2.4 %copy-start.17 = (s32[128]{0:T(128)S(1)}, s32[128]{0:T(128)}, u32[]{:S(2)}) copy-start(s32[128]{0:T(128)} %param.17) | copy-start | bytes 1540
  11.5 13.9 %collective-permute-start = (f32[2,5,5,1,2,128]{5,4,3,2,1,0:T(2,128)S(1)}, f32[2,5,5,1,2,128]{5,4,3,2,1,0:T(2,128)S(1)}, u32[]{:S(2)}, u32[]{:S(2)}) collective-permute-start(f32[2,5,5,1,2,128]{5,4,3,2,1,0:T(2,128)S(1)} %bitcast.413), channel_id=1, source_target_pairs={{0,32},{32,64},{64,96},{96,128},{128,160},{160,192},{192,224},{224... | collective-permute-start | bytes 153608 | tf_op jit(solution)/shard_map/ppermute | solution.py:25
  14.0 0.7 copy-start.5
  15.2 0.7 copy-start.4
  15.9 1.0 copy-start.2
  18.6 0.7 copy-start.6
  22.8 0.7 copy-start.10
  25.4 0.7 copy-start.8
  25.4 0.7 copy-start.9
  27.6 0.7 copy-start.13
  28.2 0.8 copy-start.7
  31.7 57.9 %all-to-all-start = ((bf16[32,16,256]{2,1,0:T(8,128)(2,1)}), bf16[32,16,256]{2,1,0:T(8,128)(2,1)S(1)}, u32[]{:S(2)}, u32[]{:S(2)}) async-start(bf16[32,16,256]{2,1,0:T(8,128)(2,1)} %bitcast.141), calls=%async_computation | async-start | bytes 524288 | tf_op jit(solution)/shard_map/all_to_all | solution.py:226
  89.6 1.5 copy-start.15
  91.1 0.9 copy-start.14
  92.3 0.9 copy-start.3
  93.2 0.8 copy-start.16
  97.2 12.0 %collective-permute-start.4 = (f32[512,128]{1,0:T(8,128)S(1)}, f32[512,128]{1,0:T(8,128)S(1)}, u32[]{:S(2)}, u32[]{:S(2)}) collective-permute-start(f32[512,128]{1,0:T(8,128)S(1)} %get-tuple-element.29), channel_id=1, source_target_pairs={{0,1},{1,2},{2,3},{3,0},{4,5},{5,6},{6,7},{7,4},{8,9},{9,10},{10,1... | collective-permute-start | bytes 786440 | tf_op jit(solution)/shard_map/ppermute | solution.py:273
  101.8 10.9 %collective-permute-start.6 = (f32[512,128]{1,0:T(8,128)S(1)}, f32[512,128]{1,0:T(8,128)S(1)}, u32[]{:S(2)}, u32[]{:S(2)}) collective-permute-start(f32[512,128]{1,0:T(8,128)S(1)} %get-tuple-element.30), channel_id=1, source_target_pairs={{0,3},{1,0},{2,1},{3,2},{4,7},{5,4},{6,5},{7,6},{8,11},{9,8},{10,9... | collective-permute-start | bytes 786440 | tf_op jit(solution)/shard_map/ppermute | solution.py:273
  105.0 10.6 %collective-permute-start.5 = (f32[512,128]{1,0:T(8,128)S(1)}, f32[512,128]{1,0:T(8,128)S(1)}, u32[]{:S(2)}, u32[]{:S(2)}) collective-permute-start(f32[512,128]{1,0:T(8,128)S(1)} %get-tuple-element.31), channel_id=1, source_target_pairs={{0,2},{1,3},{2,0},{3,1},{4,6},{5,7},{6,4},{7,5},{8,10},{9,11},{10,... | collective-permute-start | bytes 786440 | tf_op jit(solution)/shard_map/ppermute | solution.py:273
  115.7 27.6 %collective-permute-start.7 = (f32[128,128]{1,0:T(8,128)S(1)}, f32[128,128]{1,0:T(8,128)S(1)}, u32[]{:S(2)}, u32[]{:S(2)}) collective-permute-start(f32[128,128]{1,0:T(8,128)S(1)} %get-tuple-element.46), channel_id=1, source_target_pairs={{0,4},{1,5},{2,6},{3,7},{4,8},{5,9},{6,10},{7,11},{8,12},{9,13},{1... | collective-permute-start | bytes 196616 | tf_op jit(solution)/shard_map/ppermute | solution.py:273
  121.5 21.8 %collective-permute-start.9 = (f32[128,128]{1,0:T(8,128)S(1)}, f32[128,128]{1,0:T(8,128)S(1)}, u32[]{:S(2)}, u32[]{:S(2)}) collective-permute-start(f32[128,128]{1,0:T(8,128)S(1)} %get-tuple-element.47), channel_id=1, source_target_pairs={{0,12},{1,13},{2,14},{3,15},{4,0},{5,1},{6,2},{7,3},{8,4},{9,5},{1... | collective-permute-start | bytes 196616 | tf_op jit(solution)/shard_map/ppermute | solution.py:273
  139.9 7.7 %collective-permute-start.8 = (f32[128,128]{1,0:T(8,128)S(1)}, f32[128,128]{1,0:T(8,128)S(1)}, u32[]{:S(2)}, u32[]{:S(2)}) collective-permute-start(f32[128,128]{1,0:T(8,128)S(1)} %get-tuple-element.48), channel_id=1, source_target_pairs={{0,8},{1,9},{2,10},{3,11},{4,12},{5,13},{6,14},{7,15},{8,0},{9,1},... | collective-permute-start | bytes 196616 | tf_op jit(solution)/shard_map/ppermute | solution.py:273
  147.6 24.9 %collective-permute-start.10 = (f32[128,128]{1,0:T(8,128)S(1)}, f32[128,128]{1,0:T(8,128)S(1)}, u32[]{:S(2)}, u32[]{:S(2)}) collective-permute-start(f32[128,128]{1,0:T(8,128)S(1)} %fusion.97), channel_id=1, source_target_pairs={{0,16},{1,17},{2,18},{3,19},{4,20},{5,21},{6,22},{7,23},{8,24},{9,... | collective-permute-start | bytes 196616 | tf_op jit(solution)/shard_map/ppermute | solution.py:276
  172.5 15.8 %collective-permute-start.13 = (bf16[128,128]{1,0:T(8,128)(2,1)S(1)}, bf16[128,128]{1,0:T(8,128)(2,1)S(1)}, u32[]{:S(2)}, u32[]{:S(2)}) collective-permute-start(bf16[128,128]{1,0:T(8,128)(2,1)S(1)} %add_convert_fusion), channel_id=1, source_target_pairs={{0,12},{1,13},{2,14},{3,15},{4,0},{5,1},{6,2},{7,3},{8,4},{9,5},{1... | collective-permute-start | bytes 98312 | tf_op jit(solution)/shard_map/ppermute | solution.py:281
  183.2 7.3 %collective-permute-start.12 = (bf16[128,128]{1,0:T(8,128)(2,1)S(1)}, bf16[128,128]{1,0:T(8,128)(2,1)S(1)}, u32[]{:S(2)}, u32[]{:S(2)}) collective-permute-start(bf16[128,128]{1,0:T(8,128)(2,1)S(1)} %add_convert_fusion), channel_id=1, source_target_pairs={{0,8},{1,9},{2,10},{3,11},{4,12},{5,13},{6,14},{7,15},{8,0},{9,1},... | collective-permute-start | bytes 98312 | tf_op jit(solution)/shard_map/ppermute | solution.py:281
  185.2 7.0 %collective-permute-start.11 = (bf16[128,128]{1,0:T(8,128)(2,1)S(1)}, bf16[128,128]{1,0:T(8,128)(2,1)S(1)}, u32[]{:S(2)}, u32[]{:S(2)}) collective-permute-start(bf16[128,128]{1,0:T(8,128)(2,1)S(1)} %add_convert_fusion), channel_id=1, source_target_pairs={{0,4},{1,5},{2,6},{3,7},{4,8},{5,9},{6,10},{7,11},{8,12},{9,13},{1... | collective-permute-start | bytes 98312 | tf_op jit(solution)/shard_map/ppermute | solution.py:281
  192.3 12.6 %collective-permute-start.15 = (bf16[512,128]{1,0:T(8,128)(2,1)S(1)}, bf16[512,128]{1,0:T(8,128)(2,1)S(1)}, u32[]{:S(2)}, u32[]{:S(2)}) collective-permute-start(bf16[512,128]{1,0:T(8,128)(2,1)S(1)} %get-tuple-element.50), channel_id=1, source_target_pairs={{0,2},{1,3},{2,0},{3,1},{4,6},{5,7},{6,4},{7,5},{8,10},{9,11},{10,... | collective-permute-start | bytes 393224 | tf_op jit(solution)/shard_map/ppermute | solution.py:281
  195.7 9.4 %collective-permute-start.14 = (bf16[512,128]{1,0:T(8,128)(2,1)S(1)}, bf16[512,128]{1,0:T(8,128)(2,1)S(1)}, u32[]{:S(2)}, u32[]{:S(2)}) collective-permute-start(bf16[512,128]{1,0:T(8,128)(2,1)S(1)} %get-tuple-element.50), channel_id=1, source_target_pairs={{0,1},{1,2},{2,3},{3,0},{4,5},{5,6},{6,7},{7,4},{8,9},{9,10},{10,1... | collective-permute-start | bytes 393224 | tf_op jit(solution)/shard_map/ppermute | solution.py:281
  201.0 6.9 %collective-permute-start.16 = (bf16[512,128]{1,0:T(8,128)(2,1)S(1)}, bf16[512,128]{1,0:T(8,128)(2,1)S(1)}, u32[]{:S(2)}, u32[]{:S(2)}) collective-permute-start(bf16[512,128]{1,0:T(8,128)(2,1)S(1)} %get-tuple-element.50), channel_id=1, source_target_pairs={{0,3},{1,0},{2,1},{3,2},{4,7},{5,4},{6,5},{7,6},{8,11},{9,8},{10,9... | collective-permute-start | bytes 393224 | tf_op jit(solution)/shard_map/ppermute | solution.py:281
